TPU v7x, 128 devices: a whole 4x4x4 slice. The times are simulated.
128 devices in a mesh: outer: 4 (over z), inner: 32 (over y, x, core).
Axes of the slice: x: 4, y: 4, z: 4, core: 2. Of those that a mesh axis runs over, the one named last changes fastest.
Arguments:
- tiles: bfloat16 [65536, 128, 128], P(('outer', 'inner')), as said below
- tile_row: int32 [65536], P(('outer', 'inner')), may hold values from 0 to 3, as said below
- tile_col: int32 [65536], P(('outer', 'inner')), may hold values from 0 to 3, as said below
- counts: int32 [16384], P(('outer', 'inner')), may hold values from 1 to 4, as said below
- vectors: bfloat16 [65536, 64], P(('outer', 'inner')), may hold values from -6 to 6
Outputs:
- basis: float32 [65536, 64], P(('outer', 'inner'))
- degree: float32 [65536], P(('outer', 'inner'))
Inputs may be any that keep to these rules, and one draw needn't show every extreme that they name: Slot s from sender g to destination h is live exactly when s < counts[g * 128 + h]; the tiles of dead slots hold values that are no part of P. counts is 4 from every sender to itself and 1 to 4 from every sender to every other destination. `tile_row`: A slot from a sender to itself with number s lies in block row s % 4. `tile_col`: A slot from a sender to itself with number s lies in block column s % 4. `tiles`: entries are affinities, zero or positive.
All inputs are finite; a program needn't handle non-finite values.
Results may differ from a plain program's by a relative error of at most 0.004.
Values may be sent and summed in bfloat16 or wider, within the bound.
No kernel may reach another device: no remote copies, remote signals or barrier semaphores. Data moves between devices by JAX's collectives and lax.ppermute only.
A program may use at most 192 MiB of HBM per device.

v0:
```python
import jax
import jax.numpy as jnp
from jax import lax
from jax.sharding import PartitionSpec as P
from jax.experimental import pallas as pl
from jax.experimental.pallas import tpu as pltpu

AXES = ("outer", "inner")


def butterfly_sum(x, peer_count):
    step = 1
    while step < peer_count:
        perm = [(i, i ^ step) for i in range(peer_count)]
        x = x + lax.ppermute(x, AXES, perm)
        step *= 2
    return x


GROUP = 32


def terms_kernel(rows_ref, live_ref, tiles_ref, own_ref, out_ref):
    step = pl.program_id(0)
    size = tiles_ref.shape[1]

    def body(j, carry):
        t = step * GROUP + j
        start = pl.multiple_of(rows_ref[t] * size, size)
        block = own_ref[pl.ds(start, size), :]
        term = lax.dot_general(
            tiles_ref[j], block, (((0,), (0,)), ((), ())), preferred_element_type=jnp.float32
        ).astype(out_ref.dtype)
        out_ref[j] = jnp.where(live_ref[t] > 0, term, jnp.zeros_like(term))
        return carry

    lax.fori_loop(0, GROUP, body, 0)


def mirror_terms(tiles, rows, live, own):
    slots, size, _ = tiles.shape
    width = own.shape[1]
    return pl.pallas_call(
        terms_kernel,
        grid_spec=pltpu.PrefetchScalarGridSpec(
            num_scalar_prefetch=2,
            grid=(slots // GROUP,),
            in_specs=[
                pl.BlockSpec((GROUP, size, size), lambda i, r, l: (i, 0, 0)),
                pl.BlockSpec(memory_space=pltpu.VMEM),
            ],
            out_specs=pl.BlockSpec((GROUP, size, width), lambda i, r, l: (i, 0, 0)),
        ),
        out_shape=jax.ShapeDtypeStruct((slots, size, width), jnp.bfloat16),
    )(rows, live, tiles, own)


def forward_kernel(blocks_ref, rows_ref, live_ref, tiles_ref, all_ref, out_ref):
    step = pl.program_id(0)
    size = tiles_ref.shape[1]

    @pl.when(step == 0)
    def _():
        out_ref[...] = jnp.zeros_like(out_ref)

    def body(j, carry):
        t = step * GROUP + j
        start = pl.multiple_of(blocks_ref[t] * size, size)
        block = all_ref[pl.ds(start, size), :]
        prod = jnp.dot(tiles_ref[j], block, preferred_element_type=jnp.float32)
        r = rows_ref[t]
        out_ref[r] += jnp.where(live_ref[t] > 0, prod, jnp.zeros_like(prod))
        return carry

    lax.fori_loop(0, GROUP, body, 0)


def forward_product(tiles, blocks, rows, live, scaled_all, block_count):
    slots, size, _ = tiles.shape
    width = scaled_all.shape[1]
    return pl.pallas_call(
        forward_kernel,
        grid_spec=pltpu.PrefetchScalarGridSpec(
            num_scalar_prefetch=3,
            grid=(slots // GROUP,),
            in_specs=[
                pl.BlockSpec((GROUP, size, size), lambda i, b, r, l: (i, 0, 0)),
                pl.BlockSpec(memory_space=pltpu.VMEM),
            ],
            out_specs=pl.BlockSpec((block_count, size, width), lambda i, b, r, l: (0, 0, 0)),
        ),
        out_shape=jax.ShapeDtypeStruct((block_count, size, width), jnp.float32),
    )(blocks, rows, live, tiles, scaled_all)


def shards(tiles, tile_row, tile_col, counts, vectors):
    peer_count = lax.axis_size(AXES)
    outer_count = lax.axis_size("outer")
    inner_count = lax.axis_size("inner")
    slot_total = tiles.shape[0]
    slot_count = slot_total // peer_count
    tile_size = tiles.shape[1]
    rows_dev = vectors.shape[0]
    block_count = rows_dev // tile_size
    vec_width = vectors.shape[1]
    highest = lax.Precision.HIGHEST

    vec_all = lax.all_gather(lax.all_gather(vectors, "outer", axis=0, tiled=True), "inner", axis=0, tiled=True)

    slot_number = jnp.arange(slot_total, dtype=jnp.int32) % slot_count
    live = slot_number < jnp.repeat(counts, slot_count)
    block_ids = jnp.arange(block_count, dtype=jnp.int32)[None, :]
    row_hot = (tile_row[:, None] == block_ids) & live[:, None]
    col_hot = (tile_col[:, None] == block_ids) & live[:, None]

    row_sums = jnp.sum(tiles, axis=2, dtype=jnp.float32)
    col_sums = jnp.sum(tiles, axis=1, dtype=jnp.float32)
    own_part = jnp.einsum("tr,ta->ra", row_hot.astype(jnp.float32), row_sums, precision=highest)
    col_part = jnp.einsum(
        "htr,hta->hra",
        col_hot.astype(jnp.float32).reshape(peer_count, slot_count, block_count),
        col_sums.reshape(peer_count, slot_count, tile_size),
        precision=highest,
    ).reshape(peer_count, block_count * tile_size)
    payload = jnp.concatenate(
        [col_part, tile_col.reshape(peer_count, slot_count).astype(jnp.float32)], axis=1
    )
    got = lax.all_to_all(payload, AXES, split_axis=0, concat_axis=0, tiled=True)
    degree_blocks = own_part + jnp.sum(got[:, : block_count * tile_size], axis=0).reshape(block_count, tile_size)
    got_cols = got[:, block_count * tile_size :].astype(jnp.int32).reshape(peer_count * slot_count)

    degree = 1.0 + degree_blocks.reshape(rows_dev)
    inv_root = lax.rsqrt(degree)
    scaled = (inv_root[:, None] * vectors.astype(jnp.float32)).astype(jnp.bfloat16)

    live_i = live.astype(jnp.int32)
    inv_all = lax.all_gather(inv_root, AXES, axis=0, tiled=True)
    terms = mirror_terms(tiles, tile_row, live_i, scaled)
    terms, inv_all = lax.optimization_barrier((terms, inv_all))
    got_terms = lax.all_to_all(terms, AXES, split_axis=0, concat_axis=0, tiled=True)

    inv_perm = inv_all.reshape(outer_count, inner_count, rows_dev).transpose(1, 0, 2).reshape(-1)
    scaled_all = (inv_perm[:, None] * vec_all.astype(jnp.float32)).astype(jnp.bfloat16)
    dest = jnp.arange(slot_total, dtype=jnp.int32) // slot_count
    place = (dest % inner_count) * outer_count + dest // inner_count
    forward = forward_product(tiles, place * block_count + tile_col, tile_row, live_i, scaled_all, block_count)
    forward, got_terms = lax.optimization_barrier((forward, got_terms))
    got_hot = (got_cols[:, None] == block_ids).astype(jnp.bfloat16)
    mirror = jnp.einsum("tr,tak->rak", got_hot, got_terms, preferred_element_type=jnp.float32)
    total = forward + mirror

    image = inv_root[:, None] * (total.reshape(rows_dev, vec_width) + scaled.astype(jnp.float32))
    local_gram = jnp.dot(image.T, image, precision=highest)
    gram = butterfly_sum(local_gram, peer_count) / jnp.float32(rows_dev * peer_count)
    lower = jnp.linalg.cholesky(gram)
    basis = jax.scipy.linalg.solve_triangular(lower, image.T, lower=True).T
    return (basis, degree)


def solution(mesh):
    placed = (
        P(AXES, None, None),
        P(AXES),
        P(AXES),
        P(AXES),
        P(AXES, None),
    )
    return jax.shard_map(
        shards,
        mesh=mesh,
        in_specs=placed,
        out_specs=(P(AXES, None), P(AXES)),
        check_vma=False,
    )
```

profile of v0, /device:TPU:0, one launch (start us, length us, event | category | flops | bytes accessed | tf_op | source)
XLA Modules:
  0.0 384.7 jit_solution(6885578256320365226)
XLA Ops:
  7.2 1.0 copy.42
  8.2 14.8 %all_gather.10 = bf16[2048,64]{1,0:T(8,128)(2,1)} all-gather(bf16[512,64]{1,0:T(8,128)(2,1)S(1)} %copy.42), channel_id=1, replica_groups=mesh['outer'=4,'inner'=32] {'outer'}, dimensions={0}, use_global_device_ids=true | all-gather | bytes 327680 | tf_op jit(solution)/shard_map/all_gather | solution.py:108
  23.0 0.8 eq.50
  23.9 0.8 fusion.14
  24.7 10.2 %convert_reduce_fusion = (f32[512,128]{1,0:T(8,128)S(1)}, f32[512,128]{1,0:T(8,128)S(1)}) fusion(bf16[512,128,128]{2,1,0:T(8,128)(2,1)} %tiles_ref.3), kind=kLoop, calls=%fused_computation | loop fusion | flops 25034752 | bytes 17301504 | tf_op jit(solution)/shard_map/reduce_sum | solution.py:117
  35.7 0.9 copy.40
  36.6 10.6 %all-to-all-start = ((f32[128,1,516]{2,1,0:T(1,128)}), f32[128,1,516]{2,1,0:T(1,128)S(1)}, u32[]{:S(2)}, u32[]{:S(2)}) async-start(f32[128,1,516]{2,1,0:T(1,128)} %copy.40), calls=%async_computation | async-start | bytes 655360 | tf_op jit(solution)/shard_map/all_to_all | solution.py:128
  48.6 10.0 %all-to-all-done = f32[128,1,516]{2,1,0:T(1,128)S(1)} async-done(((f32[128,1,516]{2,1,0:T(1,128)}), f32[128,1,516]{2,1,0:T(1,128)S(1)}, u32[]{:S(2)}, u32[]{:S(2)}) %all-to-all-start) | async-done | bytes 264224 | tf_op jit(solution)/shard_map/all_to_all | solution.py:128
  59.2 1.1 fusion.42
  60.3 0.8 multiply_convert_fusion.1.own_ref
  61.1 99.4 %shard_map.68 = bf16[512,128,64]{2,1,0:T(8,128)(2,1)} custom-call(s32[512]{0:T(512)} %rows_ref.3, s32[512]{0:T(512)} %get-tuple-element.12.live_ref, bf16[512,128,128]{2,1,0:T(8,128)(2,1)} %tiles_ref.3, bf16[512,64]{1,0:T(8,128)(2,1)} %multiply_convert_fusion.1.own_ref), custom_call_target="tpu_custom_call" | custom-call | tf_op jit(solution)/shard_map/pallas_call | solution.py:43
  160.5 33.2 %all-gather = f32[128,1,512]{2,1,0:T(1,128)S(1)} all-gather(f32[1,1,512]{2,1,0:T(1,128)S(1)} %bitcast.45), channel_id=1, replica_groups=mesh['outer'=4,'inner'=32] {'outer','inner'}, dimensions={0}, use_global_device_ids=true | all-gather | bytes 264192 | tf_op jit(solution)/shard_map/all_gather | solution.py:137
  194.0 15.8 %copy.45 = bf16[512,128,64]{1,2,0:T(8,128)(2,1)} copy(bf16[512,128,64]{2,1,0:T(8,128)(2,1)} %shard_map.68) | data formatting | bytes 16777216 | tf_op jit(solution)/shard_map/optimization_barrier | solution.py:139
  209.8 6.2 %all-to-all-start.1 = ((bf16[512,128,64]{1,2,0:T(8,128)(2,1)}), bf16[512,128,64]{1,2,0:T(8,128)(2,1)}, u32[]{:S(2)}, u32[]{:S(2)}) async-start(bf16[512,128,64]{1,2,0:T(8,128)(2,1)} %copy.45), calls=%async_computation.1 | async-start | bytes 16777216 | tf_op jit(solution)/shard_map/all_to_all | solution.py:140
  216.1 29.6 %multiply_convert_fusion.all_ref = bf16[65536,64]{1,0:T(8,128)(2,1)} fusion(bf16[65536,64]{1,0:T(8,128)(2,1)} %all-gather.3.cloned.1.call-done, f32[65536]{0:T(1024)S(1)} %bitcast.40), kind=kLoop, calls=%fused_computation.2 | loop fusion | flops 12582912 | bytes 17039360 | tf_op jit(solution)/shard_map/convert_element_type | solution.py:143
  245.7 79.8 %shard_map.69 = f32[4,128,64]{2,1,0:T(8,128)} custom-call(s32[512]{0:T(512)} %fusion.33.blocks_ref, s32[512]{0:T(512)} %rows_ref.3, s32[512]{0:T(512)} %get-tuple-element.12.live_ref, bf16[512,128,128]{2,1,0:T(8,128)(2,1)} %tiles_ref.3, bf16[65536,64]{1,0:T(8,128)(2,1)} %multiply_convert_fusion.all_ref), custom_call_target="tpu_custom_call" | custom-call | tf_op jit(solution)/shard_map/pallas_call | solution.py:81
  325.6 7.8 %fusion = f32[4,128,64]{1,0,2:T(4,128)S(1)} fusion(bf16[512,128,64]{1,2,0:T(8,128)(2,1)} %all-to-all-done.1, s32[512]{0:T(512)S(1)} %eq.54), kind=kOutput, calls=%fused_computation.3 | convolution fusion | flops 33556480 | bytes 8521728 | tf_op jit(solution)/shard_map/tr,tak->rak/dot_general | solution.py:149
  333.6 1.0 add.90
  335.4 1.2 collective-permute-done
  337.3 3.2 collective-permute-done.1
  340.5 2.2 collective-permute-start.2
  342.7 3.2 collective-permute-done.2
  346.6 3.2 collective-permute-done.3
  349.8 2.3 collective-permute-start.4
  352.1 3.1 collective-permute-done.4
  355.3 0.8 collective-permute-start.5
  356.1 3.1 collective-permute-done.5
  359.2 2.6 collective-permute-start.6
  361.8 2.8 collective-permute-done.6
  364.7 5.8 %cholesky.16 = f32[64,64]{1,0:T(8,128)S(1)} custom-call(f32[64,64]{1,0:T(8,128)S(1)} %fusion.21), custom_call_target="Cholesky" | custom-call | tf_op jit(solution)/shard_map/jit(cholesky)/cholesky | solution.py:155
  371.9 4.9 %custom-call.7 = f32[1,64,64]{1,2,0:T(8,128)S(1)} custom-call(f32[1,64,64]{2,1,0:T(8,128)S(1)} %fusion.18), custom_call_target="InvertDiagBlocksLowerTriangular" | custom-call | tf_op jit(solution)/shard_map/jit(_solve_triangular)/triangular_solve | solution.py:156
  376.8 1.1 fusion.19
  (45 shorter events, 6.9 us)
Async XLA Ops:
  7.2 40.0 %copy-start.1 = (s32[512]{0:T(512)S(1)}, s32[512]{0:T(512)}, u32[]{:S(2)}) copy-start(s32[512]{0:T(512)} %param.7) | copy-start | bytes 6148
  7.2 40.6 %copy-start.2 = (s32[128]{0:T(128)S(1)}, s32[128]{0:T(128)}, u32[]{:S(2)}) copy-start(s32[128]{0:T(128)} %param.8) | copy-start | bytes 1540
  7.2 52.0 %copy-start = (s32[512]{0:T(512)S(1)}, s32[512]{0:T(512)}, u32[]{:S(2)}) copy-start(s32[512]{0:T(512)} %rows_ref.3) | copy-start | bytes 6148
  7.2 208.9 %all-gather.3.cloned.1.call-start = ((), (), s32[]{:S(2)}) async-start(), calls=%async_computation.2 | async-start | bytes 17301504 | tf_op jit(solution)/shard_map/all_gather | solution.py:108
  36.6 22.0 %all-to-all-start = ((f32[128,1,516]{2,1,0:T(1,128)}), f32[128,1,516]{2,1,0:T(1,128)S(1)}, u32[]{:S(2)}, u32[]{:S(2)}) async-start(f32[128,1,516]{2,1,0:T(1,128)} %copy.40), calls=%async_computation | async-start | bytes 655360 | tf_op jit(solution)/shard_map/all_to_all | solution.py:128
  209.8 115.7 %all-to-all-start.1 = ((bf16[512,128,64]{1,2,0:T(8,128)(2,1)}), bf16[512,128,64]{1,2,0:T(8,128)(2,1)}, u32[]{:S(2)}, u32[]{:S(2)}) async-start(bf16[512,128,64]{1,2,0:T(8,128)(2,1)} %copy.45), calls=%async_computation.1 | async-start | bytes 16777216 | tf_op jit(solution)/shard_map/all_to_all | solution.py:140
  335.3 1.3 collective-permute-start
  336.6 3.9 %collective-permute-start.1 = (f32[64,64]{0,1:T(8,128)S(1)}, f32[64,64]{0,1:T(8,128)S(1)}, u32[]{:S(2)}, u32[]{:S(2)}) collective-permute-start(f32[64,64]{0,1:T(8,128)S(1)} %add.92), channel_id=1, source_target_pairs={{0,2},{1,3},{2,0},{3,1},{4,6},{5,7},{6,4},{7,5},{8,10},{9,11},{10,... | collective-permute-start | bytes 49160 | tf_op jit(solution)/shard_map/ppermute | solution.py:15
  340.5 5.4 %collective-permute-start.2 = (f32[64,64]{0,1:T(8,128)S(1)}, f32[64,64]{0,1:T(8,128)S(1)}, u32[]{:S(2)}, u32[]{:S(2)}) collective-permute-start(f32[64,64]{0,1:T(8,128)S(1)} %add.93), channel_id=1, source_target_pairs={{0,4},{1,5},{2,6},{3,7},{4,0},{5,1},{6,2},{7,3},{8,12},{9,13},{10,... | collective-permute-start | bytes 49160 | tf_op jit(solution)/shard_map/ppermute | solution.py:15
  345.9 3.9 %collective-permute-start.3 = (f32[64,64]{0,1:T(8,128)S(1)}, f32[64,64]{0,1:T(8,128)S(1)}, u32[]{:S(2)}, u32[]{:S(2)}) collective-permute-start(f32[64,64]{0,1:T(8,128)S(1)} %add.94), channel_id=1, source_target_pairs={{0,8},{1,9},{2,10},{3,11},{4,12},{5,13},{6,14},{7,15},{8,0},{9,1},... | collective-permute-start | bytes 49160 | tf_op jit(solution)/shard_map/ppermute | solution.py:15
  349.8 5.4 %collective-permute-start.4 = (f32[64,64]{0,1:T(8,128)S(1)}, f32[64,64]{0,1:T(8,128)S(1)}, u32[]{:S(2)}, u32[]{:S(2)}) collective-permute-start(f32[64,64]{0,1:T(8,128)S(1)} %add.95), channel_id=1, source_target_pairs={{0,16},{1,17},{2,18},{3,19},{4,20},{5,21},{6,22},{7,23},{8,24},{9,... | collective-permute-start | bytes 49160 | tf_op jit(solution)/shard_map/ppermute | solution.py:15
  355.3 3.9 %collective-permute-start.5 = (f32[64,64]{0,1:T(8,128)S(1)}, f32[64,64]{0,1:T(8,128)S(1)}, u32[]{:S(2)}, u32[]{:S(2)}) collective-permute-start(f32[64,64]{0,1:T(8,128)S(1)} %add.96), channel_id=1, source_target_pairs={{0,32},{1,33},{2,34},{3,35},{4,36},{5,37},{6,38},{7,39},{8,40},{9,... | collective-permute-start | bytes 49160 | tf_op jit(solution)/shard_map/ppermute | solution.py:15
  359.2 5.4 %collective-permute-start.6 = (f32[64,64]{0,1:T(8,128)S(1)}, f32[64,64]{0,1:T(8,128)S(1)}, u32[]{:S(2)}, u32[]{:S(2)}) collective-permute-start(f32[64,64]{0,1:T(8,128)S(1)} %add.97), channel_id=1, source_target_pairs={{0,64},{1,65},{2,66},{3,67},{4,68},{5,69},{6,70},{7,71},{8,72},{9,... | collective-permute-start | bytes 49160 | tf_op jit(solution)/shard_map/ppermute | solution.py:15
Sparse Core Ops, SparseCore 0:
  23.2 76.6 all-gather.2
where the time goes:
time: 386 us; the launch traced here: 385 us
  Pallas kernels  179 us (46%)
  other arithmetic  56 us (15%)
  blocking collectives  48 us (12%)
  waiting for transfers between devices  29.8 us (8%)
  starting transfers between devices  26.4 us (7%)
  local copies, waits for them, and re-layouts  19.7 us (5%)
  between operations  14.3 us (4%)
  matrix products  11.2 us (3%)
    pallas_call x1, Pallas kernels, mirror_terms(): pl.pallas_call(terms_kernel, grid_spec=pltpu.PrefetchScalarGridSpec(num_s...  99.4 us
    pallas_call x1, Pallas kernels, forward_product(): pl.pallas_call(forward_kernel, grid_spec=pltpu.PrefetchScalarGridSpec(num...  79.8 us
    all_gather x1, blocking collectives, shards(): inv_all = lax.all_gather(inv_root, AXES, axis=0, tiled=True)  33.2 us
    convert_element_type x1, other arithmetic, shards(): (inv_perm[:, None] * vec_all.astype(jnp.float32)).astype(jnp.bfloat16)  29.6 us
    ppermute x7, waiting for transfers between devices, butterfly_sum(): x = x + lax.ppermute(x, AXES, perm)  19.8 us
    optimization_barrier x1, local copies, waits for them, and re-layouts, shards(): terms, inv_all = lax.optimization_barrier((terms, inv_all))  15.8 us
    all_gather x1, blocking collectives, shards(): lax.all_gather(vectors, 'outer', axis=0, tiled=True)  14.8 us
    all_to_all x1, starting transfers between devices, shards(): got = lax.all_to_all(payload, AXES, split_axis=0, concat_axis=0, tiled=True)  10.6 us
  transfers between devices with their start and end apart: 10, of which 8 were waited for; matrix products, arithmetic and copies ran while one was open for 16% of the time, Pallas kernels for 47%

commit v1 on v0

--- a/solution.py
+++ b/solution.py
@@ -27,19 +27,17 @@
     def body(j, carry):
         t = step * GROUP + j
         start = pl.multiple_of(rows_ref[t] * size, size)
-        block = own_ref[pl.ds(start, size), :]
-        term = lax.dot_general(
-            tiles_ref[j], block, (((0,), (0,)), ((), ())), preferred_element_type=jnp.float32
-        ).astype(out_ref.dtype)
+        block = own_ref[:, pl.ds(start, size)]
+        term = jnp.dot(block, tiles_ref[j], preferred_element_type=jnp.float32).astype(out_ref.dtype)
         out_ref[j] = jnp.where(live_ref[t] > 0, term, jnp.zeros_like(term))
         return carry
 
-    lax.fori_loop(0, GROUP, body, 0)
+    lax.fori_loop(0, GROUP, body, 0, unroll=True)
 
 
-def mirror_terms(tiles, rows, live, own):
+def mirror_terms(tiles, rows, live, own_t):
     slots, size, _ = tiles.shape
-    width = own.shape[1]
+    width = own_t.shape[0]
     return pl.pallas_call(
         terms_kernel,
         grid_spec=pltpu.PrefetchScalarGridSpec(
@@ -49,13 +47,13 @@
                 pl.BlockSpec((GROUP, size, size), lambda i, r, l: (i, 0, 0)),
                 pl.BlockSpec(memory_space=pltpu.VMEM),
             ],
-            out_specs=pl.BlockSpec((GROUP, size, width), lambda i, r, l: (i, 0, 0)),
+            out_specs=pl.BlockSpec((GROUP, width, size), lambda i, r, l: (i, 0, 0)),
         ),
-        out_shape=jax.ShapeDtypeStruct((slots, size, width), jnp.bfloat16),
-    )(rows, live, tiles, own)
+        out_shape=jax.ShapeDtypeStruct((slots, width, size), jnp.bfloat16),
+    )(rows, live, tiles, own_t)
 
 
-def forward_kernel(blocks_ref, rows_ref, live_ref, tiles_ref, all_ref, out_ref):
+def forward_kernel(places_ref, cols_ref, rows_ref, live_ref, tiles_ref, all_ref, out_ref):
     step = pl.program_id(0)
     size = tiles_ref.shape[1]
 
@@ -65,32 +63,34 @@
 
     def body(j, carry):
         t = step * GROUP + j
-        start = pl.multiple_of(blocks_ref[t] * size, size)
-        block = all_ref[pl.ds(start, size), :]
-        prod = jnp.dot(tiles_ref[j], block, preferred_element_type=jnp.float32)
+        start = pl.multiple_of(cols_ref[t] * size, size)
+        block = all_ref[places_ref[t], :, pl.ds(start, size)]
+        prod = lax.dot_general(
+            block, tiles_ref[j], (((1,), (1,)), ((), ())), preferred_element_type=jnp.float32
+        )
         r = rows_ref[t]
         out_ref[r] += jnp.where(live_ref[t] > 0, prod, jnp.zeros_like(prod))
         return carry
 
-    lax.fori_loop(0, GROUP, body, 0)
+    lax.fori_loop(0, GROUP, body, 0, unroll=True)
 
 
-def forward_product(tiles, blocks, rows, live, scaled_all, block_count):
+def forward_product(tiles, places, cols, rows, live, scaled_all_t, block_count):
     slots, size, _ = tiles.shape
-    width = scaled_all.shape[1]
+    width = scaled_all_t.shape[1]
     return pl.pallas_call(
         forward_kernel,
         grid_spec=pltpu.PrefetchScalarGridSpec(
-            num_scalar_prefetch=3,
+            num_scalar_prefetch=4,
             grid=(slots // GROUP,),
             in_specs=[
-                pl.BlockSpec((GROUP, size, size), lambda i, b, r, l: (i, 0, 0)),
+                pl.BlockSpec((GROUP, size, size), lambda i, p, c, r, l: (i, 0, 0)),
                 pl.BlockSpec(memory_space=pltpu.VMEM),
             ],
-            out_specs=pl.BlockSpec((block_count, size, width), lambda i, b, r, l: (0, 0, 0)),
+            out_specs=pl.BlockSpec((block_count, width, size), lambda i, p, c, r, l: (0, 0, 0)),
         ),
-        out_shape=jax.ShapeDtypeStruct((block_count, size, width), jnp.float32),
-    )(blocks, rows, live, tiles, scaled_all)
+        out_shape=jax.ShapeDtypeStruct((block_count, width, size), jnp.float32),
+    )(places, cols, rows, live, tiles, scaled_all_t)
 
 
 def shards(tiles, tile_row, tile_col, counts, vectors):
@@ -105,7 +105,8 @@
     vec_width = vectors.shape[1]
     highest = lax.Precision.HIGHEST
 
-    vec_all = lax.all_gather(lax.all_gather(vectors, "outer", axis=0, tiled=True), "inner", axis=0, tiled=True)
+    vec_t = vectors.T
+    vec_all = lax.all_gather(lax.all_gather(vec_t, "outer", axis=0), "inner", axis=0)
 
     slot_number = jnp.arange(slot_total, dtype=jnp.int32) % slot_count
     live = slot_number < jnp.repeat(counts, slot_count)
@@ -133,27 +134,29 @@
     inv_root = lax.rsqrt(degree)
     scaled = (inv_root[:, None] * vectors.astype(jnp.float32)).astype(jnp.bfloat16)
 
+    scaled_t = scaled.T
     live_i = live.astype(jnp.int32)
-    inv_all = lax.all_gather(inv_root, AXES, axis=0, tiled=True)
-    terms = mirror_terms(tiles, tile_row, live_i, scaled)
+    inv_all = lax.all_gather(inv_root, AXES, axis=0)
+    terms = mirror_terms(tiles, tile_row, live_i, scaled_t)
     terms, inv_all = lax.optimization_barrier((terms, inv_all))
     got_terms = lax.all_to_all(terms, AXES, split_axis=0, concat_axis=0, tiled=True)
 
-    inv_perm = inv_all.reshape(outer_count, inner_count, rows_dev).transpose(1, 0, 2).reshape(-1)
-    scaled_all = (inv_perm[:, None] * vec_all.astype(jnp.float32)).astype(jnp.bfloat16)
+    inv_perm = inv_all.reshape(outer_count, inner_count, 1, rows_dev).transpose(1, 0, 2, 3)
+    scaled_all_t = (inv_perm * vec_all.astype(jnp.float32)).astype(jnp.bfloat16)
+    scaled_all_t = scaled_all_t.reshape(peer_count, vec_width, rows_dev)
     dest = jnp.arange(slot_total, dtype=jnp.int32) // slot_count
     place = (dest % inner_count) * outer_count + dest // inner_count
-    forward = forward_product(tiles, place * block_count + tile_col, tile_row, live_i, scaled_all, block_count)
+    forward = forward_product(tiles, place, tile_col, tile_row, live_i, scaled_all_t, block_count)
     forward, got_terms = lax.optimization_barrier((forward, got_terms))
     got_hot = (got_cols[:, None] == block_ids).astype(jnp.bfloat16)
-    mirror = jnp.einsum("tr,tak->rak", got_hot, got_terms, preferred_element_type=jnp.float32)
-    total = forward + mirror
+    mirror = jnp.einsum("tr,tka->rka", got_hot, got_terms, preferred_element_type=jnp.float32)
+    total_t = (forward + mirror).transpose(1, 0, 2).reshape(vec_width, rows_dev)
 
-    image = inv_root[:, None] * (total.reshape(rows_dev, vec_width) + scaled.astype(jnp.float32))
-    local_gram = jnp.dot(image.T, image, precision=highest)
+    image_t = inv_root[None, :] * (total_t + scaled_t.astype(jnp.float32))
+    local_gram = jnp.dot(image_t, image_t.T, precision=highest)
     gram = butterfly_sum(local_gram, peer_count) / jnp.float32(rows_dev * peer_count)
     lower = jnp.linalg.cholesky(gram)
-    basis = jax.scipy.linalg.solve_triangular(lower, image.T, lower=True).T
+    basis = jax.scipy.linalg.solve_triangular(lower, image_t, lower=True).T
     return (basis, degree)
 
 

time: 386 us -> 276 us (0.72)
  Pallas kernels: 179 us -> 39.1 us
  waiting for transfers between devices: 29.8 us -> 95.3 us
  other arithmetic: 56 us -> 35.1 us
  local copies, waits for them, and re-layouts: 19.7 us -> 2.73 us
    pallas_call x1, Pallas kernels: 99.4 us -> 17.4 us  [mirror_terms(): pl.pallas_call(terms_kernel, grid_spec=pltpu.PrefetchScalarGridSpec(num_s...]
    all_to_all x1, waiting for transfers between devices: 0.01 us -> 65.5 us  [shards(): lax.all_to_all(terms, AXES, split_axis=0, concat_axis=0, tiled=True)]
    pallas_call x1, Pallas kernels: 79.8 us -> 21.8 us  [forward_product(): pl.pallas_call(forward_kernel, grid_spec=pltpu.PrefetchScalarGridSpec(num...]
    convert_element_type x2 -> x1, other arithmetic: 30.4 us -> 10.1 us  [shards(): scaled_all_t = (inv_perm * vec_all.astype(jnp.float32)).astype(jnp.bfloat16)]
    optimization_barrier x1 -> x0, local copies, waits for them, and re-layouts: 15.8 us -> none  [shards(): terms, inv_all = lax.optimization_barrier((terms, inv_all))]
  transfers between devices with their start and end apart: 10 -> 10, of which waited for: 8 -> 9; matrix products, arithmetic and copies ran while one was open for 16% -> 10% of each run, Pallas kernels for 47% -> 14%
where the time goes in v1:
time: 276 us; the launch traced here: 273 us
  waiting for transfers between devices  95.3 us (35%)
  blocking collectives  48.8 us (18%)
  Pallas kernels  39.1 us (14%)
  other arithmetic  35.1 us (13%)
  starting transfers between devices  27.8 us (10%)
  between operations  14.2 us (5%)
  matrix products  10.2 us (4%)
    all_to_all x1, waiting for transfers between devices, shards(): lax.all_to_all(terms, AXES, split_axis=0, concat_axis=0, tiled=True)  65.5 us
    all_gather x1, blocking collectives, shards(): inv_all = lax.all_gather(inv_root, AXES, axis=0)  33.3 us
    pallas_call x1, Pallas kernels, forward_product(): pl.pallas_call(forward_kernel, grid_spec=pltpu.PrefetchScalarGridSpec(num...  21.8 us
    ppermute x7, waiting for transfers between devices, butterfly_sum(): x = x + lax.ppermute(x, AXES, perm)  19.2 us
    pallas_call x1, Pallas kernels, mirror_terms(): pl.pallas_call(terms_kernel, grid_spec=pltpu.PrefetchScalarGridSpec(num_s...  17.4 us
    all_gather x1, blocking collectives, shards(): lax.all_gather(vec_t, 'outer', axis=0)  15.6 us
    ppermute x7, starting transfers between devices, butterfly_sum(): x = x + lax.ppermute(x, AXES, perm)  12.7 us
    all_to_all x1, waiting for transfers between devices, shards(): got = lax.all_to_all(payload, AXES, split_axis=0, concat_axis=0, tiled=True)  10.7 us
  transfers between devices with their start and end apart: 10, of which 9 were waited for; matrix products, arithmetic and copies ran while one was open for 10% of the time, Pallas kernels for 14%

profile of v1, /device:TPU:0, one launch (start us, length us, event | category | flops | bytes accessed | tf_op | source)
XLA Modules:
  0.0 273.4 jit_solution(3894482590393346508)
XLA Ops:
  7.2 15.6 %all-gather = bf16[256,512]{1,0:T(8,128)(2,1)} all-gather(bf16[64,512]{1,0:T(8,128)(2,1)} %bitcast.64), channel_id=2, replica_groups=mesh['outer'=4,'inner'=32] {'outer'}, dimensions={0}, use_global_device_ids=true | all-gather | bytes 327680 | tf_op jit(solution)/shard_map/all_gather | solution.py:109
  22.8 0.8 eq.50
  23.7 0.8 fusion.19
  24.5 10.3 %convert_reduce_fusion = (f32[512,128]{1,0:T(8,128)S(1)}, f32[512,128]{1,0:T(8,128)S(1)}) fusion(bf16[512,128,128]{2,1,0:T(8,128)(2,1)} %tiles_ref.3), kind=kLoop, calls=%fused_computation | loop fusion | flops 25034752 | bytes 17301504 | tf_op jit(solution)/shard_map/reduce_sum | solution.py:118
  34.7 0.6 fusion.7
  35.5 0.9 copy.29
  36.4 8.8 %all-to-all-start = ((f32[128,1,516]{2,1,0:T(1,128)}), f32[128,1,516]{2,1,0:T(1,128)S(1)}, u32[]{:S(2)}, u32[]{:S(2)}) async-start(f32[128,1,516]{2,1,0:T(1,128)} %copy.29), calls=%async_computation | async-start | bytes 655360 | tf_op jit(solution)/shard_map/all_to_all | solution.py:129
  46.0 10.7 %all-to-all-done = f32[128,1,516]{2,1,0:T(1,128)S(1)} async-done(((f32[128,1,516]{2,1,0:T(1,128)}), f32[128,1,516]{2,1,0:T(1,128)S(1)}, u32[]{:S(2)}, u32[]{:S(2)}) %all-to-all-start) | async-done | bytes 264224 | tf_op jit(solution)/shard_map/all_to_all | solution.py:129
  57.5 33.3 %all-gather.2 = f32[128,1,512]{2,1,0:T(1,128)S(1)} all-gather(f32[1,1,512]{2,1,0:T(1,128)S(1)} %bitcast.67), channel_id=1, replica_groups=mesh['outer'=4,'inner'=32] {'outer','inner'}, dimensions={0}, use_global_device_ids=true | all-gather | bytes 264192 | tf_op jit(solution)/shard_map/all_gather | solution.py:139
  90.8 0.6 fusion.20.own_ref
  91.4 17.4 %shard_map.68 = bf16[512,64,128]{2,1,0:T(8,128)(2,1)} custom-call(s32[512]{0:T(512)} %rows_ref.3, s32[512]{0:T(512)} %get-tuple-element.12.live_ref, bf16[512,128,128]{2,1,0:T(8,128)(2,1)} %tiles_ref.3, bf16[64,512]{1,0:T(8,128)(2,1)} %fusion.20.own_ref), custom_call_target="tpu_custom_call" | custom-call | tf_op jit(solution)/shard_map/pallas_call | solution.py:41
  108.8 6.2 %all-to-all-start.1 = ((bf16[512,64,128]{2,1,0:T(8,128)(2,1)}), bf16[512,64,128]{2,1,0:T(8,128)(2,1)}, u32[]{:S(2)}, u32[]{:S(2)}) async-start(bf16[512,64,128]{2,1,0:T(8,128)(2,1)} %shard_map.68), calls=%async_computation.1 | async-start | bytes 16777216 | tf_op jit(solution)/shard_map/all_to_all | solution.py:142
  116.0 10.1 %fusion = bf16[32,4,64,512]{3,2,1,0:T(8,128)(2,1)} fusion(bf16[32,4,64,512]{3,2,1,0:T(8,128)(2,1)} %bitcast.59, f32[32,4,512]{2,1,0:T(4,128)S(1)} %copy.31), kind=kLoop, calls=%fused_computation.3 | loop fusion | flops 12582912 | bytes 17039360 | tf_op jit(solution)/shard_map/convert_element_type | solution.py:145
  126.1 21.8 %shard_map.69 = f32[4,64,128]{2,1,0:T(8,128)} custom-call(s32[512]{0:T(512)} %fusion.38.places_ref, s32[512]{0:T(512)} %cols_ref.1, s32[512]{0:T(512)} %rows_ref.3, s32[512]{0:T(512)} %get-tuple-element.12.live_ref, bf16[512,128,128]{2,1,0:T(8,128)(2,1)} %tiles_ref.3, bf16[128,64,512]{2,1,0:T(8,128)(2,1)} %bitcast.58), custom_call_target="tpu_custom_call" | custom-call | tf_op jit(solution)/shard_map/pallas_call | solution.py:81
  147.9 65.5 %all-to-all-done.1 = bf16[512,64,128]{2,1,0:T(8,128)(2,1)} async-done(((bf16[512,64,128]{2,1,0:T(8,128)(2,1)}), bf16[512,64,128]{2,1,0:T(8,128)(2,1)}, u32[]{:S(2)}, u32[]{:S(2)}) %all-to-all-start.1) | async-done | bytes 8388640 | tf_op jit(solution)/shard_map/all_to_all | solution.py:142
  213.3 7.8 %fusion.1 = f32[4,64,128]{2,0,1:T(4,128)S(1)} fusion(bf16[512,64,128]{2,1,0:T(8,128)(2,1)} %all-to-all-done.1, s32[512]{0:T(512)S(1)} %eq.54), kind=kOutput, calls=%fused_computation.4 | convolution fusion | flops 33556480 | bytes 8521728 | tf_op jit(solution)/shard_map/tr,tka->rka/dot_general | solution.py:152
  221.5 1.2 collective-permute-done
  222.7 3.4 %collective-permute-start.1 = (f32[64,64]{0,1:T(8,128)S(1)}, f32[64,64]{0,1:T(8,128)S(1)}, u32[]{:S(2)}, u32[]{:S(2)}) collective-permute-start(f32[64,64]{0,1:T(8,128)S(1)} %add.97), channel_id=1, source_target_pairs={{0,2},{1,3},{2,0},{3,1},{4,6},{5,7},{6,4},{7,5},{8,10},{9,11},{10,... | collective-permute-start | bytes 49160 | tf_op jit(solution)/shard_map/ppermute | solution.py:15
  226.2 1.9 collective-permute-done.1
  228.3 5.2 %collective-permute-done.2 = f32[64,64]{0,1:T(8,128)S(1)} collective-permute-done((f32[64,64]{0,1:T(8,128)S(1)}, f32[64,64]{0,1:T(8,128)S(1)}, u32[]{:S(2)}, u32[]{:S(2)}) %collective-permute-start.2) | collective-permute-done | bytes 16416 | tf_op jit(solution)/shard_map/ppermute | solution.py:15
  233.5 2.9 %collective-permute-start.3 = (f32[64,64]{0,1:T(8,128)S(1)}, f32[64,64]{0,1:T(8,128)S(1)}, u32[]{:S(2)}, u32[]{:S(2)}) collective-permute-start(f32[64,64]{0,1:T(8,128)S(1)} %add.99), channel_id=1, source_target_pairs={{0,8},{1,9},{2,10},{3,11},{4,12},{5,13},{6,14},{7,15},{8,0},{9,1},... | collective-permute-start | bytes 49160 | tf_op jit(solution)/shard_map/ppermute | solution.py:15
  236.4 1.9 collective-permute-done.3
  238.3 2.2 collective-permute-start.4
  240.5 3.2 %collective-permute-done.4 = f32[64,64]{0,1:T(8,128)S(1)} collective-permute-done((f32[64,64]{0,1:T(8,128)S(1)}, f32[64,64]{0,1:T(8,128)S(1)}, u32[]{:S(2)}, u32[]{:S(2)}) %collective-permute-start.4) | collective-permute-done | bytes 16416 | tf_op jit(solution)/shard_map/ppermute | solution.py:15
  243.7 3.9 %collective-permute-done.5 = f32[64,64]{0,1:T(8,128)S(1)} collective-permute-done((f32[64,64]{0,1:T(8,128)S(1)}, f32[64,64]{0,1:T(8,128)S(1)}, u32[]{:S(2)}, u32[]{:S(2)}) %collective-permute-start.5) | collective-permute-done | bytes 16416 | tf_op jit(solution)/shard_map/ppermute | solution.py:15
  247.6 3.9 %collective-permute-start.6 = (f32[64,64]{0,1:T(8,128)S(1)}, f32[64,64]{0,1:T(8,128)S(1)}, u32[]{:S(2)}, u32[]{:S(2)}) collective-permute-start(f32[64,64]{0,1:T(8,128)S(1)} %add.102), channel_id=1, source_target_pairs={{0,64},{1,65},{2,66},{3,67},{4,68},{5,69},{6,70},{7,71},{8,72},{9,... | collective-permute-start | bytes 49160 | tf_op jit(solution)/shard_map/ppermute | solution.py:15
  251.5 1.9 collective-permute-done.6
  253.5 5.8 %cholesky.16 = f32[64,64]{1,0:T(8,128)S(1)} custom-call(f32[64,64]{1,0:T(8,128)S(1)} %fusion.28), custom_call_target="Cholesky" | custom-call | tf_op jit(solution)/shard_map/jit(cholesky)/cholesky | solution.py:158
  259.4 0.6 compare_reduce_fusion
  260.0 0.7 fusion.26
  260.7 4.9 %custom-call.7 = f32[1,64,64]{1,2,0:T(8,128)S(1)} custom-call(f32[1,64,64]{2,1,0:T(8,128)S(1)} %fusion.26), custom_call_target="InvertDiagBlocksLowerTriangular" | custom-call | tf_op jit(solution)/shard_map/jit(_solve_triangular)/triangular_solve | solution.py:159
  265.6 1.0 fusion.15
  (44 shorter events, 3.5 us)
Async XLA Ops:
  7.2 108.8 %all-gather.5.cloned.1.call-start = ((), (), s32[]{:S(2)}) async-start(), calls=%async_computation.2 | async-start | bytes 8650752 | tf_op jit(solution)/shard_map/all_gather | solution.py:109
  24.4 20.8 %copy-start.4 = (s32[128]{0:T(128)S(1)}, s32[128]{0:T(128)}, u32[]{:S(2)}) copy-start(s32[128]{0:T(128)} %param.8) | copy-start | bytes 1540
  24.4 32.5 %copy-start.2 = (s32[512]{0:T(512)S(1)}, s32[512]{0:T(512)}, u32[]{:S(2)}) copy-start(s32[512]{0:T(512)} %rows_ref.3) | copy-start | bytes 6148
  24.4 66.3 %copy-start.1 = (bf16[512,64]{0,1:T(8,128)(2,1)S(1)}, bf16[512,64]{0,1:T(8,128)(2,1)}, u32[]{:S(2)}) copy-start(bf16[512,64]{0,1:T(8,128)(2,1)} %param.9) | copy-start | bytes 196612
  36.4 20.2 %all-to-all-start = ((f32[128,1,516]{2,1,0:T(1,128)}), f32[128,1,516]{2,1,0:T(1,128)S(1)}, u32[]{:S(2)}, u32[]{:S(2)}) async-start(f32[128,1,516]{2,1,0:T(1,128)} %copy.29), calls=%async_computation | async-start | bytes 655360 | tf_op jit(solution)/shard_map/all_to_all | solution.py:129
  57.5 51.3 %copy-start.3 = (f32[4,128]{1,0:T(4,128)}, f32[4,128]{1,0:T(4,128)S(1)}, u32[]{:S(2)}) copy-start(f32[4,128]{1,0:T(4,128)S(1)} %get-tuple-element.15) | copy-start | bytes 6148
  108.8 104.5 %all-to-all-start.1 = ((bf16[512,64,128]{2,1,0:T(8,128)(2,1)}), bf16[512,64,128]{2,1,0:T(8,128)(2,1)}, u32[]{:S(2)}, u32[]{:S(2)}) async-start(bf16[512,64,128]{2,1,0:T(8,128)(2,1)} %shard_map.68), calls=%async_computation.1 | async-start | bytes 16777216 | tf_op jit(solution)/shard_map/all_to_all | solution.py:142
  147.9 73.3 %copy-start = (f32[4,64,128]{2,1,0:T(8,128)S(1)}, f32[4,64,128]{2,1,0:T(8,128)}, u32[]{:S(2)}) copy-start(f32[4,64,128]{2,1,0:T(8,128)} %shard_map.69) | copy-start | bytes 393220
  221.4 1.3 collective-permute-start
  222.7 5.3 %collective-permute-start.1 = (f32[64,64]{0,1:T(8,128)S(1)}, f32[64,64]{0,1:T(8,128)S(1)}, u32[]{:S(2)}, u32[]{:S(2)}) collective-permute-start(f32[64,64]{0,1:T(8,128)S(1)} %add.97), channel_id=1, source_target_pairs={{0,2},{1,3},{2,0},{3,1},{4,6},{5,7},{6,4},{7,5},{8,10},{9,11},{10,... | collective-permute-start | bytes 49160 | tf_op jit(solution)/shard_map/ppermute | solution.py:15
  228.1 5.4 %collective-permute-start.2 = (f32[64,64]{0,1:T(8,128)S(1)}, f32[64,64]{0,1:T(8,128)S(1)}, u32[]{:S(2)}, u32[]{:S(2)}) collective-permute-start(f32[64,64]{0,1:T(8,128)S(1)} %add.98), channel_id=1, source_target_pairs={{0,4},{1,5},{2,6},{3,7},{4,0},{5,1},{6,2},{7,3},{8,12},{9,13},{10,... | collective-permute-start | bytes 49160 | tf_op jit(solution)/shard_map/ppermute | solution.py:15
  233.5 4.8 %collective-permute-start.3 = (f32[64,64]{0,1:T(8,128)S(1)}, f32[64,64]{0,1:T(8,128)S(1)}, u32[]{:S(2)}, u32[]{:S(2)}) collective-permute-start(f32[64,64]{0,1:T(8,128)S(1)} %add.99), channel_id=1, source_target_pairs={{0,8},{1,9},{2,10},{3,11},{4,12},{5,13},{6,14},{7,15},{8,0},{9,1},... | collective-permute-start | bytes 49160 | tf_op jit(solution)/shard_map/ppermute | solution.py:15
  238.3 5.4 %collective-permute-start.4 = (f32[64,64]{0,1:T(8,128)S(1)}, f32[64,64]{0,1:T(8,128)S(1)}, u32[]{:S(2)}, u32[]{:S(2)}) collective-permute-start(f32[64,64]{0,1:T(8,128)S(1)} %add.100), channel_id=1, source_target_pairs={{0,16},{1,17},{2,18},{3,19},{4,20},{5,21},{6,22},{7,23},{8,24},{9,... | collective-permute-start | bytes 49160 | tf_op jit(solution)/shard_map/ppermute | solution.py:15
  243.7 3.9 %collective-permute-start.5 = (f32[64,64]{0,1:T(8,128)S(1)}, f32[64,64]{0,1:T(8,128)S(1)}, u32[]{:S(2)}, u32[]{:S(2)}) collective-permute-start(f32[64,64]{0,1:T(8,128)S(1)} %add.101), channel_id=1, source_target_pairs={{0,32},{1,33},{2,34},{3,35},{4,36},{5,37},{6,38},{7,39},{8,40},{9,... | collective-permute-start | bytes 49160 | tf_op jit(solution)/shard_map/ppermute | solution.py:15
  247.6 5.8 %collective-permute-start.6 = (f32[64,64]{0,1:T(8,128)S(1)}, f32[64,64]{0,1:T(8,128)S(1)}, u32[]{:S(2)}, u32[]{:S(2)}) collective-permute-start(f32[64,64]{0,1:T(8,128)S(1)} %add.102), channel_id=1, source_target_pairs={{0,64},{1,65},{2,66},{3,67},{4,68},{5,69},{6,70},{7,71},{8,72},{9,... | collective-permute-start | bytes 49160 | tf_op jit(solution)/shard_map/ppermute | solution.py:15
Sparse Core Ops, SparseCore 0:
  22.9 52.8 all-gather.4

commit v2 on v1

--- a/solution.py
+++ b/solution.py
@@ -11,9 +11,15 @@
 def butterfly_sum(x, peer_count):
     step = 1
     while step < peer_count:
-        perm = [(i, i ^ step) for i in range(peer_count)]
-        x = x + lax.ppermute(x, AXES, perm)
-        step *= 2
+        if step * 4 <= peer_count:
+            near = lax.ppermute(x, AXES, [(i, i ^ step) for i in range(peer_count)])
+            far = lax.ppermute(x, AXES, [(i, i ^ (2 * step)) for i in range(peer_count)])
+            far_near = lax.ppermute(x, AXES, [(i, i ^ (3 * step)) for i in range(peer_count)])
+            x = (x + near) + (far + far_near)
+            step *= 4
+        else:
+            x = x + lax.ppermute(x, AXES, [(i, i ^ step) for i in range(peer_count)])
+            step *= 2
     return x
 
 
@@ -106,7 +112,7 @@
     highest = lax.Precision.HIGHEST
 
     vec_t = vectors.T
-    vec_all = lax.all_gather(lax.all_gather(vec_t, "outer", axis=0), "inner", axis=0)
+    vec_all = lax.all_gather(vec_t, AXES, axis=0)
 
     slot_number = jnp.arange(slot_total, dtype=jnp.int32) % slot_count
     live = slot_number < jnp.repeat(counts, slot_count)
@@ -141,11 +147,8 @@
     terms, inv_all = lax.optimization_barrier((terms, inv_all))
     got_terms = lax.all_to_all(terms, AXES, split_axis=0, concat_axis=0, tiled=True)
 
-    inv_perm = inv_all.reshape(outer_count, inner_count, 1, rows_dev).transpose(1, 0, 2, 3)
-    scaled_all_t = (inv_perm * vec_all.astype(jnp.float32)).astype(jnp.bfloat16)
-    scaled_all_t = scaled_all_t.reshape(peer_count, vec_width, rows_dev)
-    dest = jnp.arange(slot_total, dtype=jnp.int32) // slot_count
-    place = (dest % inner_count) * outer_count + dest // inner_count
+    scaled_all_t = (inv_all[:, None, :] * vec_all.astype(jnp.float32)).astype(jnp.bfloat16)
+    place = jnp.arange(slot_total, dtype=jnp.int32) // slot_count
     forward = forward_product(tiles, place, tile_col, tile_row, live_i, scaled_all_t, block_count)
     forward, got_terms = lax.optimization_barrier((forward, got_terms))
     got_hot = (got_cols[:, None] == block_ids).astype(jnp.bfloat16)

time: 276 us -> 262 us (0.949)
  blocking collectives: 48.8 us -> 33.6 us
  starting transfers between devices: 27.8 us -> 35.9 us
  waiting for transfers between devices: 95.3 us -> 90.3 us
    all_gather x1 -> x0, blocking collectives: 15.6 us -> none  [shards(): lax.all_gather(vec_t, 'outer', axis=0)]
    ppermute x7 -> x10, waiting for transfers between devices: 19.2 us -> 13.1 us  [the longest x3 4.01 us: butterfly_sum(): lax.ppermute(x, AXES, [(i, i ^ 3 * step) for i in range(peer_count)])]
    ppermute x7 -> x10, starting transfers between devices: 12.7 us -> 18.4 us  [the longest x3 5.97 us: butterfly_sum(): far = lax.ppermute(x, AXES, [(i, i ^ 2 * step) for i in range(peer_count)])]
  transfers between devices with their start and end apart: 10 -> 13, of which waited for: 9 -> 10; matrix products, arithmetic and copies ran while one was open for 10% -> 10% of each run, Pallas kernels for 14% -> 15%
where the time goes in v2:
time: 262 us; the launch traced here: 261 us
  waiting for transfers between devices  90.3 us (34%)
  Pallas kernels  39.2 us (15%)
  starting transfers between devices  35.9 us (14%)
  other arithmetic  34.9 us (13%)
  blocking collectives  33.6 us (13%)
  between operations  14.2 us (5%)
  matrix products  10.2 us (4%)
    all_to_all x1, waiting for transfers between devices, shards(): lax.all_to_all(terms, AXES, split_axis=0, concat_axis=0, tiled=True)  65.8 us
    all_gather x1, blocking collectives, shards(): inv_all = lax.all_gather(inv_root, AXES, axis=0)  33.6 us
    pallas_call x1, Pallas kernels, forward_product(): pl.pallas_call(forward_kernel, grid_spec=pltpu.PrefetchScalarGridSpec(num...  21.8 us
    pallas_call x1, Pallas kernels, mirror_terms(): pl.pallas_call(terms_kernel, grid_spec=pltpu.PrefetchScalarGridSpec(num_s...  17.5 us
    all_to_all x1, starting transfers between devices, shards(): got = lax.all_to_all(payload, AXES, split_axis=0, concat_axis=0, tiled=True)  11.1 us
    all_to_all x1, waiting for transfers between devices, shards(): got = lax.all_to_all(payload, AXES, split_axis=0, concat_axis=0, tiled=True)  10.7 us
    reduce_sum x1, other arithmetic, shards(): col_sums = jnp.sum(tiles, axis=1, dtype=jnp.float32)  10.2 us
    convert_element_type x1, other arithmetic, shards(): (inv_all[:, None, :] * vec_all.astype(jnp.float32)).astype(jnp.bfloat16)  9.94 us
  transfers between devices with their start and end apart: 13, of which 10 were waited for; matrix products, arithmetic and copies ran while one was open for 10% of the time, Pallas kernels for 15%

profile of v2, /device:TPU:0, one launch (start us, length us, event | category | flops | bytes accessed | tf_op | source)
XLA Modules:
  0.0 260.9 jit_solution(15933113987354401029)
XLA Ops:
  7.2 0.7 all-gather.4.cloned.1.call-update
  7.9 0.8 eq.49
  8.8 0.8 fusion.19
  9.6 10.2 %convert_reduce_fusion = (f32[512,128]{1,0:T(8,128)S(1)}, f32[512,128]{1,0:T(8,128)S(1)}) fusion(bf16[512,128,128]{2,1,0:T(8,128)(2,1)} %tiles_ref.3), kind=kLoop, calls=%fused_computation | loop fusion | flops 25034752 | bytes 17301504 | tf_op jit(solution)/shard_map/reduce_sum | solution.py:124
  20.6 0.9 copy.34
  21.5 11.1 %all-to-all-start = ((f32[128,1,516]{2,1,0:T(1,128)}), f32[128,1,516]{2,1,0:T(1,128)S(1)}, u32[]{:S(2)}, u32[]{:S(2)}) async-start(f32[128,1,516]{2,1,0:T(1,128)} %copy.34), calls=%async_computation | async-start | bytes 655360 | tf_op jit(solution)/shard_map/all_to_all | solution.py:135
  33.4 10.7 %all-to-all-done = f32[128,1,516]{2,1,0:T(1,128)S(1)} async-done(((f32[128,1,516]{2,1,0:T(1,128)}), f32[128,1,516]{2,1,0:T(1,128)S(1)}, u32[]{:S(2)}, u32[]{:S(2)}) %all-to-all-start) | async-done | bytes 264224 | tf_op jit(solution)/shard_map/all_to_all | solution.py:135
  44.9 33.6 %all-gather.1 = f32[128,1,512]{2,1,0:T(1,128)S(1)} all-gather(f32[1,1,512]{2,1,0:T(1,128)S(1)} %bitcast.58), channel_id=1, replica_groups=mesh['outer'=4,'inner'=32] {'outer','inner'}, dimensions={0}, use_global_device_ids=true | all-gather | bytes 264192 | tf_op jit(solution)/shard_map/all_gather | solution.py:145
  79.1 17.5 %shard_map.68 = bf16[512,64,128]{2,1,0:T(8,128)(2,1)} custom-call(s32[512]{0:T(512)} %rows_ref.3, s32[512]{0:T(512)} %get-tuple-element.12.live_ref, bf16[512,128,128]{2,1,0:T(8,128)(2,1)} %tiles_ref.3, bf16[64,512]{1,0:T(8,128)(2,1)} %fusion.20.own_ref), custom_call_target="tpu_custom_call" | custom-call | tf_op jit(solution)/shard_map/pallas_call | solution.py:47
  96.6 6.3 %all-to-all-start.1 = ((bf16[512,64,128]{2,1,0:T(8,128)(2,1)}), bf16[512,64,128]{2,1,0:T(8,128)(2,1)}, u32[]{:S(2)}, u32[]{:S(2)}) async-start(bf16[512,64,128]{2,1,0:T(8,128)(2,1)} %shard_map.68), calls=%async_computation.1 | async-start | bytes 16777216 | tf_op jit(solution)/shard_map/all_to_all | solution.py:148
  103.7 9.9 %fusion.all_ref = bf16[128,64,512]{2,1,0:T(8,128)(2,1)} fusion(bf16[128,64,512]{2,1,0:T(8,128)(2,1)} %bitcast.51, f32[128,512]{1,0:T(8,128)S(1)} %bitcast.55), kind=kLoop, calls=%fused_computation.3 | loop fusion | flops 12582912 | bytes 17039360 | tf_op jit(solution)/shard_map/convert_element_type | solution.py:150
  113.6 21.8 %shard_map.69 = f32[4,64,128]{2,1,0:T(8,128)} custom-call(s32[512]{0:T(512)} %add_select_fusion.1.places_ref, s32[512]{0:T(512)} %cols_ref.1, s32[512]{0:T(512)} %rows_ref.3, s32[512]{0:T(512)} %get-tuple-element.12.live_ref, bf16[512,128,128]{2,1,0:T(8,128)(2,1)} %tiles_ref.3, bf16[128,64,512]{2,1,0:T(8,128)(2,1)} %fusion.all_ref), custom_call_target="tpu_custom_call" | custom-call | tf_op jit(solution)/shard_map/pallas_call | solution.py:87
  135.4 65.8 %all-to-all-done.1 = bf16[512,64,128]{2,1,0:T(8,128)(2,1)} async-done(((bf16[512,64,128]{2,1,0:T(8,128)(2,1)}), bf16[512,64,128]{2,1,0:T(8,128)(2,1)}, u32[]{:S(2)}, u32[]{:S(2)}) %all-to-all-start.1) | async-done | bytes 8388640 | tf_op jit(solution)/shard_map/all_to_all | solution.py:148
  201.2 7.8 %fusion.1 = f32[4,64,128]{2,0,1:T(4,128)S(1)} fusion(bf16[512,64,128]{2,1,0:T(8,128)(2,1)} %all-to-all-done.1, s32[512]{0:T(512)S(1)} %eq.53), kind=kOutput, calls=%fused_computation.4 | convolution fusion | flops 33556480 | bytes 8521728 | tf_op jit(solution)/shard_map/tr,tka->rka/dot_general | solution.py:155
  209.3 3.5 %collective-permute-start.1 = (f32[64,64]{0,1:T(8,128)S(1)}, f32[64,64]{0,1:T(8,128)S(1)}, u32[]{:S(2)}, u32[]{:S(2)}) collective-permute-start(f32[64,64]{0,1:T(8,128)S(1)} %fusion.17), channel_id=1, source_target_pairs={{0,2},{1,3},{2,0},{3,1},{4,6},{5,7},{6,4},{7,5},{8,10},{9,11},{10,... | collective-permute-start | bytes 49160 | tf_op jit(solution)/shard_map/ppermute | solution.py:16
  213.0 1.7 collective-permute-done.1
  214.7 1.4 collective-permute-done.2
  216.2 4.6 %collective-permute-start.5 = (f32[64,64]{0,1:T(8,128)S(1)}, f32[64,64]{0,1:T(8,128)S(1)}, u32[]{:S(2)}, u32[]{:S(2)}) collective-permute-start(f32[64,64]{0,1:T(8,128)S(1)} %add_add_fusion.2), channel_id=1, source_target_pairs={{0,12},{1,13},{2,14},{3,15},{4,8},{5,9},{6,10},{7,11},{8,4},{9,5},... | collective-permute-start | bytes 49160 | tf_op jit(solution)/shard_map/ppermute | solution.py:17
  220.8 0.7 collective-permute-start.3
  221.5 1.2 collective-permute-done.5
  222.7 2.0 collective-permute-done.4
  224.7 1.5 collective-permute-done.3
  226.8 2.5 collective-permute-start.7
  229.3 2.1 collective-permute-start.6
  231.3 1.3 collective-permute-done.8
  232.6 2.0 collective-permute-done.6
  234.7 4.3 %collective-permute-start.9 = (f32[64,64]{0,1:T(8,128)S(1)}, f32[64,64]{0,1:T(8,128)S(1)}, u32[]{:S(2)}, u32[]{:S(2)}) collective-permute-start(f32[64,64]{0,1:T(8,128)S(1)} %add_add_fusion), channel_id=1, source_target_pairs={{0,64},{1,65},{2,66},{3,67},{4,68},{5,69},{6,70},{7,71},{8,72},{9,... | collective-permute-start | bytes 49160 | tf_op jit(solution)/shard_map/ppermute | solution.py:21
  239.0 1.9 collective-permute-done.9
  241.0 5.8 %cholesky.16 = f32[64,64]{1,0:T(8,128)S(1)} custom-call(f32[64,64]{1,0:T(8,128)S(1)} %fusion.28), custom_call_target="Cholesky" | custom-call | tf_op jit(solution)/shard_map/jit(cholesky)/cholesky | solution.py:161
  247.6 0.7 fusion.26
  248.2 4.9 %custom-call.7 = f32[1,64,64]{1,2,0:T(8,128)S(1)} custom-call(f32[1,64,64]{2,1,0:T(8,128)S(1)} %fusion.26), custom_call_target="InvertDiagBlocksLowerTriangular" | custom-call | tf_op jit(solution)/shard_map/jit(_solve_triangular)/triangular_solve | solution.py:162
  253.1 1.0 fusion.15
  (45 shorter events, 5.7 us)
Async XLA Ops:
  7.2 96.5 %all-gather.4.cloned.1.call-start = ((), (), s32[]{:S(2)}) async-start(), calls=%async_computation.2 | async-start | bytes 8454144 | tf_op jit(solution)/shard_map/all_gather | solution.py:115
  9.5 23.1 %copy-start.4 = (s32[128]{0:T(128)S(1)}, s32[128]{0:T(128)}, u32[]{:S(2)}) copy-start(s32[128]{0:T(128)} %param.8) | copy-start | bytes 1540
  9.5 34.8 %copy-start.2 = (s32[512]{0:T(512)S(1)}, s32[512]{0:T(512)}, u32[]{:S(2)}) copy-start(s32[512]{0:T(512)} %rows_ref.3) | copy-start | bytes 6148
  9.6 68.9 %copy-start.1 = (bf16[512,64]{0,1:T(8,128)(2,1)S(1)}, bf16[512,64]{0,1:T(8,128)(2,1)}, u32[]{:S(2)}) copy-start(bf16[512,64]{0,1:T(8,128)(2,1)} %param.9) | copy-start | bytes 196612
  21.5 22.6 %all-to-all-start = ((f32[128,1,516]{2,1,0:T(1,128)}), f32[128,1,516]{2,1,0:T(1,128)S(1)}, u32[]{:S(2)}, u32[]{:S(2)}) async-start(f32[128,1,516]{2,1,0:T(1,128)} %copy.34), calls=%async_computation | async-start | bytes 655360 | tf_op jit(solution)/shard_map/all_to_all | solution.py:135
  44.9 51.7 %copy-start.3 = (f32[4,128]{1,0:T(4,128)}, f32[4,128]{1,0:T(4,128)S(1)}, u32[]{:S(2)}) copy-start(f32[4,128]{1,0:T(4,128)S(1)} %get-tuple-element.15) | copy-start | bytes 6148
  96.6 104.6 %all-to-all-start.1 = ((bf16[512,64,128]{2,1,0:T(8,128)(2,1)}), bf16[512,64,128]{2,1,0:T(8,128)(2,1)}, u32[]{:S(2)}, u32[]{:S(2)}) async-start(bf16[512,64,128]{2,1,0:T(8,128)(2,1)} %shard_map.68), calls=%async_computation.1 | async-start | bytes 16777216 | tf_op jit(solution)/shard_map/all_to_all | solution.py:148
  135.4 73.6 %copy-start = (f32[4,64,128]{2,1,0:T(8,128)S(1)}, f32[4,64,128]{2,1,0:T(8,128)}, u32[]{:S(2)}) copy-start(f32[4,64,128]{2,1,0:T(8,128)} %shard_map.69) | copy-start | bytes 393220
  209.3 5.4 %collective-permute-start.1 = (f32[64,64]{0,1:T(8,128)S(1)}, f32[64,64]{0,1:T(8,128)S(1)}, u32[]{:S(2)}, u32[]{:S(2)}) collective-permute-start(f32[64,64]{0,1:T(8,128)S(1)} %fusion.17), channel_id=1, source_target_pairs={{0,2},{1,3},{2,0},{3,1},{4,6},{5,7},{6,4},{7,5},{8,10},{9,11},{10,... | collective-permute-start | bytes 49160 | tf_op jit(solution)/shard_map/ppermute | solution.py:16
  212.8 1.9 collective-permute-start
  212.8 3.3 %collective-permute-start.2 = (f32[64,64]{0,1:T(8,128)S(1)}, f32[64,64]{0,1:T(8,128)S(1)}, u32[]{:S(2)}, u32[]{:S(2)}) collective-permute-start(f32[64,64]{0,1:T(8,128)S(1)} %fusion.17), channel_id=1, source_target_pairs={{0,3},{1,2},{2,1},{3,0},{4,7},{5,6},{6,5},{7,4},{8,11},{9,10},{10,... | collective-permute-start | bytes 49160 | tf_op jit(solution)/shard_map/ppermute | solution.py:17
  216.2 6.5 %collective-permute-start.5 = (f32[64,64]{0,1:T(8,128)S(1)}, f32[64,64]{0,1:T(8,128)S(1)}, u32[]{:S(2)}, u32[]{:S(2)}) collective-permute-start(f32[64,64]{0,1:T(8,128)S(1)} %add_add_fusion.2), channel_id=1, source_target_pairs={{0,12},{1,13},{2,14},{3,15},{4,8},{5,9},{6,10},{7,11},{8,4},{9,5},... | collective-permute-start | bytes 49160 | tf_op jit(solution)/shard_map/ppermute | solution.py:17
  220.8 3.9 %collective-permute-start.4 = (f32[64,64]{0,1:T(8,128)S(1)}, f32[64,64]{0,1:T(8,128)S(1)}, u32[]{:S(2)}, u32[]{:S(2)}) collective-permute-start(f32[64,64]{0,1:T(8,128)S(1)} %add_add_fusion.2), channel_id=1, source_target_pairs={{0,8},{1,9},{2,10},{3,11},{4,12},{5,13},{6,14},{7,15},{8,0},{9,1},... | collective-permute-start | bytes 49160 | tf_op jit(solution)/shard_map/ppermute | solution.py:16
  220.8 5.4 %collective-permute-start.3 = (f32[64,64]{0,1:T(8,128)S(1)}, f32[64,64]{0,1:T(8,128)S(1)}, u32[]{:S(2)}, u32[]{:S(2)}) collective-permute-start(f32[64,64]{0,1:T(8,128)S(1)} %add_add_fusion.2), channel_id=1, source_target_pairs={{0,4},{1,5},{2,6},{3,7},{4,0},{5,1},{6,2},{7,3},{8,12},{9,13},{10,... | collective-permute-start | bytes 49160 | tf_op jit(solution)/shard_map/ppermute | solution.py:15
  226.2 6.4 %collective-permute-start.8 = (f32[64,64]{0,1:T(8,128)S(1)}, f32[64,64]{0,1:T(8,128)S(1)}, u32[]{:S(2)}, u32[]{:S(2)}) collective-permute-start(f32[64,64]{0,1:T(8,128)S(1)} %add_add_fusion.1), channel_id=1, source_target_pairs={{0,48},{1,49},{2,50},{3,51},{4,52},{5,53},{6,54},{7,55},{8,56},{9,... | collective-permute-start | bytes 49160 | tf_op jit(solution)/shard_map/ppermute | solution.py:17
  226.8 5.9 %collective-permute-start.7 = (f32[64,64]{0,1:T(8,128)S(1)}, f32[64,64]{0,1:T(8,128)S(1)}, u32[]{:S(2)}, u32[]{:S(2)}) collective-permute-start(f32[64,64]{0,1:T(8,128)S(1)} %add_add_fusion.1), channel_id=1, source_target_pairs={{0,32},{1,33},{2,34},{3,35},{4,36},{5,37},{6,38},{7,39},{8,40},{9,... | collective-permute-start | bytes 49160 | tf_op jit(solution)/shard_map/ppermute | solution.py:16
  229.3 5.4 %collective-permute-start.6 = (f32[64,64]{0,1:T(8,128)S(1)}, f32[64,64]{0,1:T(8,128)S(1)}, u32[]{:S(2)}, u32[]{:S(2)}) collective-permute-start(f32[64,64]{0,1:T(8,128)S(1)} %add_add_fusion.1), channel_id=1, source_target_pairs={{0,16},{1,17},{2,18},{3,19},{4,20},{5,21},{6,22},{7,23},{8,24},{9,... | collective-permute-start | bytes 49160 | tf_op jit(solution)/shard_map/ppermute | solution.py:15
  234.7 6.2 %collective-permute-start.9 = (f32[64,64]{0,1:T(8,128)S(1)}, f32[64,64]{0,1:T(8,128)S(1)}, u32[]{:S(2)}, u32[]{:S(2)}) collective-permute-start(f32[64,64]{0,1:T(8,128)S(1)} %add_add_fusion), channel_id=1, source_target_pairs={{0,64},{1,65},{2,66},{3,67},{4,68},{5,69},{6,70},{7,71},{8,72},{9,... | collective-permute-start | bytes 49160 | tf_op jit(solution)/shard_map/ppermute | solution.py:21
Sparse Core Ops, SparseCore 0:
  11.0 73.7 all-gather.3

commit v3 on v2

--- a/solution.py
+++ b/solution.py
@@ -142,9 +142,9 @@
 
     scaled_t = scaled.T
     live_i = live.astype(jnp.int32)
-    inv_all = lax.all_gather(inv_root, AXES, axis=0)
+    inv_rows, vec_all = lax.optimization_barrier((jnp.broadcast_to(inv_root[None, :], (8, rows_dev)), vec_all))
+    inv_all = lax.all_gather(inv_rows, AXES, axis=0)[:, 0, :]
     terms = mirror_terms(tiles, tile_row, live_i, scaled_t)
-    terms, inv_all = lax.optimization_barrier((terms, inv_all))
     got_terms = lax.all_to_all(terms, AXES, split_axis=0, concat_axis=0, tiled=True)
 
     scaled_all_t = (inv_all[:, None, :] * vec_all.astype(jnp.float32)).astype(jnp.bfloat16)

time: 262 us -> 328 us (1.25)
  waiting for transfers between devices: 90.3 us -> 191 us
  blocking collectives: 33.6 us -> 0 us
  starting transfers between devices: 35.9 us -> 31.3 us
    all_gather x1, waiting for transfers between devices: 0.02 us -> 84.7 us  [shards(): vec_all = lax.all_gather(vec_t, AXES, axis=0)]
    all_gather x0 -> x1, waiting for transfers between devices: none -> 80.9 us  [shards(): inv_all = lax.all_gather(inv_rows, AXES, axis=0)[:, 0, :]]
    all_to_all x1, waiting for transfers between devices: 65.8 us -> 0.01 us  [shards(): lax.all_to_all(terms, AXES, split_axis=0, concat_axis=0, tiled=True)]
    all_gather x1 -> x0, blocking collectives: 33.6 us -> none  [shards(): inv_all = lax.all_gather(inv_root, AXES, axis=0)]
  transfers between devices with their start and end apart: 13 -> 14, of which waited for: 10 -> 10; matrix products, arithmetic and copies ran while one was open for 10% -> 9% of each run, Pallas kernels for 15% -> 12%
where the time goes in v3:
time: 328 us; the launch traced here: 326 us
  waiting for transfers between devices  191 us (58%)
  Pallas kernels  39.1 us (12%)
  other arithmetic  35 us (11%)
  starting transfers between devices  31.3 us (10%)
  between operations  14.2 us (4%)
  matrix products  10.9 us (3%)
  local copies, waits for them, and re-layouts  4.91 us (1%)
    all_gather x1, waiting for transfers between devices, shards(): vec_all = lax.all_gather(vec_t, AXES, axis=0)  84.7 us
    all_gather x1, waiting for transfers between devices, shards(): inv_all = lax.all_gather(inv_rows, AXES, axis=0)[:, 0, :]  80.9 us
    pallas_call x1, Pallas kernels, forward_product(): pl.pallas_call(forward_kernel, grid_spec=pltpu.PrefetchScalarGridSpec(num...  21.8 us
    pallas_call x1, Pallas kernels, mirror_terms(): pl.pallas_call(terms_kernel, grid_spec=pltpu.PrefetchScalarGridSpec(num_s...  17.3 us
    all_to_all x1, starting transfers between devices, shards(): got = lax.all_to_all(payload, AXES, split_axis=0, concat_axis=0, tiled=True)  11.1 us
    all_to_all x1, waiting for transfers between devices, shards(): got = lax.all_to_all(payload, AXES, split_axis=0, concat_axis=0, tiled=True)  10.7 us
    reduce_sum x1, other arithmetic, shards(): col_sums = jnp.sum(tiles, axis=1, dtype=jnp.float32)  10.2 us
    convert_element_type x1, other arithmetic, shards(): (inv_all[:, None, :] * vec_all.astype(jnp.float32)).astype(jnp.bfloat16)  9.93 us
  transfers between devices with their start and end apart: 14, of which 10 were waited for; matrix products, arithmetic and copies ran while one was open for 9% of the time, Pallas kernels for 12%

profile of v3, /device:TPU:0, one launch (start us, length us, event | category | flops | bytes accessed | tf_op | source)
XLA Modules:
  0.0 326.3 jit_solution(4159947225100432614)
XLA Ops:
  7.9 0.8 eq.49
  8.8 0.8 fusion.19
  9.6 10.2 %convert_reduce_fusion = (f32[512,128]{1,0:T(8,128)S(1)}, f32[512,128]{1,0:T(8,128)S(1)}) fusion(bf16[512,128,128]{2,1,0:T(8,128)(2,1)} %tiles_ref.3), kind=kLoop, calls=%fused_computation | loop fusion | flops 25034752 | bytes 17301504 | tf_op jit(solution)/shard_map/reduce_sum | solution.py:124
  20.6 0.9 copy.33
  21.5 11.1 %all-to-all-start = ((f32[128,1,516]{2,1,0:T(1,128)}), f32[128,1,516]{2,1,0:T(1,128)S(1)}, u32[]{:S(2)}, u32[]{:S(2)}) async-start(f32[128,1,516]{2,1,0:T(1,128)} %copy.33), calls=%async_computation | async-start | bytes 655360 | tf_op jit(solution)/shard_map/all_to_all | solution.py:135
  33.4 10.7 %all-to-all-done = f32[128,1,516]{2,1,0:T(1,128)S(1)} async-done(((f32[128,1,516]{2,1,0:T(1,128)}), f32[128,1,516]{2,1,0:T(1,128)S(1)}, u32[]{:S(2)}, u32[]{:S(2)}) %all-to-all-start) | async-done | bytes 264224 | tf_op jit(solution)/shard_map/all_to_all | solution.py:135
  44.3 1.1 fusion.40
  46.1 17.3 %shard_map.69 = bf16[512,64,128]{2,1,0:T(8,128)(2,1)} custom-call(s32[512]{0:T(512)} %rows_ref.3, s32[512]{0:T(512)} %get-tuple-element.12.live_ref, bf16[512,128,128]{2,1,0:T(8,128)(2,1)} %tiles_ref.3, bf16[64,512]{1,0:T(8,128)(2,1)} %fusion.20.own_ref), custom_call_target="tpu_custom_call" | custom-call | tf_op jit(solution)/shard_map/pallas_call | solution.py:47
  63.4 6.0 %all-to-all-start.1 = ((bf16[512,64,128]{2,1,0:T(8,128)(2,1)}), bf16[512,64,128]{2,1,0:T(8,128)(2,1)}, u32[]{:S(2)}, u32[]{:S(2)}) async-start(bf16[512,64,128]{2,1,0:T(8,128)(2,1)} %shard_map.69), calls=%async_computation.1 | async-start | bytes 16777216 | tf_op jit(solution)/shard_map/all_to_all | solution.py:148
  69.6 84.7 %all-gather.5.cloned.1.call-done = bf16[8192,512]{1,0:T(8,128)(2,1)} async-done(((bf16[64,512]{1,0:T(8,128)(2,1)}), bf16[8192,512]{1,0:T(8,128)(2,1)}) %all-gather.5.cloned.1.call-update) | async-done | bytes 8388624 | tf_op jit(solution)/shard_map/all_gather | solution.py:115
  155.8 80.9 %all-gather.7.cloned.1.call-done = f32[1024,512]{1,0:T(8,128)} async-done(((f32[8,512]{1,0:T(8,128)}), f32[1024,512]{1,0:T(8,128)}) %all-gather.7.cloned.1.call-update) | async-done | bytes 2097168 | tf_op jit(solution)/shard_map/all_gather | solution.py:146
  236.7 1.8 slice.25
  238.5 9.9 %multiply_convert_fusion.all_ref = bf16[128,64,512]{2,1,0:T(8,128)(2,1)} fusion(bf16[128,64,512]{2,1,0:T(8,128)(2,1)} %bitcast.50, f32[128,512]{1,0:T(8,128)S(1)} %bitcast.54), kind=kLoop, calls=%fused_computation.2 | loop fusion | flops 12582912 | bytes 17039360 | tf_op jit(solution)/shard_map/convert_element_type | solution.py:150
  248.4 21.8 %shard_map.68 = f32[4,64,128]{2,1,0:T(8,128)} custom-call(s32[512]{0:T(512)} %add_select_fusion.1.places_ref, s32[512]{0:T(512)} %cols_ref.1, s32[512]{0:T(512)} %rows_ref.3, s32[512]{0:T(512)} %get-tuple-element.12.live_ref, bf16[512,128,128]{2,1,0:T(8,128)(2,1)} %tiles_ref.3, bf16[128,64,512]{2,1,0:T(8,128)(2,1)} %multiply_convert_fusion.all_ref), custom_call_target="tpu_custom_call" | custom-call | tf_op jit(solution)/shard_map/pallas_call | solution.py:87
  270.2 7.9 %fusion = f32[4,64,128]{2,0,1:T(4,128)S(1)} fusion(bf16[512,64,128]{2,1,0:T(8,128)(2,1)} %all-to-all-done.1, s32[512]{0:T(512)S(1)} %eq.53), kind=kOutput, calls=%fused_computation.3 | convolution fusion | flops 33556480 | bytes 8521728 | tf_op jit(solution)/shard_map/tr,tka->rka/dot_general | solution.py:155
  278.8 1.8 collective-permute-start.2
  280.6 2.0 collective-permute-done.1
  282.5 2.3 collective-permute-start.5
  284.8 0.9 collective-permute-start.4
  285.7 1.9 collective-permute-start.3
  287.6 1.4 collective-permute-done.5
  289.1 2.1 collective-permute-done.3
  291.2 2.2 collective-permute-start.8
  293.4 1.9 collective-permute-start.7
  295.3 0.9 collective-permute-start.6
  296.3 1.5 collective-permute-done.8
  297.8 2.9 collective-permute-done.6
  300.7 1.6 collective-permute-start.9
  302.3 3.9 %collective-permute-done.9 = f32[64,64]{0,1:T(8,128)S(1)} collective-permute-done((f32[64,64]{0,1:T(8,128)S(1)}, f32[64,64]{0,1:T(8,128)S(1)}, u32[]{:S(2)}, u32[]{:S(2)}) %collective-permute-start.9) | collective-permute-done | bytes 16416 | tf_op jit(solution)/shard_map/ppermute | solution.py:21
  306.3 5.8 %cholesky.16 = f32[64,64]{1,0:T(8,128)S(1)} custom-call(f32[64,64]{1,0:T(8,128)S(1)} %fusion.28), custom_call_target="Cholesky" | custom-call | tf_op jit(solution)/shard_map/jit(cholesky)/cholesky | solution.py:161
  313.5 4.9 %custom-call.7 = f32[1,64,64]{1,2,0:T(8,128)S(1)} custom-call(f32[1,64,64]{2,1,0:T(8,128)S(1)} %fusion.26), custom_call_target="InvertDiagBlocksLowerTriangular" | custom-call | tf_op jit(solution)/shard_map/jit(_solve_triangular)/triangular_solve | solution.py:162
  318.4 1.0 fusion.15
  (46 shorter events, 7.2 us)
Async XLA Ops:
  7.2 147.2 %all-gather.5.cloned.1.call-start = ((), (), s32[]{:S(2)}) async-start(), calls=%async_computation.2 | async-start | bytes 8454144 | tf_op jit(solution)/shard_map/all_gather | solution.py:115
  9.5 23.1 %copy-start.3 = (s32[128]{0:T(128)S(1)}, s32[128]{0:T(128)}, u32[]{:S(2)}) copy-start(s32[128]{0:T(128)} %param.8) | copy-start | bytes 1540
  9.5 34.8 %copy-start.2 = (s32[512]{0:T(512)S(1)}, s32[512]{0:T(512)}, u32[]{:S(2)}) copy-start(s32[512]{0:T(512)} %rows_ref.3) | copy-start | bytes 6148
  9.6 35.9 %copy-start.1 = (bf16[512,64]{0,1:T(8,128)(2,1)S(1)}, bf16[512,64]{0,1:T(8,128)(2,1)}, u32[]{:S(2)}) copy-start(bf16[512,64]{0,1:T(8,128)(2,1)} %param.9) | copy-start | bytes 196612
  21.5 22.6 %all-to-all-start = ((f32[128,1,516]{2,1,0:T(1,128)}), f32[128,1,516]{2,1,0:T(1,128)S(1)}, u32[]{:S(2)}, u32[]{:S(2)}) async-start(f32[128,1,516]{2,1,0:T(1,128)} %copy.33), calls=%async_computation | async-start | bytes 655360 | tf_op jit(solution)/shard_map/all_to_all | solution.py:135
  63.4 206.8 %all-to-all-start.1 = ((bf16[512,64,128]{2,1,0:T(8,128)(2,1)}), bf16[512,64,128]{2,1,0:T(8,128)(2,1)}, u32[]{:S(2)}, u32[]{:S(2)}) async-start(bf16[512,64,128]{2,1,0:T(8,128)(2,1)} %shard_map.69), calls=%async_computation.1 | async-start | bytes 16777216 | tf_op jit(solution)/shard_map/all_to_all | solution.py:148
  69.4 167.3 %all-gather.7.cloned.1.call-start = ((), (), s32[]{:S(2)}) async-start(), calls=%async_computation.3 | async-start | bytes 2113536 | tf_op jit(solution)/shard_map/all_gather | solution.py:146
  270.2 7.9 %copy-start = (f32[4,64,128]{2,1,0:T(8,128)S(1)}, f32[4,64,128]{2,1,0:T(8,128)}, u32[]{:S(2)}) copy-start(f32[4,64,128]{2,1,0:T(8,128)} %shard_map.68) | copy-start | bytes 393220
  278.4 4.2 %collective-permute-start.1 = (f32[64,64]{0,1:T(8,128)S(1)}, f32[64,64]{0,1:T(8,128)S(1)}, u32[]{:S(2)}, u32[]{:S(2)}) collective-permute-start(f32[64,64]{0,1:T(8,128)S(1)} %fusion.17), channel_id=1, source_target_pairs={{0,2},{1,3},{2,0},{3,1},{4,6},{5,7},{6,4},{7,5},{8,10},{9,11},{10,... | collective-permute-start | bytes 49160 | tf_op jit(solution)/shard_map/ppermute | solution.py:16
  278.7 3.8 %collective-permute-start = (f32[64,64]{0,1:T(8,128)S(1)}, f32[64,64]{0,1:T(8,128)S(1)}, u32[]{:S(2)}, u32[]{:S(2)}) collective-permute-start(f32[64,64]{0,1:T(8,128)S(1)} %fusion.17), channel_id=1, source_target_pairs={{0,1},{1,0},{2,3},{3,2},{4,5},{5,4},{6,7},{7,6},{8,9},{9,8},{10,11... | collective-permute-start | bytes 49160 | tf_op jit(solution)/shard_map/ppermute | solution.py:15
  278.8 3.7 %collective-permute-start.2 = (f32[64,64]{0,1:T(8,128)S(1)}, f32[64,64]{0,1:T(8,128)S(1)}, u32[]{:S(2)}, u32[]{:S(2)}) collective-permute-start(f32[64,64]{0,1:T(8,128)S(1)} %fusion.17), channel_id=1, source_target_pairs={{0,3},{1,2},{2,1},{3,0},{4,7},{5,6},{6,5},{7,4},{8,11},{9,10},{10,... | collective-permute-start | bytes 49160 | tf_op jit(solution)/shard_map/ppermute | solution.py:17
  282.5 6.4 %collective-permute-start.5 = (f32[64,64]{0,1:T(8,128)S(1)}, f32[64,64]{0,1:T(8,128)S(1)}, u32[]{:S(2)}, u32[]{:S(2)}) collective-permute-start(f32[64,64]{0,1:T(8,128)S(1)} %add_add_fusion.2), channel_id=1, source_target_pairs={{0,12},{1,13},{2,14},{3,15},{4,8},{5,9},{6,10},{7,11},{8,4},{9,5},... | collective-permute-start | bytes 49160 | tf_op jit(solution)/shard_map/ppermute | solution.py:17
  284.8 4.3 %collective-permute-start.4 = (f32[64,64]{0,1:T(8,128)S(1)}, f32[64,64]{0,1:T(8,128)S(1)}, u32[]{:S(2)}, u32[]{:S(2)}) collective-permute-start(f32[64,64]{0,1:T(8,128)S(1)} %add_add_fusion.2), channel_id=1, source_target_pairs={{0,8},{1,9},{2,10},{3,11},{4,12},{5,13},{6,14},{7,15},{8,0},{9,1},... | collective-permute-start | bytes 49160 | tf_op jit(solution)/shard_map/ppermute | solution.py:16
  285.7 5.4 %collective-permute-start.3 = (f32[64,64]{0,1:T(8,128)S(1)}, f32[64,64]{0,1:T(8,128)S(1)}, u32[]{:S(2)}, u32[]{:S(2)}) collective-permute-start(f32[64,64]{0,1:T(8,128)S(1)} %add_add_fusion.2), channel_id=1, source_target_pairs={{0,4},{1,5},{2,6},{3,7},{4,0},{5,1},{6,2},{7,3},{8,12},{9,13},{10,... | collective-permute-start | bytes 49160 | tf_op jit(solution)/shard_map/ppermute | solution.py:15
  291.2 6.6 %collective-permute-start.8 = (f32[64,64]{0,1:T(8,128)S(1)}, f32[64,64]{0,1:T(8,128)S(1)}, u32[]{:S(2)}, u32[]{:S(2)}) collective-permute-start(f32[64,64]{0,1:T(8,128)S(1)} %add_add_fusion.1), channel_id=1, source_target_pairs={{0,48},{1,49},{2,50},{3,51},{4,52},{5,53},{6,54},{7,55},{8,56},{9,... | collective-permute-start | bytes 49160 | tf_op jit(solution)/shard_map/ppermute | solution.py:17
  293.4 4.4 %collective-permute-start.7 = (f32[64,64]{0,1:T(8,128)S(1)}, f32[64,64]{0,1:T(8,128)S(1)}, u32[]{:S(2)}, u32[]{:S(2)}) collective-permute-start(f32[64,64]{0,1:T(8,128)S(1)} %add_add_fusion.1), channel_id=1, source_target_pairs={{0,32},{1,33},{2,34},{3,35},{4,36},{5,37},{6,38},{7,39},{8,40},{9,... | collective-permute-start | bytes 49160 | tf_op jit(solution)/shard_map/ppermute | solution.py:16
  295.3 5.4 %collective-permute-start.6 = (f32[64,64]{0,1:T(8,128)S(1)}, f32[64,64]{0,1:T(8,128)S(1)}, u32[]{:S(2)}, u32[]{:S(2)}) collective-permute-start(f32[64,64]{0,1:T(8,128)S(1)} %add_add_fusion.1), channel_id=1, source_target_pairs={{0,16},{1,17},{2,18},{3,19},{4,20},{5,21},{6,22},{7,23},{8,24},{9,... | collective-permute-start | bytes 49160 | tf_op jit(solution)/shard_map/ppermute | solution.py:15
  300.7 5.5 %collective-permute-start.9 = (f32[64,64]{0,1:T(8,128)S(1)}, f32[64,64]{0,1:T(8,128)S(1)}, u32[]{:S(2)}, u32[]{:S(2)}) collective-permute-start(f32[64,64]{0,1:T(8,128)S(1)} %add_add_fusion), channel_id=1, source_target_pairs={{0,64},{1,65},{2,66},{3,67},{4,68},{5,69},{6,70},{7,71},{8,72},{9,... | collective-permute-start | bytes 49160 | tf_op jit(solution)/shard_map/ppermute | solution.py:21
Sparse Core Ops, SparseCore 0:
  11.0 143.3 all-gather.4
  158.0 78.5 all-gather.6

commit v4 on v2

--- a/solution.py
+++ b/solution.py
@@ -142,7 +142,9 @@
 
     scaled_t = scaled.T
     live_i = live.astype(jnp.int32)
-    inv_all = lax.all_gather(inv_root, AXES, axis=0)
+    inv_all = lax.all_to_all(
+        jnp.broadcast_to(inv_root[None, :], (peer_count, rows_dev)), AXES, split_axis=0, concat_axis=0, tiled=True
+    )
     terms = mirror_terms(tiles, tile_row, live_i, scaled_t)
     terms, inv_all = lax.optimization_barrier((terms, inv_all))
     got_terms = lax.all_to_all(terms, AXES, split_axis=0, concat_axis=0, tiled=True)

time: 262 us -> 242 us (0.924)
  blocking collectives: 33.6 us -> 0 us
  waiting for transfers between devices: 90.3 us -> 96.2 us
  starting transfers between devices: 35.9 us -> 41.6 us
    all_gather x1 -> x0, blocking collectives: 33.6 us -> none  [shards(): inv_all = lax.all_gather(inv_root, AXES, axis=0)]
    all_gather x1, waiting for transfers between devices: 0.02 us -> 13.3 us  [shards(): vec_all = lax.all_gather(vec_t, AXES, axis=0)]
    all_to_all x1, waiting for transfers between devices: 65.8 us -> 52.5 us  [shards(): lax.all_to_all(terms, AXES, split_axis=0, concat_axis=0, tiled=True)]
    all_to_all x0 -> x1, starting transfers between devices: none -> 4.77 us  [shards(): lax.all_to_all(jnp.broadcast_to(inv_root[None, :], (peer_count, rows_dev)...]
    ppermute x1, starting transfers between devices: 4.34 us -> 0.09 us  [butterfly_sum(): x = x + lax.ppermute(x, AXES, [(i, i ^ step) for i in range(peer_count)])]
    all_to_all x1, starting transfers between devices: 6.3 us -> 10.4 us  [shards(): lax.all_to_all(terms, AXES, split_axis=0, concat_axis=0, tiled=True)]
    ppermute x1, waiting for transfers between devices: 1.89 us -> 5.41 us  [butterfly_sum(): x = x + lax.ppermute(x, AXES, [(i, i ^ step) for i in range(peer_count)])]
  transfers between devices with their start and end apart: 13 -> 14, of which waited for: 10 -> 13; matrix products, arithmetic and copies ran while one was open for 10% -> 12% of each run, Pallas kernels for 15% -> 16%
where the time goes in v4:
time: 242 us; the launch traced here: 241 us
  waiting for transfers between devices  96.2 us (40%)
  starting transfers between devices  41.6 us (17%)
  Pallas kernels  39.4 us (16%)
  other arithmetic  34.9 us (14%)
  between operations  14.2 us (6%)
  matrix products  10.8 us (4%)
  local copies, waits for them, and re-layouts  3.41 us (1%)
    all_to_all x1, waiting for transfers between devices, shards(): lax.all_to_all(terms, AXES, split_axis=0, concat_axis=0, tiled=True)  52.5 us
    pallas_call x1, Pallas kernels, forward_product(): pl.pallas_call(forward_kernel, grid_spec=pltpu.PrefetchScalarGridSpec(num...  21.8 us
    pallas_call x1, Pallas kernels, mirror_terms(): pl.pallas_call(terms_kernel, grid_spec=pltpu.PrefetchScalarGridSpec(num_s...  17.6 us
    all_gather x1, waiting for transfers between devices, shards(): vec_all = lax.all_gather(vec_t, AXES, axis=0)  13.3 us
    all_to_all x1, starting transfers between devices, shards(): got = lax.all_to_all(payload, AXES, split_axis=0, concat_axis=0, tiled=True)  11.1 us
    all_to_all x1, waiting for transfers between devices, shards(): got = lax.all_to_all(payload, AXES, split_axis=0, concat_axis=0, tiled=True)  10.7 us
    all_to_all x1, starting transfers between devices, shards(): lax.all_to_all(terms, AXES, split_axis=0, concat_axis=0, tiled=True)  10.4 us
    reduce_sum x1, other arithmetic, shards(): col_sums = jnp.sum(tiles, axis=1, dtype=jnp.float32)  10.2 us
  transfers between devices with their start and end apart: 14, of which 13 were waited for; matrix products, arithmetic and copies ran while one was open for 12% of the time, Pallas kernels for 16%

profile of v4, /device:TPU:0, one launch (start us, length us, event | category | flops | bytes accessed | tf_op | source)
XLA Modules:
  0.0 240.6 jit_solution(11431155848496159902)
XLA Ops:
  7.9 0.8 eq.49
  8.8 0.8 fusion.20
  9.6 10.2 %convert_reduce_fusion = (f32[512,128]{1,0:T(8,128)S(1)}, f32[512,128]{1,0:T(8,128)S(1)}) fusion(bf16[512,128,128]{2,1,0:T(8,128)(2,1)} %tiles_ref.3), kind=kLoop, calls=%fused_computation | loop fusion | flops 25034752 | bytes 17301504 | tf_op jit(solution)/shard_map/reduce_sum | solution.py:124
  20.6 0.9 copy.32
  21.5 11.1 %all-to-all-start = ((f32[128,1,516]{2,1,0:T(1,128)}), f32[128,1,516]{2,1,0:T(1,128)S(1)}, u32[]{:S(2)}, u32[]{:S(2)}) async-start(f32[128,1,516]{2,1,0:T(1,128)} %copy.32), calls=%async_computation | async-start | bytes 655360 | tf_op jit(solution)/shard_map/all_to_all | solution.py:135
  33.4 10.7 %all-to-all-done = f32[128,1,516]{2,1,0:T(1,128)S(1)} async-done(((f32[128,1,516]{2,1,0:T(1,128)}), f32[128,1,516]{2,1,0:T(1,128)S(1)}, u32[]{:S(2)}, u32[]{:S(2)}) %all-to-all-start) | async-done | bytes 264224 | tf_op jit(solution)/shard_map/all_to_all | solution.py:135
  44.4 1.1 fusion.41
  45.5 0.8 broadcast_in_dim.6
  46.3 4.8 %all-to-all-start.1 = ((f32[128,1,512]{2,1,0:T(1,128)}), f32[128,1,512]{2,1,0:T(1,128)S(1)}, u32[]{:S(2)}, u32[]{:S(2)}) async-start(f32[128,1,512]{2,1,0:T(1,128)} %broadcast_in_dim.6), calls=%async_computation.1 | async-start | bytes 524288 | tf_op jit(solution)/shard_map/all_to_all | solution.py:145
  51.7 17.6 %shard_map.68 = bf16[512,64,128]{2,1,0:T(8,128)(2,1)} custom-call(s32[512]{0:T(512)} %rows_ref.3, s32[512]{0:T(512)} %get-tuple-element.12.live_ref, bf16[512,128,128]{2,1,0:T(8,128)(2,1)} %tiles_ref.3, bf16[64,512]{1,0:T(8,128)(2,1)} %fusion.21.own_ref), custom_call_target="tpu_custom_call" | custom-call | tf_op jit(solution)/shard_map/pallas_call | solution.py:47
  69.4 10.4 %all-to-all-start.2 = ((bf16[512,64,128]{2,1,0:T(8,128)(2,1)}), bf16[512,64,128]{2,1,0:T(8,128)(2,1)}, u32[]{:S(2)}, u32[]{:S(2)}) async-start(bf16[512,64,128]{2,1,0:T(8,128)(2,1)} %shard_map.68), calls=%async_computation.2 | async-start | bytes 16777216 | tf_op jit(solution)/shard_map/all_to_all | solution.py:150
  80.5 13.3 %all-gather.3.cloned.1.call-done = bf16[8192,512]{1,0:T(8,128)(2,1)} async-done(((bf16[64,512]{1,0:T(8,128)(2,1)}), bf16[8192,512]{1,0:T(8,128)(2,1)}) %all-gather.3.cloned.1.call-update) | async-done | bytes 8388624 | tf_op jit(solution)/shard_map/all_gather | solution.py:115
  93.8 9.9 %fusion.all_ref = bf16[128,64,512]{2,1,0:T(8,128)(2,1)} fusion(bf16[128,64,512]{2,1,0:T(8,128)(2,1)} %bitcast.50, f32[128,512]{1,0:T(8,128)S(1)} %bitcast.54), kind=kLoop, calls=%fused_computation.3 | loop fusion | flops 12582912 | bytes 17039360 | tf_op jit(solution)/shard_map/convert_element_type | solution.py:152
  103.8 21.8 %shard_map.69 = f32[4,64,128]{2,1,0:T(8,128)} custom-call(s32[512]{0:T(512)} %add_select_fusion.1.places_ref, s32[512]{0:T(512)} %cols_ref.1, s32[512]{0:T(512)} %rows_ref.3, s32[512]{0:T(512)} %get-tuple-element.12.live_ref, bf16[512,128,128]{2,1,0:T(8,128)(2,1)} %tiles_ref.3, bf16[128,64,512]{2,1,0:T(8,128)(2,1)} %fusion.all_ref), custom_call_target="tpu_custom_call" | custom-call | tf_op jit(solution)/shard_map/pallas_call | solution.py:87
  125.5 52.5 %all-to-all-done.2 = bf16[512,64,128]{2,1,0:T(8,128)(2,1)} async-done(((bf16[512,64,128]{2,1,0:T(8,128)(2,1)}), bf16[512,64,128]{2,1,0:T(8,128)(2,1)}, u32[]{:S(2)}, u32[]{:S(2)}) %all-to-all-start.2) | async-done | bytes 8388640 | tf_op jit(solution)/shard_map/all_to_all | solution.py:150
  178.1 7.8 %fusion.1 = f32[4,64,128]{2,0,1:T(4,128)S(1)} fusion(bf16[512,64,128]{2,1,0:T(8,128)(2,1)} %all-to-all-done.2, s32[512]{0:T(512)S(1)} %eq.53), kind=kOutput, calls=%fused_computation.4 | convolution fusion | flops 33556480 | bytes 8521728 | tf_op jit(solution)/shard_map/tr,tka->rka/dot_general | solution.py:157
  186.2 3.3 %collective-permute-start.1 = (f32[64,64]{0,1:T(8,128)S(1)}, f32[64,64]{0,1:T(8,128)S(1)}, u32[]{:S(2)}, u32[]{:S(2)}) collective-permute-start(f32[64,64]{0,1:T(8,128)S(1)} %fusion.18), channel_id=1, source_target_pairs={{0,2},{1,3},{2,0},{3,1},{4,6},{5,7},{6,4},{7,5},{8,10},{9,11},{10,... | collective-permute-start | bytes 49160 | tf_op jit(solution)/shard_map/ppermute | solution.py:16
  189.5 1.2 collective-permute-start
  191.5 2.6 %collective-permute-done.2 = f32[64,64]{0,1:T(8,128)S(1)} collective-permute-done((f32[64,64]{0,1:T(8,128)S(1)}, f32[64,64]{0,1:T(8,128)S(1)}, u32[]{:S(2)}, u32[]{:S(2)}) %collective-permute-start.2) | collective-permute-done | bytes 16416 | tf_op jit(solution)/shard_map/ppermute | solution.py:17
  194.2 4.8 %collective-permute-start.5 = (f32[64,64]{0,1:T(8,128)S(1)}, f32[64,64]{0,1:T(8,128)S(1)}, u32[]{:S(2)}, u32[]{:S(2)}) collective-permute-start(f32[64,64]{0,1:T(8,128)S(1)} %add_add_fusion.2), channel_id=1, source_target_pairs={{0,12},{1,13},{2,14},{3,15},{4,8},{5,9},{6,10},{7,11},{8,4},{9,5},... | collective-permute-start | bytes 49160 | tf_op jit(solution)/shard_map/ppermute | solution.py:17
  199.6 1.2 collective-permute-done.5
  200.9 2.0 collective-permute-done.4
  202.9 1.5 collective-permute-done.3
  204.4 3.0 %collective-permute-start.8 = (f32[64,64]{0,1:T(8,128)S(1)}, f32[64,64]{0,1:T(8,128)S(1)}, u32[]{:S(2)}, u32[]{:S(2)}) collective-permute-start(f32[64,64]{0,1:T(8,128)S(1)} %add_add_fusion.1), channel_id=1, source_target_pairs={{0,48},{1,49},{2,50},{3,51},{4,52},{5,53},{6,54},{7,55},{8,56},{9,... | collective-permute-start | bytes 49160 | tf_op jit(solution)/shard_map/ppermute | solution.py:17
  207.5 2.2 collective-permute-start.7
  209.6 1.2 collective-permute-done.8
  210.8 0.7 collective-permute-done.7
  211.5 3.5 %collective-permute-done.6 = f32[64,64]{0,1:T(8,128)S(1)} collective-permute-done((f32[64,64]{0,1:T(8,128)S(1)}, f32[64,64]{0,1:T(8,128)S(1)}, u32[]{:S(2)}, u32[]{:S(2)}) %collective-permute-start.6) | collective-permute-done | bytes 16416 | tf_op jit(solution)/shard_map/ppermute | solution.py:15
  215.2 5.4 %collective-permute-done.9 = f32[64,64]{0,1:T(8,128)S(1)} collective-permute-done((f32[64,64]{0,1:T(8,128)S(1)}, f32[64,64]{0,1:T(8,128)S(1)}, u32[]{:S(2)}, u32[]{:S(2)}) %collective-permute-start.9) | collective-permute-done | bytes 16416 | tf_op jit(solution)/shard_map/ppermute | solution.py:21
  220.7 5.8 %cholesky.16 = f32[64,64]{1,0:T(8,128)S(1)} custom-call(f32[64,64]{1,0:T(8,128)S(1)} %fusion.29), custom_call_target="Cholesky" | custom-call | tf_op jit(solution)/shard_map/jit(cholesky)/cholesky | solution.py:163
  227.9 4.9 %custom-call.7 = f32[1,64,64]{1,2,0:T(8,128)S(1)} custom-call(f32[1,64,64]{2,1,0:T(8,128)S(1)} %fusion.27), custom_call_target="InvertDiagBlocksLowerTriangular" | custom-call | tf_op jit(solution)/shard_map/jit(_solve_triangular)/triangular_solve | solution.py:164
  232.8 1.0 fusion.16
  (44 shorter events, 7.4 us)
Async XLA Ops:
  7.2 86.7 %all-gather.3.cloned.1.call-start = ((), (), s32[]{:S(2)}) async-start(), calls=%async_computation.3 | async-start | bytes 8454144 | tf_op jit(solution)/shard_map/all_gather | solution.py:115
  9.5 23.1 %copy-start.3 = (s32[128]{0:T(128)S(1)}, s32[128]{0:T(128)}, u32[]{:S(2)}) copy-start(s32[128]{0:T(128)} %param.8) | copy-start | bytes 1540
  9.5 34.8 %copy-start.2 = (s32[512]{0:T(512)S(1)}, s32[512]{0:T(512)}, u32[]{:S(2)}) copy-start(s32[512]{0:T(512)} %rows_ref.3) | copy-start | bytes 6148
  9.6 41.5 %copy-start.1 = (bf16[512,64]{0,1:T(8,128)(2,1)S(1)}, bf16[512,64]{0,1:T(8,128)(2,1)}, u32[]{:S(2)}) copy-start(bf16[512,64]{0,1:T(8,128)(2,1)} %param.9) | copy-start | bytes 196612
  21.5 22.6 %all-to-all-start = ((f32[128,1,516]{2,1,0:T(1,128)}), f32[128,1,516]{2,1,0:T(1,128)S(1)}, u32[]{:S(2)}, u32[]{:S(2)}) async-start(f32[128,1,516]{2,1,0:T(1,128)} %copy.32), calls=%async_computation | async-start | bytes 655360 | tf_op jit(solution)/shard_map/all_to_all | solution.py:135
  46.3 23.0 %all-to-all-start.1 = ((f32[128,1,512]{2,1,0:T(1,128)}), f32[128,1,512]{2,1,0:T(1,128)S(1)}, u32[]{:S(2)}, u32[]{:S(2)}) async-start(f32[128,1,512]{2,1,0:T(1,128)} %broadcast_in_dim.6), calls=%async_computation.1 | async-start | bytes 524288 | tf_op jit(solution)/shard_map/all_to_all | solution.py:145
  69.4 108.7 %all-to-all-start.2 = ((bf16[512,64,128]{2,1,0:T(8,128)(2,1)}), bf16[512,64,128]{2,1,0:T(8,128)(2,1)}, u32[]{:S(2)}, u32[]{:S(2)}) async-start(bf16[512,64,128]{2,1,0:T(8,128)(2,1)} %shard_map.68), calls=%async_computation.2 | async-start | bytes 16777216 | tf_op jit(solution)/shard_map/all_to_all | solution.py:150
  125.5 60.4 %copy-start = (f32[4,64,128]{2,1,0:T(8,128)S(1)}, f32[4,64,128]{2,1,0:T(8,128)}, u32[]{:S(2)}) copy-start(f32[4,64,128]{2,1,0:T(8,128)} %shard_map.69) | copy-start | bytes 393220
  186.2 5.2 %collective-permute-start.1 = (f32[64,64]{0,1:T(8,128)S(1)}, f32[64,64]{0,1:T(8,128)S(1)}, u32[]{:S(2)}, u32[]{:S(2)}) collective-permute-start(f32[64,64]{0,1:T(8,128)S(1)} %fusion.18), channel_id=1, source_target_pairs={{0,2},{1,3},{2,0},{3,1},{4,6},{5,7},{6,4},{7,5},{8,10},{9,11},{10,... | collective-permute-start | bytes 49160 | tf_op jit(solution)/shard_map/ppermute | solution.py:16
  189.5 2.0 collective-permute-start
  190.6 3.5 %collective-permute-start.2 = (f32[64,64]{0,1:T(8,128)S(1)}, f32[64,64]{0,1:T(8,128)S(1)}, u32[]{:S(2)}, u32[]{:S(2)}) collective-permute-start(f32[64,64]{0,1:T(8,128)S(1)} %fusion.18), channel_id=1, source_target_pairs={{0,3},{1,2},{2,1},{3,0},{4,7},{5,6},{6,5},{7,4},{8,11},{9,10},{10,... | collective-permute-start | bytes 49160 | tf_op jit(solution)/shard_map/ppermute | solution.py:17
  194.2 6.7 %collective-permute-start.5 = (f32[64,64]{0,1:T(8,128)S(1)}, f32[64,64]{0,1:T(8,128)S(1)}, u32[]{:S(2)}, u32[]{:S(2)}) collective-permute-start(f32[64,64]{0,1:T(8,128)S(1)} %add_add_fusion.2), channel_id=1, source_target_pairs={{0,12},{1,13},{2,14},{3,15},{4,8},{5,9},{6,10},{7,11},{8,4},{9,5},... | collective-permute-start | bytes 49160 | tf_op jit(solution)/shard_map/ppermute | solution.py:17
  199.0 3.9 %collective-permute-start.4 = (f32[64,64]{0,1:T(8,128)S(1)}, f32[64,64]{0,1:T(8,128)S(1)}, u32[]{:S(2)}, u32[]{:S(2)}) collective-permute-start(f32[64,64]{0,1:T(8,128)S(1)} %add_add_fusion.2), channel_id=1, source_target_pairs={{0,8},{1,9},{2,10},{3,11},{4,12},{5,13},{6,14},{7,15},{8,0},{9,1},... | collective-permute-start | bytes 49160 | tf_op jit(solution)/shard_map/ppermute | solution.py:16
  199.0 5.4 %collective-permute-start.3 = (f32[64,64]{0,1:T(8,128)S(1)}, f32[64,64]{0,1:T(8,128)S(1)}, u32[]{:S(2)}, u32[]{:S(2)}) collective-permute-start(f32[64,64]{0,1:T(8,128)S(1)} %add_add_fusion.2), channel_id=1, source_target_pairs={{0,4},{1,5},{2,6},{3,7},{4,0},{5,1},{6,2},{7,3},{8,12},{9,13},{10,... | collective-permute-start | bytes 49160 | tf_op jit(solution)/shard_map/ppermute | solution.py:15
  204.4 6.4 %collective-permute-start.8 = (f32[64,64]{0,1:T(8,128)S(1)}, f32[64,64]{0,1:T(8,128)S(1)}, u32[]{:S(2)}, u32[]{:S(2)}) collective-permute-start(f32[64,64]{0,1:T(8,128)S(1)} %add_add_fusion.1), channel_id=1, source_target_pairs={{0,48},{1,49},{2,50},{3,51},{4,52},{5,53},{6,54},{7,55},{8,56},{9,... | collective-permute-start | bytes 49160 | tf_op jit(solution)/shard_map/ppermute | solution.py:17
  207.5 4.1 %collective-permute-start.7 = (f32[64,64]{0,1:T(8,128)S(1)}, f32[64,64]{0,1:T(8,128)S(1)}, u32[]{:S(2)}, u32[]{:S(2)}) collective-permute-start(f32[64,64]{0,1:T(8,128)S(1)} %add_add_fusion.1), channel_id=1, source_target_pairs={{0,32},{1,33},{2,34},{3,35},{4,36},{5,37},{6,38},{7,39},{8,40},{9,... | collective-permute-start | bytes 49160 | tf_op jit(solution)/shard_map/ppermute | solution.py:16
  209.6 5.4 %collective-permute-start.6 = (f32[64,64]{0,1:T(8,128)S(1)}, f32[64,64]{0,1:T(8,128)S(1)}, u32[]{:S(2)}, u32[]{:S(2)}) collective-permute-start(f32[64,64]{0,1:T(8,128)S(1)} %add_add_fusion.1), channel_id=1, source_target_pairs={{0,16},{1,17},{2,18},{3,19},{4,20},{5,21},{6,22},{7,23},{8,24},{9,... | collective-permute-start | bytes 49160 | tf_op jit(solution)/shard_map/ppermute | solution.py:15
  215.1 5.5 %collective-permute-start.9 = (f32[64,64]{0,1:T(8,128)S(1)}, f32[64,64]{0,1:T(8,128)S(1)}, u32[]{:S(2)}, u32[]{:S(2)}) collective-permute-start(f32[64,64]{0,1:T(8,128)S(1)} %add_add_fusion), channel_id=1, source_target_pairs={{0,64},{1,65},{2,66},{3,67},{4,68},{5,69},{6,70},{7,71},{8,72},{9,... | collective-permute-start | bytes 49160 | tf_op jit(solution)/shard_map/ppermute | solution.py:21
Sparse Core Ops, SparseCore 0:
  11.0 82.7 all-gather.2

commit v5 on v4

--- a/solution.py
+++ b/solution.py
@@ -99,6 +99,38 @@
     )(places, cols, rows, live, tiles, scaled_all_t)
 
 
+MIRROR_GROUP = 64
+
+
+def mirror_kernel(cols_ref, got_ref, out_ref):
+    step = pl.program_id(0)
+
+    @pl.when(step == 0)
+    def _():
+        out_ref[...] = jnp.zeros_like(out_ref)
+
+    def body(j, carry):
+        c = cols_ref[step * MIRROR_GROUP + j]
+        out_ref[c] += got_ref[j].astype(jnp.float32)
+        return carry
+
+    lax.fori_loop(0, MIRROR_GROUP, body, 0, unroll=True)
+
+
+def mirror_sum(cols, got_terms, block_count):
+    slots, width, size = got_terms.shape
+    return pl.pallas_call(
+        mirror_kernel,
+        grid_spec=pltpu.PrefetchScalarGridSpec(
+            num_scalar_prefetch=1,
+            grid=(slots // MIRROR_GROUP,),
+            in_specs=[pl.BlockSpec((MIRROR_GROUP, width, size), lambda i, c: (i, 0, 0))],
+            out_specs=pl.BlockSpec((block_count, width, size), lambda i, c: (0, 0, 0)),
+        ),
+        out_shape=jax.ShapeDtypeStruct((block_count, width, size), jnp.float32),
+    )(cols, got_terms)
+
+
 def shards(tiles, tile_row, tile_col, counts, vectors):
     peer_count = lax.axis_size(AXES)
     outer_count = lax.axis_size("outer")
@@ -145,16 +177,17 @@
     inv_all = lax.all_to_all(
         jnp.broadcast_to(inv_root[None, :], (peer_count, rows_dev)), AXES, split_axis=0, concat_axis=0, tiled=True
     )
-    terms = mirror_terms(tiles, tile_row, live_i, scaled_t)
+    terms = mirror_terms(tiles, jnp.clip(tile_row, 0, block_count - 1), live_i, scaled_t)
     terms, inv_all = lax.optimization_barrier((terms, inv_all))
     got_terms = lax.all_to_all(terms, AXES, split_axis=0, concat_axis=0, tiled=True)
 
     scaled_all_t = (inv_all[:, None, :] * vec_all.astype(jnp.float32)).astype(jnp.bfloat16)
     place = jnp.arange(slot_total, dtype=jnp.int32) // slot_count
-    forward = forward_product(tiles, place, tile_col, tile_row, live_i, scaled_all_t, block_count)
+    row_idx = jnp.clip(tile_row, 0, block_count - 1)
+    col_idx = jnp.clip(tile_col, 0, block_count - 1)
+    forward = forward_product(tiles, place, col_idx, row_idx, live_i, scaled_all_t, block_count)
     forward, got_terms = lax.optimization_barrier((forward, got_terms))
-    got_hot = (got_cols[:, None] == block_ids).astype(jnp.bfloat16)
-    mirror = jnp.einsum("tr,tka->rka", got_hot, got_terms, preferred_element_type=jnp.float32)
+    mirror = mirror_sum(jnp.clip(got_cols, 0, block_count - 1), got_terms, block_count)
     total_t = (forward + mirror).transpose(1, 0, 2).reshape(vec_width, rows_dev)
 
     image_t = inv_root[None, :] * (total_t + scaled_t.astype(jnp.float32))

time: 242 us -> 243 us (level)
  Pallas kernels: 39.4 us -> 48.2 us
  waiting for transfers between devices: 96.2 us -> 89.8 us
  matrix products: 10.8 us -> 5.04 us
  starting transfers between devices: 41.6 us -> 45.1 us
    all_gather x1, waiting for transfers between devices: 13.3 us -> 4.58 us  [shards(): vec_all = lax.all_gather(vec_t, AXES, axis=0)]
    pallas_call x0 -> x1, Pallas kernels: none -> 8.63 us  [mirror_sum(): pl.pallas_call(mirror_kernel, grid_spec=pltpu.PrefetchScalarGridSpec(num_...]
    all_to_all x1, waiting for transfers between devices: 52.5 us -> 60.7 us  [shards(): lax.all_to_all(terms, AXES, split_axis=0, concat_axis=0, tiled=True)]
    dot_general x1 -> x0, matrix products: 7.83 us -> none  [shards(): jnp.einsum('tr,tka->rka', got_hot, got_terms, preferred_element_type=jnp....]
    ppermute x1, starting transfers between devices: 0.09 us -> 4.35 us  [butterfly_sum(): x = x + lax.ppermute(x, AXES, [(i, i ^ step) for i in range(peer_count)])]
    ppermute x1, waiting for transfers between devices: 5.41 us -> 1.89 us  [butterfly_sum(): x = x + lax.ppermute(x, AXES, [(i, i ^ step) for i in range(peer_count)])]
  transfers between devices with their start and end apart: 14 -> 14, of which waited for: 13 -> 11; matrix products, arithmetic and copies ran while one was open for 12% -> 12% of each run, Pallas kernels for 16% -> 16%
where the time goes in v5:
time: 243 us; the launch traced here: 242 us
  waiting for transfers between devices  89.8 us (37%)
  Pallas kernels  48.2 us (20%)
  starting transfers between devices  45.1 us (19%)
  other arithmetic  35.4 us (15%)
  between operations  14.2 us (6%)
  matrix products  5.04 us (2%)
  local copies, waits for them, and re-layouts  4.11 us (2%)
    all_to_all x1, waiting for transfers between devices, shards(): lax.all_to_all(terms, AXES, split_axis=0, concat_axis=0, tiled=True)  60.7 us
    pallas_call x1, Pallas kernels, forward_product(): pl.pallas_call(forward_kernel, grid_spec=pltpu.PrefetchScalarGridSpec(num...  21.8 us
    pallas_call x1, Pallas kernels, mirror_terms(): pl.pallas_call(terms_kernel, grid_spec=pltpu.PrefetchScalarGridSpec(num_s...  17.8 us
    all_to_all x1, starting transfers between devices, shards(): got = lax.all_to_all(payload, AXES, split_axis=0, concat_axis=0, tiled=True)  11.1 us
    all_to_all x1, waiting for transfers between devices, shards(): got = lax.all_to_all(payload, AXES, split_axis=0, concat_axis=0, tiled=True)  10.7 us
    all_to_all x1, starting transfers between devices, shards(): lax.all_to_all(terms, AXES, split_axis=0, concat_axis=0, tiled=True)  10.3 us
    reduce_sum x1, other arithmetic, shards(): col_sums = jnp.sum(tiles, axis=1, dtype=jnp.float32)  10.2 us
    convert_element_type x1, other arithmetic, shards(): (inv_all[:, None, :] * vec_all.astype(jnp.float32)).astype(jnp.bfloat16)  9.93 us
  transfers between devices with their start and end apart: 14, of which 11 were waited for; matrix products, arithmetic and copies ran while one was open for 12% of the time, Pallas kernels for 16%

profile of v5, /device:TPU:0, one launch (start us, length us, event | category | flops | bytes accessed | tf_op | source)
XLA Modules:
  0.0 241.9 jit_solution(13570225026498524814)
XLA Ops:
  9.6 10.2 %convert_reduce_fusion = (f32[512,128]{1,0:T(8,128)S(1)}, f32[512,128]{1,0:T(8,128)S(1)}) fusion(bf16[512,128,128]{2,1,0:T(8,128)(2,1)} %tiles_ref.3), kind=kLoop, calls=%fused_computation | loop fusion | flops 25034752 | bytes 17301504 | tf_op jit(solution)/shard_map/reduce_sum | solution.py:156
  20.6 0.9 copy.28
  21.5 11.1 %all-to-all-start = ((f32[128,1,516]{2,1,0:T(1,128)}), f32[128,1,516]{2,1,0:T(1,128)S(1)}, u32[]{:S(2)}, u32[]{:S(2)}) async-start(f32[128,1,516]{2,1,0:T(1,128)} %copy.28), calls=%async_computation | async-start | bytes 655360 | tf_op jit(solution)/shard_map/all_to_all | solution.py:167
  33.4 10.7 %all-to-all-done = f32[128,1,516]{2,1,0:T(1,128)S(1)} async-done(((f32[128,1,516]{2,1,0:T(1,128)}), f32[128,1,516]{2,1,0:T(1,128)S(1)}, u32[]{:S(2)}, u32[]{:S(2)}) %all-to-all-start) | async-done | bytes 264224 | tf_op jit(solution)/shard_map/all_to_all | solution.py:167
  44.4 1.1 fusion.36
  45.5 0.8 broadcast_in_dim.6
  46.3 4.8 %all-to-all-start.1 = ((f32[128,1,512]{2,1,0:T(1,128)}), f32[128,1,512]{2,1,0:T(1,128)S(1)}, u32[]{:S(2)}, u32[]{:S(2)}) async-start(f32[128,1,512]{2,1,0:T(1,128)} %broadcast_in_dim.6), calls=%async_computation.1 | async-start | bytes 524288 | tf_op jit(solution)/shard_map/all_to_all | solution.py:177
  52.3 17.8 %shard_map.68 = bf16[512,64,128]{2,1,0:T(8,128)(2,1)} custom-call(s32[512]{0:T(512)} %broadcast_clamp_fusion.rows_ref, s32[512]{0:T(512)} %get-tuple-element.12.live_ref, bf16[512,128,128]{2,1,0:T(8,128)(2,1)} %tiles_ref.3, bf16[64,512]{1,0:T(8,128)(2,1)} %fusion.17.own_ref), custom_call_target="tpu_custom_call" | custom-call | tf_op jit(solution)/shard_map/pallas_call | solution.py:47
  70.2 10.3 %all-to-all-start.2 = ((bf16[512,64,128]{2,1,0:T(8,128)(2,1)}), bf16[512,64,128]{2,1,0:T(8,128)(2,1)}, u32[]{:S(2)}, u32[]{:S(2)}) async-start(bf16[512,64,128]{2,1,0:T(8,128)(2,1)} %shard_map.68), calls=%async_computation.2 | async-start | bytes 16777216 | tf_op jit(solution)/shard_map/all_to_all | solution.py:182
  81.9 4.6 %all-gather.3.cloned.1.call-done = bf16[8192,512]{1,0:T(8,128)(2,1)} async-done(((bf16[64,512]{1,0:T(8,128)(2,1)}), bf16[8192,512]{1,0:T(8,128)(2,1)}) %all-gather.3.cloned.1.call-update) | async-done | bytes 8388624 | tf_op jit(solution)/shard_map/all_gather | solution.py:147
  86.5 9.9 %fusion.all_ref = bf16[128,64,512]{2,1,0:T(8,128)(2,1)} fusion(bf16[128,64,512]{2,1,0:T(8,128)(2,1)} %bitcast.47, f32[128,512]{1,0:T(8,128)S(1)} %bitcast.51), kind=kLoop, calls=%fused_computation.3 | loop fusion | flops 12582912 | bytes 17039360 | tf_op jit(solution)/shard_map/convert_element_type | solution.py:184
  96.4 21.8 %shard_map.69 = f32[4,64,128]{2,1,0:T(8,128)} custom-call(s32[512]{0:T(512)} %get-tuple-element.16.places_ref, s32[512]{0:T(512)} %get-tuple-element.17.cols_ref, s32[512]{0:T(512)} %broadcast_clamp_fusion.rows_ref, s32[512]{0:T(512)} %get-tuple-element.12.live_ref, bf16[512,128,128]{2,1,0:T(8,128)(2,1)} %tiles_ref.3, bf16[128,64,512]{2,1,0:T(8,128)(2,1)} %fusion.all_ref), custom_call_target="tpu_custom_call" | custom-call | tf_op jit(solution)/shard_map/pallas_call | solution.py:87
  118.2 60.7 %all-to-all-done.2.got_ref = bf16[512,64,128]{2,1,0:T(8,128)(2,1)} async-done(((bf16[512,64,128]{2,1,0:T(8,128)(2,1)}), bf16[512,64,128]{2,1,0:T(8,128)(2,1)}, u32[]{:S(2)}, u32[]{:S(2)}) %all-to-all-start.2) | async-done | bytes 8388640 | tf_op jit(solution)/shard_map/all_to_all | solution.py:182
  178.9 8.6 %shard_map.70 = f32[4,64,128]{2,1,0:T(8,128)} custom-call(s32[512]{0:T(512)} %min.21.cols_ref, bf16[512,64,128]{2,1,0:T(8,128)(2,1)} %all-to-all-done.2.got_ref), custom_call_target="tpu_custom_call" | custom-call | tf_op jit(solution)/shard_map/pallas_call | solution.py:122
  187.5 1.4 fusion.15
  188.9 3.6 %collective-permute-start.1 = (f32[64,64]{0,1:T(8,128)S(1)}, f32[64,64]{0,1:T(8,128)S(1)}, u32[]{:S(2)}, u32[]{:S(2)}) collective-permute-start(f32[64,64]{0,1:T(8,128)S(1)} %fusion.15), channel_id=1, source_target_pairs={{0,2},{1,3},{2,0},{3,1},{4,6},{5,7},{6,4},{7,5},{8,10},{9,11},{10,... | collective-permute-start | bytes 49160 | tf_op jit(solution)/shard_map/ppermute | solution.py:16
  192.8 1.7 collective-permute-done.1
  194.4 1.4 collective-permute-done.2
  195.9 4.9 %collective-permute-start.5 = (f32[64,64]{0,1:T(8,128)S(1)}, f32[64,64]{0,1:T(8,128)S(1)}, u32[]{:S(2)}, u32[]{:S(2)}) collective-permute-start(f32[64,64]{0,1:T(8,128)S(1)} %add_add_fusion.2), channel_id=1, source_target_pairs={{0,12},{1,13},{2,14},{3,15},{4,8},{5,9},{6,10},{7,11},{8,4},{9,5},... | collective-permute-start | bytes 49160 | tf_op jit(solution)/shard_map/ppermute | solution.py:17
  201.5 1.2 collective-permute-done.5
  202.7 2.0 collective-permute-done.4
  204.7 1.5 collective-permute-done.3
  206.2 0.9 collective-permute-start.8
  207.2 2.1 collective-permute-start.7
  209.3 2.1 collective-permute-start.6
  211.3 1.3 collective-permute-done.8
  212.7 2.0 collective-permute-done.6
  214.7 4.3 %collective-permute-start.9 = (f32[64,64]{0,1:T(8,128)S(1)}, f32[64,64]{0,1:T(8,128)S(1)}, u32[]{:S(2)}, u32[]{:S(2)}) collective-permute-start(f32[64,64]{0,1:T(8,128)S(1)} %add_add_fusion), channel_id=1, source_target_pairs={{0,64},{1,65},{2,66},{3,67},{4,68},{5,69},{6,70},{7,71},{8,72},{9,... | collective-permute-start | bytes 49160 | tf_op jit(solution)/shard_map/ppermute | solution.py:21
  219.0 1.9 collective-permute-done.9
  221.0 5.8 %cholesky.16 = f32[64,64]{1,0:T(8,128)S(1)} custom-call(f32[64,64]{1,0:T(8,128)S(1)} %fusion.22), custom_call_target="Cholesky" | custom-call | tf_op jit(solution)/shard_map/jit(cholesky)/cholesky | solution.py:196
  228.2 4.9 %custom-call.7 = f32[1,64,64]{1,2,0:T(8,128)S(1)} custom-call(f32[1,64,64]{2,1,0:T(8,128)S(1)} %fusion.20), custom_call_target="InvertDiagBlocksLowerTriangular" | custom-call | tf_op jit(solution)/shard_map/jit(_solve_triangular)/triangular_solve | solution.py:197
  233.1 2.0 fusion.13
  (46 shorter events, 9.1 us)
Async XLA Ops:
  7.2 44.5 %copy-start = (bf16[512,64]{0,1:T(8,128)(2,1)S(1)}, bf16[512,64]{0,1:T(8,128)(2,1)}, u32[]{:S(2)}) copy-start(bf16[512,64]{0,1:T(8,128)(2,1)} %param.9) | copy-start | bytes 196612
  7.2 25.5 %copy-start.3 = (s32[128]{0:T(128)S(1)}, s32[128]{0:T(128)}, u32[]{:S(2)}) copy-start(s32[128]{0:T(128)} %param.8) | copy-start | bytes 1540
  7.2 37.2 %copy-start.1 = (s32[512]{0:T(512)S(1)}, s32[512]{0:T(512)}, u32[]{:S(2)}) copy-start(s32[512]{0:T(512)} %param.6) | copy-start | bytes 6148
  7.2 79.3 %all-gather.3.cloned.1.call-start = ((), (), s32[]{:S(2)}) async-start(), calls=%async_computation.3 | async-start | bytes 8454144 | tf_op jit(solution)/shard_map/all_gather | solution.py:147
  21.5 22.6 %all-to-all-start = ((f32[128,1,516]{2,1,0:T(1,128)}), f32[128,1,516]{2,1,0:T(1,128)S(1)}, u32[]{:S(2)}, u32[]{:S(2)}) async-start(f32[128,1,516]{2,1,0:T(1,128)} %copy.28), calls=%async_computation | async-start | bytes 655360 | tf_op jit(solution)/shard_map/all_to_all | solution.py:167
  46.3 23.8 %all-to-all-start.1 = ((f32[128,1,512]{2,1,0:T(1,128)}), f32[128,1,512]{2,1,0:T(1,128)S(1)}, u32[]{:S(2)}, u32[]{:S(2)}) async-start(f32[128,1,512]{2,1,0:T(1,128)} %broadcast_in_dim.6), calls=%async_computation.1 | async-start | bytes 524288 | tf_op jit(solution)/shard_map/all_to_all | solution.py:177
  52.3 28.2 %copy-start.2 = (s32[512]{0:T(512)S(1)}, s32[512]{0:T(512)}, u32[]{:S(2)}) copy-start(s32[512]{0:T(512)} %param.7) | copy-start | bytes 6148
  70.2 108.7 %all-to-all-start.2 = ((bf16[512,64,128]{2,1,0:T(8,128)(2,1)}), bf16[512,64,128]{2,1,0:T(8,128)(2,1)}, u32[]{:S(2)}, u32[]{:S(2)}) async-start(bf16[512,64,128]{2,1,0:T(8,128)(2,1)} %shard_map.68), calls=%async_computation.2 | async-start | bytes 16777216 | tf_op jit(solution)/shard_map/all_to_all | solution.py:182
  188.9 5.5 %collective-permute-start.1 = (f32[64,64]{0,1:T(8,128)S(1)}, f32[64,64]{0,1:T(8,128)S(1)}, u32[]{:S(2)}, u32[]{:S(2)}) collective-permute-start(f32[64,64]{0,1:T(8,128)S(1)} %fusion.15), channel_id=1, source_target_pairs={{0,2},{1,3},{2,0},{3,1},{4,6},{5,7},{6,4},{7,5},{8,10},{9,11},{10,... | collective-permute-start | bytes 49160 | tf_op jit(solution)/shard_map/ppermute | solution.py:16
  192.5 1.9 collective-permute-start
  192.5 3.3 %collective-permute-start.2 = (f32[64,64]{0,1:T(8,128)S(1)}, f32[64,64]{0,1:T(8,128)S(1)}, u32[]{:S(2)}, u32[]{:S(2)}) collective-permute-start(f32[64,64]{0,1:T(8,128)S(1)} %fusion.15), channel_id=1, source_target_pairs={{0,3},{1,2},{2,1},{3,0},{4,7},{5,6},{6,5},{7,4},{8,11},{9,10},{10,... | collective-permute-start | bytes 49160 | tf_op jit(solution)/shard_map/ppermute | solution.py:17
  195.9 6.8 %collective-permute-start.5 = (f32[64,64]{0,1:T(8,128)S(1)}, f32[64,64]{0,1:T(8,128)S(1)}, u32[]{:S(2)}, u32[]{:S(2)}) collective-permute-start(f32[64,64]{0,1:T(8,128)S(1)} %add_add_fusion.2), channel_id=1, source_target_pairs={{0,12},{1,13},{2,14},{3,15},{4,8},{5,9},{6,10},{7,11},{8,4},{9,5},... | collective-permute-start | bytes 49160 | tf_op jit(solution)/shard_map/ppermute | solution.py:17
  200.8 3.9 %collective-permute-start.4 = (f32[64,64]{0,1:T(8,128)S(1)}, f32[64,64]{0,1:T(8,128)S(1)}, u32[]{:S(2)}, u32[]{:S(2)}) collective-permute-start(f32[64,64]{0,1:T(8,128)S(1)} %add_add_fusion.2), channel_id=1, source_target_pairs={{0,8},{1,9},{2,10},{3,11},{4,12},{5,13},{6,14},{7,15},{8,0},{9,1},... | collective-permute-start | bytes 49160 | tf_op jit(solution)/shard_map/ppermute | solution.py:16
  200.8 5.4 %collective-permute-start.3 = (f32[64,64]{0,1:T(8,128)S(1)}, f32[64,64]{0,1:T(8,128)S(1)}, u32[]{:S(2)}, u32[]{:S(2)}) collective-permute-start(f32[64,64]{0,1:T(8,128)S(1)} %add_add_fusion.2), channel_id=1, source_target_pairs={{0,4},{1,5},{2,6},{3,7},{4,0},{5,1},{6,2},{7,3},{8,12},{9,13},{10,... | collective-permute-start | bytes 49160 | tf_op jit(solution)/shard_map/ppermute | solution.py:15
  206.2 6.4 %collective-permute-start.8 = (f32[64,64]{0,1:T(8,128)S(1)}, f32[64,64]{0,1:T(8,128)S(1)}, u32[]{:S(2)}, u32[]{:S(2)}) collective-permute-start(f32[64,64]{0,1:T(8,128)S(1)} %add_add_fusion.1), channel_id=1, source_target_pairs={{0,48},{1,49},{2,50},{3,51},{4,52},{5,53},{6,54},{7,55},{8,56},{9,... | collective-permute-start | bytes 49160 | tf_op jit(solution)/shard_map/ppermute | solution.py:17
  207.2 5.5 %collective-permute-start.7 = (f32[64,64]{0,1:T(8,128)S(1)}, f32[64,64]{0,1:T(8,128)S(1)}, u32[]{:S(2)}, u32[]{:S(2)}) collective-permute-start(f32[64,64]{0,1:T(8,128)S(1)} %add_add_fusion.1), channel_id=1, source_target_pairs={{0,32},{1,33},{2,34},{3,35},{4,36},{5,37},{6,38},{7,39},{8,40},{9,... | collective-permute-start | bytes 49160 | tf_op jit(solution)/shard_map/ppermute | solution.py:16
  209.3 5.4 %collective-permute-start.6 = (f32[64,64]{0,1:T(8,128)S(1)}, f32[64,64]{0,1:T(8,128)S(1)}, u32[]{:S(2)}, u32[]{:S(2)}) collective-permute-start(f32[64,64]{0,1:T(8,128)S(1)} %add_add_fusion.1), channel_id=1, source_target_pairs={{0,16},{1,17},{2,18},{3,19},{4,20},{5,21},{6,22},{7,23},{8,24},{9,... | collective-permute-start | bytes 49160 | tf_op jit(solution)/shard_map/ppermute | solution.py:15
  214.7 6.2 %collective-permute-start.9 = (f32[64,64]{0,1:T(8,128)S(1)}, f32[64,64]{0,1:T(8,128)S(1)}, u32[]{:S(2)}, u32[]{:S(2)}) collective-permute-start(f32[64,64]{0,1:T(8,128)S(1)} %add_add_fusion), channel_id=1, source_target_pairs={{0,64},{1,65},{2,66},{3,67},{4,68},{5,69},{6,70},{7,71},{8,72},{9,... | collective-permute-start | bytes 49160 | tf_op jit(solution)/shard_map/ppermute | solution.py:21
Sparse Core Ops, SparseCore 0:
  11.0 75.4 all-gather.2

commit v6 on v4

--- a/solution.py
+++ b/solution.py
@@ -26,19 +26,19 @@
 GROUP = 32
 
 
+TERMS_GROUP = 256
+
+
 def terms_kernel(rows_ref, live_ref, tiles_ref, own_ref, out_ref):
     step = pl.program_id(0)
     size = tiles_ref.shape[1]
 
-    def body(j, carry):
-        t = step * GROUP + j
+    for j in range(TERMS_GROUP):
+        t = step * TERMS_GROUP + j
         start = pl.multiple_of(rows_ref[t] * size, size)
         block = own_ref[:, pl.ds(start, size)]
         term = jnp.dot(block, tiles_ref[j], preferred_element_type=jnp.float32).astype(out_ref.dtype)
         out_ref[j] = jnp.where(live_ref[t] > 0, term, jnp.zeros_like(term))
-        return carry
-
-    lax.fori_loop(0, GROUP, body, 0, unroll=True)
 
 
 def mirror_terms(tiles, rows, live, own_t):
@@ -48,12 +48,12 @@
         terms_kernel,
         grid_spec=pltpu.PrefetchScalarGridSpec(
             num_scalar_prefetch=2,
-            grid=(slots // GROUP,),
+            grid=(slots // TERMS_GROUP,),
             in_specs=[
-                pl.BlockSpec((GROUP, size, size), lambda i, r, l: (i, 0, 0)),
+                pl.BlockSpec((TERMS_GROUP, size, size), lambda i, r, l: (i, 0, 0)),
                 pl.BlockSpec(memory_space=pltpu.VMEM),
             ],
-            out_specs=pl.BlockSpec((GROUP, width, size), lambda i, r, l: (i, 0, 0)),
+            out_specs=pl.BlockSpec((TERMS_GROUP, width, size), lambda i, r, l: (i, 0, 0)),
         ),
         out_shape=jax.ShapeDtypeStruct((slots, width, size), jnp.bfloat16),
     )(rows, live, tiles, own_t)
@@ -145,13 +145,15 @@
     inv_all = lax.all_to_all(
         jnp.broadcast_to(inv_root[None, :], (peer_count, rows_dev)), AXES, split_axis=0, concat_axis=0, tiled=True
     )
-    terms = mirror_terms(tiles, tile_row, live_i, scaled_t)
+    terms = mirror_terms(tiles, jnp.clip(tile_row, 0, block_count - 1), live_i, scaled_t)
     terms, inv_all = lax.optimization_barrier((terms, inv_all))
     got_terms = lax.all_to_all(terms, AXES, split_axis=0, concat_axis=0, tiled=True)
 
     scaled_all_t = (inv_all[:, None, :] * vec_all.astype(jnp.float32)).astype(jnp.bfloat16)
     place = jnp.arange(slot_total, dtype=jnp.int32) // slot_count
-    forward = forward_product(tiles, place, tile_col, tile_row, live_i, scaled_all_t, block_count)
+    row_idx = jnp.clip(tile_row, 0, block_count - 1)
+    col_idx = jnp.clip(tile_col, 0, block_count - 1)
+    forward = forward_product(tiles, place, col_idx, row_idx, live_i, scaled_all_t, block_count)
     forward, got_terms = lax.optimization_barrier((forward, got_terms))
     got_hot = (got_cols[:, None] == block_ids).astype(jnp.bfloat16)
     mirror = jnp.einsum("tr,tka->rka", got_hot, got_terms, preferred_element_type=jnp.float32)

time: 242 us -> 263 us (1.087)
  waiting for transfers between devices: 96.2 us -> 112 us
  starting transfers between devices: 41.6 us -> 52.9 us
  Pallas kernels: 39.4 us -> 32.7 us
    all_gather x1, waiting for transfers between devices: 13.3 us -> 83.3 us  [shards(): vec_all = lax.all_gather(vec_t, AXES, axis=0)]
    all_to_all x1, waiting for transfers between devices: 52.5 us -> 0.01 us  [shards(): lax.all_to_all(terms, AXES, split_axis=0, concat_axis=0, tiled=True)]
    ppermute x3, starting transfers between devices: 7.94 us -> 24.7 us  [butterfly_sum(): lax.ppermute(x, AXES, [(i, i ^ 3 * step) for i in range(peer_count)])]
    pallas_call x1, Pallas kernels: 17.6 us -> 10.9 us  [mirror_terms(): pl.pallas_call(terms_kernel, grid_spec=pltpu.PrefetchScalarGridSpec(num_s...]
    ppermute x3, starting transfers between devices: 5.47 us -> 0.44 us  [butterfly_sum(): far = lax.ppermute(x, AXES, [(i, i ^ 2 * step) for i in range(peer_count)])]
  transfers between devices with their start and end apart: 14 -> 14, of which waited for: 13 -> 10; matrix products, arithmetic and copies ran while one was open for 12% -> 11% of each run, Pallas kernels for 16% -> 13%
where the time goes in v6:
time: 263 us; the launch traced here: 261 us
  waiting for transfers between devices  112 us (43%)
  starting transfers between devices  52.9 us (20%)
  other arithmetic  35.6 us (14%)
  Pallas kernels  32.7 us (12%)
  between operations  14.2 us (5%)
  matrix products  10.9 us (4%)
  local copies, waits for them, and re-layouts  3.4 us (1%)
    all_gather x1, waiting for transfers between devices, shards(): vec_all = lax.all_gather(vec_t, AXES, axis=0)  83.3 us
    ppermute x3, starting transfers between devices, butterfly_sum(): lax.ppermute(x, AXES, [(i, i ^ 3 * step) for i in range(peer_count)])  24.7 us
    pallas_call x1, Pallas kernels, forward_product(): pl.pallas_call(forward_kernel, grid_spec=pltpu.PrefetchScalarGridSpec(num...  21.8 us
    all_to_all x1, starting transfers between devices, shards(): got = lax.all_to_all(payload, AXES, split_axis=0, concat_axis=0, tiled=True)  11.1 us
    pallas_call x1, Pallas kernels, mirror_terms(): pl.pallas_call(terms_kernel, grid_spec=pltpu.PrefetchScalarGridSpec(num_s...  10.9 us
    all_to_all x1, waiting for transfers between devices, shards(): got = lax.all_to_all(payload, AXES, split_axis=0, concat_axis=0, tiled=True)  10.6 us
    all_to_all x1, starting transfers between devices, shards(): lax.all_to_all(terms, AXES, split_axis=0, concat_axis=0, tiled=True)  10.4 us
    reduce_sum x1, other arithmetic, shards(): col_sums = jnp.sum(tiles, axis=1, dtype=jnp.float32)  10.2 us
  transfers between devices with their start and end apart: 14, of which 10 were waited for; matrix products, arithmetic and copies ran while one was open for 11% of the time, Pallas kernels for 13%

profile of v6, /device:TPU:0, one launch (start us, length us, event | category | flops | bytes accessed | tf_op | source)
XLA Modules:
  0.0 261.5 jit_solution(4446594995765251101)
XLA Ops:
  7.2 0.7 all-gather.3.cloned.1.call-update
  7.9 0.8 eq.49
  8.8 0.8 fusion.20
  9.6 10.2 %convert_reduce_fusion = (f32[512,128]{1,0:T(8,128)S(1)}, f32[512,128]{1,0:T(8,128)S(1)}) fusion(bf16[512,128,128]{2,1,0:T(8,128)(2,1)} %tiles_ref.3), kind=kLoop, calls=%fused_computation | loop fusion | flops 25034752 | bytes 17301504 | tf_op jit(solution)/shard_map/reduce_sum | solution.py:124
  20.6 0.9 copy.32
  21.5 11.1 %all-to-all-start = ((f32[128,1,516]{2,1,0:T(1,128)}), f32[128,1,516]{2,1,0:T(1,128)S(1)}, u32[]{:S(2)}, u32[]{:S(2)}) async-start(f32[128,1,516]{2,1,0:T(1,128)} %copy.32), calls=%async_computation | async-start | bytes 655360 | tf_op jit(solution)/shard_map/all_to_all | solution.py:135
  33.4 10.6 %all-to-all-done = f32[128,1,516]{2,1,0:T(1,128)S(1)} async-done(((f32[128,1,516]{2,1,0:T(1,128)}), f32[128,1,516]{2,1,0:T(1,128)S(1)}, u32[]{:S(2)}, u32[]{:S(2)}) %all-to-all-start) | async-done | bytes 264224 | tf_op jit(solution)/shard_map/all_to_all | solution.py:135
  44.4 1.1 fusion.41
  45.5 0.8 broadcast_in_dim.6
  46.3 4.8 %all-to-all-start.1 = ((f32[128,1,512]{2,1,0:T(1,128)}), f32[128,1,512]{2,1,0:T(1,128)S(1)}, u32[]{:S(2)}, u32[]{:S(2)}) async-start(f32[128,1,512]{2,1,0:T(1,128)} %broadcast_in_dim.6), calls=%async_computation.1 | async-start | bytes 524288 | tf_op jit(solution)/shard_map/all_to_all | solution.py:145
  52.3 10.9 %shard_map.68 = bf16[512,64,128]{2,1,0:T(8,128)(2,1)} custom-call(s32[512]{0:T(512)} %broadcast_clamp_fusion.rows_ref, s32[512]{0:T(512)} %get-tuple-element.12.live_ref, bf16[512,128,128]{2,1,0:T(8,128)(2,1)} %tiles_ref.3, bf16[64,512]{1,0:T(8,128)(2,1)} %fusion.21.own_ref), custom_call_target="tpu_custom_call" | custom-call | tf_op jit(solution)/shard_map/pallas_call | solution.py:47
  63.2 10.4 %all-to-all-start.2 = ((bf16[512,64,128]{2,1,0:T(8,128)(2,1)}), bf16[512,64,128]{2,1,0:T(8,128)(2,1)}, u32[]{:S(2)}, u32[]{:S(2)}) async-start(bf16[512,64,128]{2,1,0:T(8,128)(2,1)} %shard_map.68), calls=%async_computation.2 | async-start | bytes 16777216 | tf_op jit(solution)/shard_map/all_to_all | solution.py:150
  74.5 83.3 %all-gather.3.cloned.1.call-done = bf16[8192,512]{1,0:T(8,128)(2,1)} async-done(((bf16[64,512]{1,0:T(8,128)(2,1)}), bf16[8192,512]{1,0:T(8,128)(2,1)}) %all-gather.3.cloned.1.call-update) | async-done | bytes 8388624 | tf_op jit(solution)/shard_map/all_gather | solution.py:115
  157.7 9.9 %fusion.all_ref = bf16[128,64,512]{2,1,0:T(8,128)(2,1)} fusion(bf16[128,64,512]{2,1,0:T(8,128)(2,1)} %bitcast.50, f32[128,512]{1,0:T(8,128)S(1)} %bitcast.54), kind=kLoop, calls=%fused_computation.3 | loop fusion | flops 12582912 | bytes 17039360 | tf_op jit(solution)/shard_map/convert_element_type | solution.py:152
  167.7 21.8 %shard_map.69 = f32[4,64,128]{2,1,0:T(8,128)} custom-call(s32[512]{0:T(512)} %get-tuple-element.16.places_ref, s32[512]{0:T(512)} %get-tuple-element.17.cols_ref, s32[512]{0:T(512)} %broadcast_clamp_fusion.rows_ref, s32[512]{0:T(512)} %get-tuple-element.12.live_ref, bf16[512,128,128]{2,1,0:T(8,128)(2,1)} %tiles_ref.3, bf16[128,64,512]{2,1,0:T(8,128)(2,1)} %fusion.all_ref), custom_call_target="tpu_custom_call" | custom-call | tf_op jit(solution)/shard_map/pallas_call | solution.py:87
  189.4 7.9 %fusion.1 = f32[4,64,128]{2,0,1:T(4,128)S(1)} fusion(bf16[512,64,128]{2,1,0:T(8,128)(2,1)} %all-to-all-done.2, s32[512]{0:T(512)S(1)} %eq.53), kind=kOutput, calls=%fused_computation.4 | convolution fusion | flops 33556480 | bytes 8521728 | tf_op jit(solution)/shard_map/tr,tka->rka/dot_general | solution.py:159
  198.1 1.8 collective-permute-start.2
  199.8 1.9 collective-permute-done.1
  201.8 11.7 %collective-permute-start.5 = (f32[64,64]{0,1:T(8,128)S(1)}, f32[64,64]{0,1:T(8,128)S(1)}, u32[]{:S(2)}, u32[]{:S(2)}) collective-permute-start(f32[64,64]{0,1:T(8,128)S(1)} %add_add_fusion.2), channel_id=1, source_target_pairs={{0,12},{1,13},{2,14},{3,15},{4,8},{5,9},{6,10},{7,11},{8,4},{9,5},... | collective-permute-start | bytes 49160 | tf_op jit(solution)/shard_map/ppermute | solution.py:17
  213.5 0.7 collective-permute-start.3
  214.1 1.4 collective-permute-done.5
  215.5 1.9 collective-permute-done.4
  217.4 1.5 collective-permute-done.3
  218.9 11.3 %collective-permute-start.8 = (f32[64,64]{0,1:T(8,128)S(1)}, f32[64,64]{0,1:T(8,128)S(1)}, u32[]{:S(2)}, u32[]{:S(2)}) collective-permute-start(f32[64,64]{0,1:T(8,128)S(1)} %add_add_fusion.1), channel_id=1, source_target_pairs={{0,48},{1,49},{2,50},{3,51},{4,52},{5,53},{6,54},{7,55},{8,56},{9,... | collective-permute-start | bytes 49160 | tf_op jit(solution)/shard_map/ppermute | solution.py:17
  230.8 1.2 collective-permute-done.8
  232.1 2.0 collective-permute-done.7
  234.1 1.9 collective-permute-done.6
  236.0 5.4 %collective-permute-done.9 = f32[64,64]{0,1:T(8,128)S(1)} collective-permute-done((f32[64,64]{0,1:T(8,128)S(1)}, f32[64,64]{0,1:T(8,128)S(1)}, u32[]{:S(2)}, u32[]{:S(2)}) %collective-permute-start.9) | collective-permute-done | bytes 16416 | tf_op jit(solution)/shard_map/ppermute | solution.py:21
  241.5 5.8 %cholesky.16 = f32[64,64]{1,0:T(8,128)S(1)} custom-call(f32[64,64]{1,0:T(8,128)S(1)} %fusion.29), custom_call_target="Cholesky" | custom-call | tf_op jit(solution)/shard_map/jit(cholesky)/cholesky | solution.py:165
  248.1 0.7 fusion.27
  248.7 4.9 %custom-call.7 = f32[1,64,64]{1,2,0:T(8,128)S(1)} custom-call(f32[1,64,64]{2,1,0:T(8,128)S(1)} %fusion.27), custom_call_target="InvertDiagBlocksLowerTriangular" | custom-call | tf_op jit(solution)/shard_map/jit(_solve_triangular)/triangular_solve | solution.py:166
  253.6 1.0 fusion.16
  (47 shorter events, 6.3 us)
Async XLA Ops:
  7.2 150.6 %all-gather.3.cloned.1.call-start = ((), (), s32[]{:S(2)}) async-start(), calls=%async_computation.3 | async-start | bytes 8454144 | tf_op jit(solution)/shard_map/all_gather | solution.py:115
  9.5 23.1 %copy-start.4 = (s32[128]{0:T(128)S(1)}, s32[128]{0:T(128)}, u32[]{:S(2)}) copy-start(s32[128]{0:T(128)} %param.8) | copy-start | bytes 1540
  9.5 34.8 %copy-start.2 = (s32[512]{0:T(512)S(1)}, s32[512]{0:T(512)}, u32[]{:S(2)}) copy-start(s32[512]{0:T(512)} %param.6) | copy-start | bytes 6148
  9.6 42.1 %copy-start.1 = (bf16[512,64]{0,1:T(8,128)(2,1)S(1)}, bf16[512,64]{0,1:T(8,128)(2,1)}, u32[]{:S(2)}) copy-start(bf16[512,64]{0,1:T(8,128)(2,1)} %param.9) | copy-start | bytes 196612
  21.5 22.6 %all-to-all-start = ((f32[128,1,516]{2,1,0:T(1,128)}), f32[128,1,516]{2,1,0:T(1,128)S(1)}, u32[]{:S(2)}, u32[]{:S(2)}) async-start(f32[128,1,516]{2,1,0:T(1,128)} %copy.32), calls=%async_computation | async-start | bytes 655360 | tf_op jit(solution)/shard_map/all_to_all | solution.py:135
  46.3 16.9 %all-to-all-start.1 = ((f32[128,1,512]{2,1,0:T(1,128)}), f32[128,1,512]{2,1,0:T(1,128)S(1)}, u32[]{:S(2)}, u32[]{:S(2)}) async-start(f32[128,1,512]{2,1,0:T(1,128)} %broadcast_in_dim.6), calls=%async_computation.1 | async-start | bytes 524288 | tf_op jit(solution)/shard_map/all_to_all | solution.py:145
  63.2 10.4 %copy-start.3 = (s32[512]{0:T(512)S(1)}, s32[512]{0:T(512)}, u32[]{:S(2)}) copy-start(s32[512]{0:T(512)} %param.7) | copy-start | bytes 6148
  63.2 126.2 %all-to-all-start.2 = ((bf16[512,64,128]{2,1,0:T(8,128)(2,1)}), bf16[512,64,128]{2,1,0:T(8,128)(2,1)}, u32[]{:S(2)}, u32[]{:S(2)}) async-start(bf16[512,64,128]{2,1,0:T(8,128)(2,1)} %shard_map.68), calls=%async_computation.2 | async-start | bytes 16777216 | tf_op jit(solution)/shard_map/all_to_all | solution.py:150
  189.4 7.9 %copy-start = (f32[4,64,128]{2,1,0:T(8,128)S(1)}, f32[4,64,128]{2,1,0:T(8,128)}, u32[]{:S(2)}) copy-start(f32[4,64,128]{2,1,0:T(8,128)} %shard_map.69) | copy-start | bytes 393220
  197.6 4.2 %collective-permute-start.1 = (f32[64,64]{0,1:T(8,128)S(1)}, f32[64,64]{0,1:T(8,128)S(1)}, u32[]{:S(2)}, u32[]{:S(2)}) collective-permute-start(f32[64,64]{0,1:T(8,128)S(1)} %fusion.18), channel_id=1, source_target_pairs={{0,2},{1,3},{2,0},{3,1},{4,6},{5,7},{6,4},{7,5},{8,10},{9,11},{10,... | collective-permute-start | bytes 49160 | tf_op jit(solution)/shard_map/ppermute | solution.py:16
  197.7 4.1 %collective-permute-start = (f32[64,64]{0,1:T(8,128)S(1)}, f32[64,64]{0,1:T(8,128)S(1)}, u32[]{:S(2)}, u32[]{:S(2)}) collective-permute-start(f32[64,64]{0,1:T(8,128)S(1)} %fusion.18), channel_id=1, source_target_pairs={{0,1},{1,0},{2,3},{3,2},{4,5},{5,4},{6,7},{7,6},{8,9},{9,8},{10,11... | collective-permute-start | bytes 49160 | tf_op jit(solution)/shard_map/ppermute | solution.py:15
  198.1 3.7 %collective-permute-start.2 = (f32[64,64]{0,1:T(8,128)S(1)}, f32[64,64]{0,1:T(8,128)S(1)}, u32[]{:S(2)}, u32[]{:S(2)}) collective-permute-start(f32[64,64]{0,1:T(8,128)S(1)} %fusion.18), channel_id=1, source_target_pairs={{0,3},{1,2},{2,1},{3,0},{4,7},{5,6},{6,5},{7,4},{8,11},{9,10},{10,... | collective-permute-start | bytes 49160 | tf_op jit(solution)/shard_map/ppermute | solution.py:17
  201.8 13.7 %collective-permute-start.5 = (f32[64,64]{0,1:T(8,128)S(1)}, f32[64,64]{0,1:T(8,128)S(1)}, u32[]{:S(2)}, u32[]{:S(2)}) collective-permute-start(f32[64,64]{0,1:T(8,128)S(1)} %add_add_fusion.2), channel_id=1, source_target_pairs={{0,12},{1,13},{2,14},{3,15},{4,8},{5,9},{6,10},{7,11},{8,4},{9,5},... | collective-permute-start | bytes 49160 | tf_op jit(solution)/shard_map/ppermute | solution.py:17
  213.5 3.9 %collective-permute-start.4 = (f32[64,64]{0,1:T(8,128)S(1)}, f32[64,64]{0,1:T(8,128)S(1)}, u32[]{:S(2)}, u32[]{:S(2)}) collective-permute-start(f32[64,64]{0,1:T(8,128)S(1)} %add_add_fusion.2), channel_id=1, source_target_pairs={{0,8},{1,9},{2,10},{3,11},{4,12},{5,13},{6,14},{7,15},{8,0},{9,1},... | collective-permute-start | bytes 49160 | tf_op jit(solution)/shard_map/ppermute | solution.py:16
  213.5 5.4 %collective-permute-start.3 = (f32[64,64]{0,1:T(8,128)S(1)}, f32[64,64]{0,1:T(8,128)S(1)}, u32[]{:S(2)}, u32[]{:S(2)}) collective-permute-start(f32[64,64]{0,1:T(8,128)S(1)} %add_add_fusion.2), channel_id=1, source_target_pairs={{0,4},{1,5},{2,6},{3,7},{4,0},{5,1},{6,2},{7,3},{8,12},{9,13},{10,... | collective-permute-start | bytes 49160 | tf_op jit(solution)/shard_map/ppermute | solution.py:15
  218.9 13.1 %collective-permute-start.8 = (f32[64,64]{0,1:T(8,128)S(1)}, f32[64,64]{0,1:T(8,128)S(1)}, u32[]{:S(2)}, u32[]{:S(2)}) collective-permute-start(f32[64,64]{0,1:T(8,128)S(1)} %add_add_fusion.1), channel_id=1, source_target_pairs={{0,48},{1,49},{2,50},{3,51},{4,52},{5,53},{6,54},{7,55},{8,56},{9,... | collective-permute-start | bytes 49160 | tf_op jit(solution)/shard_map/ppermute | solution.py:17
  230.2 3.9 %collective-permute-start.7 = (f32[64,64]{0,1:T(8,128)S(1)}, f32[64,64]{0,1:T(8,128)S(1)}, u32[]{:S(2)}, u32[]{:S(2)}) collective-permute-start(f32[64,64]{0,1:T(8,128)S(1)} %add_add_fusion.1), channel_id=1, source_target_pairs={{0,32},{1,33},{2,34},{3,35},{4,36},{5,37},{6,38},{7,39},{8,40},{9,... | collective-permute-start | bytes 49160 | tf_op jit(solution)/shard_map/ppermute | solution.py:16
  230.5 5.4 %collective-permute-start.6 = (f32[64,64]{0,1:T(8,128)S(1)}, f32[64,64]{0,1:T(8,128)S(1)}, u32[]{:S(2)}, u32[]{:S(2)}) collective-permute-start(f32[64,64]{0,1:T(8,128)S(1)} %add_add_fusion.1), channel_id=1, source_target_pairs={{0,16},{1,17},{2,18},{3,19},{4,20},{5,21},{6,22},{7,23},{8,24},{9,... | collective-permute-start | bytes 49160 | tf_op jit(solution)/shard_map/ppermute | solution.py:15
  235.9 5.5 %collective-permute-start.9 = (f32[64,64]{0,1:T(8,128)S(1)}, f32[64,64]{0,1:T(8,128)S(1)}, u32[]{:S(2)}, u32[]{:S(2)}) collective-permute-start(f32[64,64]{0,1:T(8,128)S(1)} %add_add_fusion), channel_id=1, source_target_pairs={{0,64},{1,65},{2,66},{3,67},{4,68},{5,69},{6,70},{7,71},{8,72},{9,... | collective-permute-start | bytes 49160 | tf_op jit(solution)/shard_map/ppermute | solution.py:21
Sparse Core Ops, SparseCore 0:
  11.0 146.7 all-gather.2

commit v7 on v4

--- a/solution.py
+++ b/solution.py
@@ -11,15 +11,8 @@
 def butterfly_sum(x, peer_count):
     step = 1
     while step < peer_count:
-        if step * 4 <= peer_count:
-            near = lax.ppermute(x, AXES, [(i, i ^ step) for i in range(peer_count)])
-            far = lax.ppermute(x, AXES, [(i, i ^ (2 * step)) for i in range(peer_count)])
-            far_near = lax.ppermute(x, AXES, [(i, i ^ (3 * step)) for i in range(peer_count)])
-            x = (x + near) + (far + far_near)
-            step *= 4
-        else:
-            x = x + lax.ppermute(x, AXES, [(i, i ^ step) for i in range(peer_count)])
-            step *= 2
+        x = x + lax.ppermute(x, AXES, [(i, i ^ step) for i in range(peer_count)])
+        step *= 2
     return x
 
 
@@ -129,12 +122,8 @@
         col_sums.reshape(peer_count, slot_count, tile_size),
         precision=highest,
     ).reshape(peer_count, block_count * tile_size)
-    payload = jnp.concatenate(
-        [col_part, tile_col.reshape(peer_count, slot_count).astype(jnp.float32)], axis=1
-    )
-    got = lax.all_to_all(payload, AXES, split_axis=0, concat_axis=0, tiled=True)
-    degree_blocks = own_part + jnp.sum(got[:, : block_count * tile_size], axis=0).reshape(block_count, tile_size)
-    got_cols = got[:, block_count * tile_size :].astype(jnp.int32).reshape(peer_count * slot_count)
+    got = lax.all_to_all(col_part, AXES, split_axis=0, concat_axis=0, tiled=True)
+    degree_blocks = own_part + jnp.sum(got, axis=0).reshape(block_count, tile_size)
 
     degree = 1.0 + degree_blocks.reshape(rows_dev)
     inv_root = lax.rsqrt(degree)
@@ -142,9 +131,16 @@
 
     scaled_t = scaled.T
     live_i = live.astype(jnp.int32)
-    inv_all = lax.all_to_all(
-        jnp.broadcast_to(inv_root[None, :], (peer_count, rows_dev)), AXES, split_axis=0, concat_axis=0, tiled=True
+    inv_payload = jnp.concatenate(
+        [
+            jnp.broadcast_to(inv_root[None, :], (peer_count, rows_dev)),
+            tile_col.reshape(peer_count, slot_count).astype(jnp.float32),
+        ],
+        axis=1,
     )
+    inv_got = lax.all_to_all(inv_payload, AXES, split_axis=0, concat_axis=0, tiled=True)
+    inv_all = inv_got[:, :rows_dev]
+    got_cols = inv_got[:, rows_dev:].astype(jnp.int32).reshape(peer_count * slot_count)
     terms = mirror_terms(tiles, tile_row, live_i, scaled_t)
     terms, inv_all = lax.optimization_barrier((terms, inv_all))
     got_terms = lax.all_to_all(terms, AXES, split_axis=0, concat_axis=0, tiled=True)

time: 242 us -> 244 us (level)
  waiting for transfers between devices: 96.2 us -> 102 us
  starting transfers between devices: 41.6 us -> 38.5 us
    all_gather x1, waiting for transfers between devices: 13.3 us -> 66.7 us  [shards(): vec_all = lax.all_gather(vec_t, AXES, axis=0)]
    all_to_all x1, waiting for transfers between devices: 52.5 us -> 1.35 us  [shards(): lax.all_to_all(terms, AXES, split_axis=0, concat_axis=0, tiled=True)]
    ppermute x1 -> x7, waiting for transfers between devices: 5.41 us -> 23 us  [butterfly_sum(): x = x + lax.ppermute(x, AXES, [(i, i ^ step) for i in range(peer_count)])]
    ppermute x9 -> x0, starting transfers between devices: 15.2 us -> none  [the longest x3 7.94 us: butterfly_sum(): lax.ppermute(x, AXES, [(i, i ^ 3 * step) for i in range(peer_count)])]
    ppermute x9 -> x0, waiting for transfers between devices: 13.6 us -> none  [the longest x3 5.17 us: butterfly_sum(): near = lax.ppermute(x, AXES, [(i, i ^ step) for i in range(peer_count)])]
    ppermute x1 -> x7, starting transfers between devices: 0.09 us -> 12 us  [butterfly_sum(): x = x + lax.ppermute(x, AXES, [(i, i ^ step) for i in range(peer_count)])]
  transfers between devices with their start and end apart: 14 -> 11, of which waited for: 13 -> 10; matrix products, arithmetic and copies ran while one was open for 12% -> 11% of each run, Pallas kernels for 16% -> 16%
where the time goes in v7:
time: 244 us; the launch traced here: 243 us
  waiting for transfers between devices  102 us (42%)
  Pallas kernels  39.1 us (16%)
  starting transfers between devices  38.5 us (16%)
  other arithmetic  35.1 us (14%)
  between operations  14.2 us (6%)
  matrix products  11.5 us (5%)
  local copies, waits for them, and re-layouts  2.58 us (1%)
    all_gather x1, waiting for transfers between devices, shards(): vec_all = lax.all_gather(vec_t, AXES, axis=0)  66.7 us
    ppermute x7, waiting for transfers between devices, butterfly_sum(): x = x + lax.ppermute(x, AXES, [(i, i ^ step) for i in range(peer_count)])  23 us
    pallas_call x1, Pallas kernels, forward_product(): pl.pallas_call(forward_kernel, grid_spec=pltpu.PrefetchScalarGridSpec(num...  21.8 us
    pallas_call x1, Pallas kernels, mirror_terms(): pl.pallas_call(terms_kernel, grid_spec=pltpu.PrefetchScalarGridSpec(num_s...  17.3 us
    ppermute x7, starting transfers between devices, butterfly_sum(): x = x + lax.ppermute(x, AXES, [(i, i ^ step) for i in range(peer_count)])  12 us
    all_to_all x1, starting transfers between devices, shards(): lax.all_to_all(col_part, AXES, split_axis=0, concat_axis=0, tiled=True)  11.1 us
    all_to_all x1, starting transfers between devices, shards(): lax.all_to_all(terms, AXES, split_axis=0, concat_axis=0, tiled=True)  10.5 us
    reduce_sum x1, other arithmetic, shards(): col_sums = jnp.sum(tiles, axis=1, dtype=jnp.float32)  10.2 us
  transfers between devices with their start and end apart: 11, of which 10 were waited for; matrix products, arithmetic and copies ran while one was open for 11% of the time, Pallas kernels for 16%

profile of v7, /device:TPU:0, one launch (start us, length us, event | category | flops | bytes accessed | tf_op | source)
XLA Modules:
  0.0 242.7 jit_solution(15337869833185238868)
XLA Ops:
  7.2 0.7 all-gather.3.cloned.1.call-update
  7.9 0.8 eq.49
  8.7 0.7 fusion.20
  9.5 10.2 %convert_reduce_fusion = (f32[512,128]{1,0:T(8,128)S(1)}, f32[512,128]{1,0:T(8,128)S(1)}) fusion(bf16[512,128,128]{2,1,0:T(8,128)(2,1)} %tiles_ref.3), kind=kLoop, calls=%fused_computation | loop fusion | flops 25034752 | bytes 17301504 | tf_op jit(solution)/shard_map/reduce_sum | solution.py:117
  19.7 1.3 fusion.8
  21.0 11.1 %all-to-all-start = ((f32[128,1,512]{2,1,0:T(1,128)}), f32[128,1,512]{2,1,0:T(1,128)S(1)}, u32[]{:S(2)}, u32[]{:S(2)}) async-start(f32[128,1,512]{2,1,0:T(1,128)} %bitcast.1), calls=%async_computation | async-start | bytes 524288 | tf_op jit(solution)/shard_map/all_to_all | solution.py:125
  33.0 10.0 %all-to-all-done = f32[128,1,512]{2,1,0:T(1,128)S(1)} async-done(((f32[128,1,512]{2,1,0:T(1,128)}), f32[128,1,512]{2,1,0:T(1,128)S(1)}, u32[]{:S(2)}, u32[]{:S(2)}) %all-to-all-start) | async-done | bytes 262176 | tf_op jit(solution)/shard_map/all_to_all | solution.py:125
  43.2 1.1 fusion.41
  44.4 0.9 copy.27
  45.3 4.8 %all-to-all-start.1 = ((f32[128,1,516]{2,1,0:T(1,128)}), f32[128,1,516]{2,1,0:T(1,128)S(1)}, u32[]{:S(2)}, u32[]{:S(2)}) async-start(f32[128,1,516]{2,1,0:T(1,128)} %copy.27), calls=%async_computation.1 | async-start | bytes 655360 | tf_op jit(solution)/shard_map/all_to_all | solution.py:141
  50.1 0.6 fusion.21.own_ref
  50.8 17.3 %shard_map.68 = bf16[512,64,128]{2,1,0:T(8,128)(2,1)} custom-call(s32[512]{0:T(512)} %rows_ref.3, s32[512]{0:T(512)} %get-tuple-element.12.live_ref, bf16[512,128,128]{2,1,0:T(8,128)(2,1)} %tiles_ref.3, bf16[64,512]{1,0:T(8,128)(2,1)} %fusion.21.own_ref), custom_call_target="tpu_custom_call" | custom-call | tf_op jit(solution)/shard_map/pallas_call | solution.py:40
  68.3 10.5 %all-to-all-start.2 = ((bf16[512,64,128]{2,1,0:T(8,128)(2,1)}), bf16[512,64,128]{2,1,0:T(8,128)(2,1)}, u32[]{:S(2)}, u32[]{:S(2)}) async-start(bf16[512,64,128]{2,1,0:T(8,128)(2,1)} %shard_map.68), calls=%async_computation.2 | async-start | bytes 16777216 | tf_op jit(solution)/shard_map/all_to_all | solution.py:146
  79.7 66.7 %all-gather.3.cloned.1.call-done = bf16[8192,512]{1,0:T(8,128)(2,1)} async-done(((bf16[64,512]{1,0:T(8,128)(2,1)}), bf16[8192,512]{1,0:T(8,128)(2,1)}) %all-gather.3.cloned.1.call-update) | async-done | bytes 8388624 | tf_op jit(solution)/shard_map/all_gather | solution.py:108
  146.4 9.9 %fusion.all_ref = bf16[128,64,512]{2,1,0:T(8,128)(2,1)} fusion(bf16[128,64,512]{2,1,0:T(8,128)(2,1)} %bitcast.47, f32[128,512]{1,0:T(8,128)S(1)} %copy.29), kind=kLoop, calls=%fused_computation.3 | loop fusion | flops 12582912 | bytes 17039360 | tf_op jit(solution)/shard_map/convert_element_type | solution.py:148
  156.3 21.8 %shard_map.69 = f32[4,64,128]{2,1,0:T(8,128)} custom-call(s32[512]{0:T(512)} %add_select_fusion.1.places_ref, s32[512]{0:T(512)} %cols_ref.1, s32[512]{0:T(512)} %rows_ref.3, s32[512]{0:T(512)} %get-tuple-element.12.live_ref, bf16[512,128,128]{2,1,0:T(8,128)(2,1)} %tiles_ref.3, bf16[128,64,512]{2,1,0:T(8,128)(2,1)} %fusion.all_ref), custom_call_target="tpu_custom_call" | custom-call | tf_op jit(solution)/shard_map/pallas_call | solution.py:80
  178.1 1.4 all-to-all-done.2
  179.5 7.8 %fusion.1 = f32[4,64,128]{2,0,1:T(4,128)S(1)} fusion(bf16[512,64,128]{2,1,0:T(8,128)(2,1)} %all-to-all-done.2, s32[512]{0:T(512)S(1)} %eq.53), kind=kOutput, calls=%fused_computation.4 | convolution fusion | flops 33556480 | bytes 8521728 | tf_op jit(solution)/shard_map/tr,tka->rka/dot_general | solution.py:153
  187.7 1.2 collective-permute-done
  188.9 7.4 %collective-permute-start.1 = (f32[64,64]{0,1:T(8,128)S(1)}, f32[64,64]{0,1:T(8,128)S(1)}, u32[]{:S(2)}, u32[]{:S(2)}) collective-permute-start(f32[64,64]{0,1:T(8,128)S(1)} %add.82), channel_id=1, source_target_pairs={{0,2},{1,3},{2,0},{3,1},{4,6},{5,7},{6,4},{7,5},{8,10},{9,11},{10,... | collective-permute-start | bytes 49160 | tf_op jit(solution)/shard_map/ppermute | solution.py:14
  196.3 1.9 collective-permute-done.1
  198.2 5.4 %collective-permute-done.2 = f32[64,64]{0,1:T(8,128)S(1)} collective-permute-done((f32[64,64]{0,1:T(8,128)S(1)}, f32[64,64]{0,1:T(8,128)S(1)}, u32[]{:S(2)}, u32[]{:S(2)}) %collective-permute-start.2) | collective-permute-done | bytes 16416 | tf_op jit(solution)/shard_map/ppermute | solution.py:14
  203.6 4.2 %collective-permute-done.3 = f32[64,64]{0,1:T(8,128)S(1)} collective-permute-done((f32[64,64]{0,1:T(8,128)S(1)}, f32[64,64]{0,1:T(8,128)S(1)}, u32[]{:S(2)}, u32[]{:S(2)}) %collective-permute-start.3) | collective-permute-done | bytes 16416 | tf_op jit(solution)/shard_map/ppermute | solution.py:14
  207.9 2.4 collective-permute-start.4
  210.2 3.0 %collective-permute-done.4 = f32[64,64]{0,1:T(8,128)S(1)} collective-permute-done((f32[64,64]{0,1:T(8,128)S(1)}, f32[64,64]{0,1:T(8,128)S(1)}, u32[]{:S(2)}, u32[]{:S(2)}) %collective-permute-start.4) | collective-permute-done | bytes 16416 | tf_op jit(solution)/shard_map/ppermute | solution.py:14
  213.3 3.9 %collective-permute-done.5 = f32[64,64]{0,1:T(8,128)S(1)} collective-permute-done((f32[64,64]{0,1:T(8,128)S(1)}, f32[64,64]{0,1:T(8,128)S(1)}, u32[]{:S(2)}, u32[]{:S(2)}) %collective-permute-start.5) | collective-permute-done | bytes 16416 | tf_op jit(solution)/shard_map/ppermute | solution.py:14
  217.2 2.1 collective-permute-start.6
  219.3 3.3 %collective-permute-done.6 = f32[64,64]{0,1:T(8,128)S(1)} collective-permute-done((f32[64,64]{0,1:T(8,128)S(1)}, f32[64,64]{0,1:T(8,128)S(1)}, u32[]{:S(2)}, u32[]{:S(2)}) %collective-permute-start.6) | collective-permute-done | bytes 16416 | tf_op jit(solution)/shard_map/ppermute | solution.py:14
  222.7 5.8 %cholesky.16 = f32[64,64]{1,0:T(8,128)S(1)} custom-call(f32[64,64]{1,0:T(8,128)S(1)} %fusion.29), custom_call_target="Cholesky" | custom-call | tf_op jit(solution)/shard_map/jit(cholesky)/cholesky | solution.py:159
  229.3 0.7 fusion.27
  229.9 4.9 %custom-call.7 = f32[1,64,64]{1,2,0:T(8,128)S(1)} custom-call(f32[1,64,64]{2,1,0:T(8,128)S(1)} %fusion.27), custom_call_target="InvertDiagBlocksLowerTriangular" | custom-call | tf_op jit(solution)/shard_map/jit(_solve_triangular)/triangular_solve | solution.py:160
  234.8 1.0 fusion.16
  (41 shorter events, 3.5 us)
Async XLA Ops:
  7.2 139.2 %all-gather.3.cloned.1.call-start = ((), (), s32[]{:S(2)}) async-start(), calls=%async_computation.3 | async-start | bytes 8454144 | tf_op jit(solution)/shard_map/all_gather | solution.py:108
  9.4 22.8 %copy-start.3 = (s32[128]{0:T(128)S(1)}, s32[128]{0:T(128)}, u32[]{:S(2)}) copy-start(s32[128]{0:T(128)} %param.8) | copy-start | bytes 1540
  9.4 33.7 %copy-start.2 = (s32[512]{0:T(512)S(1)}, s32[512]{0:T(512)}, u32[]{:S(2)}) copy-start(s32[512]{0:T(512)} %rows_ref.3) | copy-start | bytes 6148
  9.5 40.7 %copy-start.1 = (bf16[512,64]{0,1:T(8,128)(2,1)S(1)}, bf16[512,64]{0,1:T(8,128)(2,1)}, u32[]{:S(2)}) copy-start(bf16[512,64]{0,1:T(8,128)(2,1)} %param.9) | copy-start | bytes 196612
  21.0 22.0 %all-to-all-start = ((f32[128,1,512]{2,1,0:T(1,128)}), f32[128,1,512]{2,1,0:T(1,128)S(1)}, u32[]{:S(2)}, u32[]{:S(2)}) async-start(f32[128,1,512]{2,1,0:T(1,128)} %bitcast.1), calls=%async_computation | async-start | bytes 524288 | tf_op jit(solution)/shard_map/all_to_all | solution.py:125
  45.3 22.8 %all-to-all-start.1 = ((f32[128,1,516]{2,1,0:T(1,128)}), f32[128,1,516]{2,1,0:T(1,128)S(1)}, u32[]{:S(2)}, u32[]{:S(2)}) async-start(f32[128,1,516]{2,1,0:T(1,128)} %copy.27), calls=%async_computation.1 | async-start | bytes 655360 | tf_op jit(solution)/shard_map/all_to_all | solution.py:141
  68.3 111.2 %all-to-all-start.2 = ((bf16[512,64,128]{2,1,0:T(8,128)(2,1)}), bf16[512,64,128]{2,1,0:T(8,128)(2,1)}, u32[]{:S(2)}, u32[]{:S(2)}) async-start(bf16[512,64,128]{2,1,0:T(8,128)(2,1)} %shard_map.68), calls=%async_computation.2 | async-start | bytes 16777216 | tf_op jit(solution)/shard_map/all_to_all | solution.py:146
  178.1 9.2 %copy-start = (f32[4,64,128]{2,1,0:T(8,128)S(1)}, f32[4,64,128]{2,1,0:T(8,128)}, u32[]{:S(2)}) copy-start(f32[4,64,128]{2,1,0:T(8,128)} %shard_map.69) | copy-start | bytes 393220
  187.6 1.3 collective-permute-start
  188.9 9.3 %collective-permute-start.1 = (f32[64,64]{0,1:T(8,128)S(1)}, f32[64,64]{0,1:T(8,128)S(1)}, u32[]{:S(2)}, u32[]{:S(2)}) collective-permute-start(f32[64,64]{0,1:T(8,128)S(1)} %add.82), channel_id=1, source_target_pairs={{0,2},{1,3},{2,0},{3,1},{4,6},{5,7},{6,4},{7,5},{8,10},{9,11},{10,... | collective-permute-start | bytes 49160 | tf_op jit(solution)/shard_map/ppermute | solution.py:14
  198.2 5.4 %collective-permute-start.2 = (f32[64,64]{0,1:T(8,128)S(1)}, f32[64,64]{0,1:T(8,128)S(1)}, u32[]{:S(2)}, u32[]{:S(2)}) collective-permute-start(f32[64,64]{0,1:T(8,128)S(1)} %add.83), channel_id=1, source_target_pairs={{0,4},{1,5},{2,6},{3,7},{4,0},{5,1},{6,2},{7,3},{8,12},{9,13},{10,... | collective-permute-start | bytes 49160 | tf_op jit(solution)/shard_map/ppermute | solution.py:14
  203.6 4.2 %collective-permute-start.3 = (f32[64,64]{0,1:T(8,128)S(1)}, f32[64,64]{0,1:T(8,128)S(1)}, u32[]{:S(2)}, u32[]{:S(2)}) collective-permute-start(f32[64,64]{0,1:T(8,128)S(1)} %add.84), channel_id=1, source_target_pairs={{0,8},{1,9},{2,10},{3,11},{4,12},{5,13},{6,14},{7,15},{8,0},{9,1},... | collective-permute-start | bytes 49160 | tf_op jit(solution)/shard_map/ppermute | solution.py:14
  207.9 5.4 %collective-permute-start.4 = (f32[64,64]{0,1:T(8,128)S(1)}, f32[64,64]{0,1:T(8,128)S(1)}, u32[]{:S(2)}, u32[]{:S(2)}) collective-permute-start(f32[64,64]{0,1:T(8,128)S(1)} %add.85), channel_id=1, source_target_pairs={{0,16},{1,17},{2,18},{3,19},{4,20},{5,21},{6,22},{7,23},{8,24},{9,... | collective-permute-start | bytes 49160 | tf_op jit(solution)/shard_map/ppermute | solution.py:14
  213.3 3.9 %collective-permute-start.5 = (f32[64,64]{0,1:T(8,128)S(1)}, f32[64,64]{0,1:T(8,128)S(1)}, u32[]{:S(2)}, u32[]{:S(2)}) collective-permute-start(f32[64,64]{0,1:T(8,128)S(1)} %add.86), channel_id=1, source_target_pairs={{0,32},{1,33},{2,34},{3,35},{4,36},{5,37},{6,38},{7,39},{8,40},{9,... | collective-permute-start | bytes 49160 | tf_op jit(solution)/shard_map/ppermute | solution.py:14
  217.2 5.4 %collective-permute-start.6 = (f32[64,64]{0,1:T(8,128)S(1)}, f32[64,64]{0,1:T(8,128)S(1)}, u32[]{:S(2)}, u32[]{:S(2)}) collective-permute-start(f32[64,64]{0,1:T(8,128)S(1)} %add.87), channel_id=1, source_target_pairs={{0,64},{1,65},{2,66},{3,67},{4,68},{5,69},{6,70},{7,71},{8,72},{9,... | collective-permute-start | bytes 49160 | tf_op jit(solution)/shard_map/ppermute | solution.py:14
Sparse Core Ops, SparseCore 0:
  11.0 135.3 all-gather.2

commit v8 on v4

--- a/solution.py
+++ b/solution.py
@@ -59,7 +59,10 @@
     )(rows, live, tiles, own_t)
 
 
-def forward_kernel(places_ref, cols_ref, rows_ref, live_ref, tiles_ref, all_ref, out_ref):
+FORWARD_GROUP = 128
+
+
+def forward_kernel(places_ref, cols_ref, rows_ref, live_ref, tiles_ref, vec_ref, inv_ref, out_ref):
     step = pl.program_id(0)
     size = tiles_ref.shape[1]
 
@@ -67,36 +70,36 @@
     def _():
         out_ref[...] = jnp.zeros_like(out_ref)
 
-    def body(j, carry):
-        t = step * GROUP + j
+    for j in range(FORWARD_GROUP):
+        t = step * FORWARD_GROUP + j
+        p = places_ref[t]
         start = pl.multiple_of(cols_ref[t] * size, size)
-        block = all_ref[places_ref[t], :, pl.ds(start, size)]
+        scale = inv_ref[p, :, pl.ds(start, size)]
+        block = (vec_ref[p, :, pl.ds(start, size)].astype(jnp.float32) * scale).astype(tiles_ref.dtype)
         prod = lax.dot_general(
             block, tiles_ref[j], (((1,), (1,)), ((), ())), preferred_element_type=jnp.float32
         )
         r = rows_ref[t]
         out_ref[r] += jnp.where(live_ref[t] > 0, prod, jnp.zeros_like(prod))
-        return carry
-
-    lax.fori_loop(0, GROUP, body, 0, unroll=True)
 
 
-def forward_product(tiles, places, cols, rows, live, scaled_all_t, block_count):
+def forward_product(tiles, places, cols, rows, live, vec_all, inv_all, block_count):
     slots, size, _ = tiles.shape
-    width = scaled_all_t.shape[1]
+    width = vec_all.shape[1]
     return pl.pallas_call(
         forward_kernel,
         grid_spec=pltpu.PrefetchScalarGridSpec(
             num_scalar_prefetch=4,
-            grid=(slots // GROUP,),
+            grid=(slots // FORWARD_GROUP,),
             in_specs=[
-                pl.BlockSpec((GROUP, size, size), lambda i, p, c, r, l: (i, 0, 0)),
+                pl.BlockSpec((FORWARD_GROUP, size, size), lambda i, p, c, r, l: (i, 0, 0)),
+                pl.BlockSpec(memory_space=pltpu.VMEM),
                 pl.BlockSpec(memory_space=pltpu.VMEM),
             ],
             out_specs=pl.BlockSpec((block_count, width, size), lambda i, p, c, r, l: (0, 0, 0)),
         ),
         out_shape=jax.ShapeDtypeStruct((block_count, width, size), jnp.float32),
-    )(places, cols, rows, live, tiles, scaled_all_t)
+    )(places, cols, rows, live, tiles, vec_all, inv_all)
 
 
 def shards(tiles, tile_row, tile_col, counts, vectors):
@@ -149,9 +152,10 @@
     terms, inv_all = lax.optimization_barrier((terms, inv_all))
     got_terms = lax.all_to_all(terms, AXES, split_axis=0, concat_axis=0, tiled=True)
 
-    scaled_all_t = (inv_all[:, None, :] * vec_all.astype(jnp.float32)).astype(jnp.bfloat16)
     place = jnp.arange(slot_total, dtype=jnp.int32) // slot_count
-    forward = forward_product(tiles, place, tile_col, tile_row, live_i, scaled_all_t, block_count)
+    forward = forward_product(
+        tiles, place, tile_col, tile_row, live_i, vec_all, inv_all.reshape(peer_count, 1, rows_dev), block_count
+    )
     forward, got_terms = lax.optimization_barrier((forward, got_terms))
     got_hot = (got_cols[:, None] == block_ids).astype(jnp.bfloat16)
     mirror = jnp.einsum("tr,tka->rka", got_hot, got_terms, preferred_element_type=jnp.float32)

time: 242 us -> 241 us (level)
  waiting for transfers between devices: 96.2 us -> 108 us
  other arithmetic: 34.9 us -> 25 us
  Pallas kernels: 39.4 us -> 35.8 us
    all_to_all x1, waiting for transfers between devices: 52.5 us -> 66 us  [shards(): lax.all_to_all(terms, AXES, split_axis=0, concat_axis=0, tiled=True)]
    convert_element_type x1 -> x0, other arithmetic: 9.93 us -> none  [shards(): (inv_all[:, None, :] * vec_all.astype(jnp.float32)).astype(jnp.bfloat16)]
    pallas_call x1, Pallas kernels: 21.8 us -> 18.2 us  [forward_product(): pl.pallas_call(forward_kernel, grid_spec=pltpu.PrefetchScalarGridSpec(num...]
  transfers between devices with their start and end apart: 14 -> 14, of which waited for: 13 -> 12; matrix products, arithmetic and copies ran while one was open for 12% -> 8% of each run, Pallas kernels for 16% -> 15%
where the time goes in v8:
time: 241 us
  waiting for transfers between devices  108 us (45%)
  starting transfers between devices  42.3 us (18%)
  Pallas kernels  35.8 us (15%)
  other arithmetic  25 us (10%)
  between operations  14.2 us (6%)
  matrix products  10.8 us (4%)
  local copies, waits for them, and re-layouts  4.31 us (2%)
    all_to_all x1, waiting for transfers between devices, shards(): lax.all_to_all(terms, AXES, split_axis=0, concat_axis=0, tiled=True)  66 us
    pallas_call x1, Pallas kernels, forward_product(): pl.pallas_call(forward_kernel, grid_spec=pltpu.PrefetchScalarGridSpec(num...  18.2 us
    pallas_call x1, Pallas kernels, mirror_terms(): pl.pallas_call(terms_kernel, grid_spec=pltpu.PrefetchScalarGridSpec(num_s...  17.6 us
    all_gather x1, waiting for transfers between devices, shards(): vec_all = lax.all_gather(vec_t, AXES, axis=0)  12.6 us
    all_to_all x1, starting transfers between devices, shards(): got = lax.all_to_all(payload, AXES, split_axis=0, concat_axis=0, tiled=True)  11.1 us
    all_to_all x1, waiting for transfers between devices, shards(): got = lax.all_to_all(payload, AXES, split_axis=0, concat_axis=0, tiled=True)  10.6 us
    all_to_all x1, starting transfers between devices, shards(): lax.all_to_all(terms, AXES, split_axis=0, concat_axis=0, tiled=True)  10.3 us
    reduce_sum x1, other arithmetic, shards(): col_sums = jnp.sum(tiles, axis=1, dtype=jnp.float32)  10.2 us
  transfers between devices with their start and end apart: 14, of which 12 were waited for; matrix products, arithmetic and copies ran while one was open for 8% of the time, Pallas kernels for 15%

profile of v8, /device:TPU:0, one launch (start us, length us, event | category | flops | bytes accessed | tf_op | source)
XLA Modules:
  0.0 240.7 jit_solution(2289228066026670858)
XLA Ops:
  7.9 0.8 eq.49
  8.8 0.8 fusion.19
  9.6 10.2 %convert_reduce_fusion = (f32[512,128]{1,0:T(8,128)S(1)}, f32[512,128]{1,0:T(8,128)S(1)}) fusion(bf16[512,128,128]{2,1,0:T(8,128)(2,1)} %tiles_ref.3), kind=kLoop, calls=%fused_computation | loop fusion | flops 25034752 | bytes 17301504 | tf_op jit(solution)/shard_map/reduce_sum | solution.py:127
  20.6 0.9 copy.32
  21.5 11.1 %all-to-all-start = ((f32[128,1,516]{2,1,0:T(1,128)}), f32[128,1,516]{2,1,0:T(1,128)S(1)}, u32[]{:S(2)}, u32[]{:S(2)}) async-start(f32[128,1,516]{2,1,0:T(1,128)} %copy.32), calls=%async_computation | async-start | bytes 655360 | tf_op jit(solution)/shard_map/all_to_all | solution.py:138
  33.4 10.6 %all-to-all-done = f32[128,1,516]{2,1,0:T(1,128)S(1)} async-done(((f32[128,1,516]{2,1,0:T(1,128)}), f32[128,1,516]{2,1,0:T(1,128)S(1)}, u32[]{:S(2)}, u32[]{:S(2)}) %all-to-all-start) | async-done | bytes 264224 | tf_op jit(solution)/shard_map/all_to_all | solution.py:138
  44.4 1.1 fusion.40
  45.5 0.8 broadcast_in_dim.6
  46.3 4.8 %all-to-all-start.1 = ((f32[128,1,512]{2,1,0:T(1,128)}), f32[128,1,512]{2,1,0:T(1,128)S(1)}, u32[]{:S(2)}, u32[]{:S(2)}) async-start(f32[128,1,512]{2,1,0:T(1,128)} %broadcast_in_dim.6), calls=%async_computation.1 | async-start | bytes 524288 | tf_op jit(solution)/shard_map/all_to_all | solution.py:148
  51.7 17.6 %shard_map.68 = bf16[512,64,128]{2,1,0:T(8,128)(2,1)} custom-call(s32[512]{0:T(512)} %rows_ref.3, s32[512]{0:T(512)} %get-tuple-element.12.live_ref, bf16[512,128,128]{2,1,0:T(8,128)(2,1)} %tiles_ref.3, bf16[64,512]{1,0:T(8,128)(2,1)} %fusion.20.own_ref), custom_call_target="tpu_custom_call" | custom-call | tf_op jit(solution)/shard_map/pallas_call | solution.py:47
  69.4 10.3 %all-to-all-start.2 = ((bf16[512,64,128]{2,1,0:T(8,128)(2,1)}), bf16[512,64,128]{2,1,0:T(8,128)(2,1)}, u32[]{:S(2)}, u32[]{:S(2)}) async-start(bf16[512,64,128]{2,1,0:T(8,128)(2,1)} %shard_map.68), calls=%async_computation.2 | async-start | bytes 16777216 | tf_op jit(solution)/shard_map/all_to_all | solution.py:153
  80.5 0.9 reshape.92.inv_ref
  81.4 12.6 %all-gather.3.cloned.1.call-done = bf16[8192,512]{1,0:T(8,128)(2,1)} async-done(((bf16[64,512]{1,0:T(8,128)(2,1)}), bf16[8192,512]{1,0:T(8,128)(2,1)}) %all-gather.3.cloned.1.call-update) | async-done | bytes 8388624 | tf_op jit(solution)/shard_map/all_gather | solution.py:118
  93.9 18.2 %shard_map.69 = f32[4,64,128]{2,1,0:T(8,128)} custom-call(s32[512]{0:T(512)} %add_select_fusion.1.places_ref, s32[512]{0:T(512)} %cols_ref.1, s32[512]{0:T(512)} %rows_ref.3, s32[512]{0:T(512)} %get-tuple-element.12.live_ref, bf16[512,128,128]{2,1,0:T(8,128)(2,1)} %tiles_ref.3, bf16[128,64,512]{2,1,0:T(8,128)(2,1)} %bitcast.49, f32[128,1,512]{2,1,0:T(1,128)} %reshape.92.inv_ref), custom_call_target="tpu_custom_call" | custom-call | tf_op jit(solution)/shard_map/pallas_call | solution.py:89
  112.1 66.0 %all-to-all-done.2 = bf16[512,64,128]{2,1,0:T(8,128)(2,1)} async-done(((bf16[512,64,128]{2,1,0:T(8,128)(2,1)}), bf16[512,64,128]{2,1,0:T(8,128)(2,1)}, u32[]{:S(2)}, u32[]{:S(2)}) %all-to-all-start.2) | async-done | bytes 8388640 | tf_op jit(solution)/shard_map/all_to_all | solution.py:153
  178.1 7.8 %fusion = f32[4,64,128]{2,0,1:T(4,128)S(1)} fusion(bf16[512,64,128]{2,1,0:T(8,128)(2,1)} %all-to-all-done.2, s32[512]{0:T(512)S(1)} %eq.53), kind=kOutput, calls=%fused_computation.2 | convolution fusion | flops 33556480 | bytes 8521728 | tf_op jit(solution)/shard_map/tr,tka->rka/dot_general | solution.py:161
  186.2 3.1 %collective-permute-start.1 = (f32[64,64]{0,1:T(8,128)S(1)}, f32[64,64]{0,1:T(8,128)S(1)}, u32[]{:S(2)}, u32[]{:S(2)}) collective-permute-start(f32[64,64]{0,1:T(8,128)S(1)} %fusion.17), channel_id=1, source_target_pairs={{0,2},{1,3},{2,0},{3,1},{4,6},{5,7},{6,4},{7,5},{8,10},{9,11},{10,... | collective-permute-start | bytes 49160 | tf_op jit(solution)/shard_map/ppermute | solution.py:16
  189.3 0.8 collective-permute-start
  190.1 1.1 collective-permute-done.1
  191.2 2.4 collective-permute-done.2
  193.6 6.2 %collective-permute-start.5 = (f32[64,64]{0,1:T(8,128)S(1)}, f32[64,64]{0,1:T(8,128)S(1)}, u32[]{:S(2)}, u32[]{:S(2)}) collective-permute-start(f32[64,64]{0,1:T(8,128)S(1)} %add_add_fusion.2), channel_id=1, source_target_pairs={{0,12},{1,13},{2,14},{3,15},{4,8},{5,9},{6,10},{7,11},{8,4},{9,5},... | collective-permute-start | bytes 49160 | tf_op jit(solution)/shard_map/ppermute | solution.py:17
  200.5 1.2 collective-permute-done.5
  201.7 2.0 collective-permute-done.4
  203.7 1.5 collective-permute-done.3
  205.3 1.2 collective-permute-start.8
  206.4 3.3 %collective-permute-start.7 = (f32[64,64]{0,1:T(8,128)S(1)}, f32[64,64]{0,1:T(8,128)S(1)}, u32[]{:S(2)}, u32[]{:S(2)}) collective-permute-start(f32[64,64]{0,1:T(8,128)S(1)} %add_add_fusion.1), channel_id=1, source_target_pairs={{0,32},{1,33},{2,34},{3,35},{4,36},{5,37},{6,38},{7,39},{8,40},{9,... | collective-permute-start | bytes 49160 | tf_op jit(solution)/shard_map/ppermute | solution.py:16
  210.3 1.5 collective-permute-done.8
  212.0 3.2 %collective-permute-done.6 = f32[64,64]{0,1:T(8,128)S(1)} collective-permute-done((f32[64,64]{0,1:T(8,128)S(1)}, f32[64,64]{0,1:T(8,128)S(1)}, u32[]{:S(2)}, u32[]{:S(2)}) %collective-permute-start.6) | collective-permute-done | bytes 16416 | tf_op jit(solution)/shard_map/ppermute | solution.py:15
  215.3 5.4 %collective-permute-done.9 = f32[64,64]{0,1:T(8,128)S(1)} collective-permute-done((f32[64,64]{0,1:T(8,128)S(1)}, f32[64,64]{0,1:T(8,128)S(1)}, u32[]{:S(2)}, u32[]{:S(2)}) %collective-permute-start.9) | collective-permute-done | bytes 16416 | tf_op jit(solution)/shard_map/ppermute | solution.py:21
  220.8 5.8 %cholesky.16 = f32[64,64]{1,0:T(8,128)S(1)} custom-call(f32[64,64]{1,0:T(8,128)S(1)} %fusion.28), custom_call_target="Cholesky" | custom-call | tf_op jit(solution)/shard_map/jit(cholesky)/cholesky | solution.py:167
  228.0 4.9 %custom-call.7 = f32[1,64,64]{1,2,0:T(8,128)S(1)} custom-call(f32[1,64,64]{2,1,0:T(8,128)S(1)} %fusion.26), custom_call_target="InvertDiagBlocksLowerTriangular" | custom-call | tf_op jit(solution)/shard_map/jit(_solve_triangular)/triangular_solve | solution.py:168
  232.9 1.0 fusion.15
  (44 shorter events, 7.4 us)
Async XLA Ops:
  7.2 86.8 %all-gather.3.cloned.1.call-start = ((), (), s32[]{:S(2)}) async-start(), calls=%async_computation.3 | async-start | bytes 8454144 | tf_op jit(solution)/shard_map/all_gather | solution.py:118
  9.5 23.1 %copy-start.3 = (s32[128]{0:T(128)S(1)}, s32[128]{0:T(128)}, u32[]{:S(2)}) copy-start(s32[128]{0:T(128)} %param.8) | copy-start | bytes 1540
  9.5 34.8 %copy-start.2 = (s32[512]{0:T(512)S(1)}, s32[512]{0:T(512)}, u32[]{:S(2)}) copy-start(s32[512]{0:T(512)} %rows_ref.3) | copy-start | bytes 6148
  9.6 41.5 %copy-start.1 = (bf16[512,64]{0,1:T(8,128)(2,1)S(1)}, bf16[512,64]{0,1:T(8,128)(2,1)}, u32[]{:S(2)}) copy-start(bf16[512,64]{0,1:T(8,128)(2,1)} %param.9) | copy-start | bytes 196612
  21.5 22.6 %all-to-all-start = ((f32[128,1,516]{2,1,0:T(1,128)}), f32[128,1,516]{2,1,0:T(1,128)S(1)}, u32[]{:S(2)}, u32[]{:S(2)}) async-start(f32[128,1,516]{2,1,0:T(1,128)} %copy.32), calls=%async_computation | async-start | bytes 655360 | tf_op jit(solution)/shard_map/all_to_all | solution.py:138
  46.3 23.0 %all-to-all-start.1 = ((f32[128,1,512]{2,1,0:T(1,128)}), f32[128,1,512]{2,1,0:T(1,128)S(1)}, u32[]{:S(2)}, u32[]{:S(2)}) async-start(f32[128,1,512]{2,1,0:T(1,128)} %broadcast_in_dim.6), calls=%async_computation.1 | async-start | bytes 524288 | tf_op jit(solution)/shard_map/all_to_all | solution.py:148
  69.4 108.7 %all-to-all-start.2 = ((bf16[512,64,128]{2,1,0:T(8,128)(2,1)}), bf16[512,64,128]{2,1,0:T(8,128)(2,1)}, u32[]{:S(2)}, u32[]{:S(2)}) async-start(bf16[512,64,128]{2,1,0:T(8,128)(2,1)} %shard_map.68), calls=%async_computation.2 | async-start | bytes 16777216 | tf_op jit(solution)/shard_map/all_to_all | solution.py:153
  112.1 73.8 %copy-start = (f32[4,64,128]{2,1,0:T(8,128)S(1)}, f32[4,64,128]{2,1,0:T(8,128)}, u32[]{:S(2)}) copy-start(f32[4,64,128]{2,1,0:T(8,128)} %shard_map.69) | copy-start | bytes 393220
  186.2 5.0 %collective-permute-start.1 = (f32[64,64]{0,1:T(8,128)S(1)}, f32[64,64]{0,1:T(8,128)S(1)}, u32[]{:S(2)}, u32[]{:S(2)}) collective-permute-start(f32[64,64]{0,1:T(8,128)S(1)} %fusion.17), channel_id=1, source_target_pairs={{0,2},{1,3},{2,0},{3,1},{4,6},{5,7},{6,4},{7,5},{8,10},{9,11},{10,... | collective-permute-start | bytes 49160 | tf_op jit(solution)/shard_map/ppermute | solution.py:16
  189.3 1.9 collective-permute-start
  190.1 3.5 %collective-permute-start.2 = (f32[64,64]{0,1:T(8,128)S(1)}, f32[64,64]{0,1:T(8,128)S(1)}, u32[]{:S(2)}, u32[]{:S(2)}) collective-permute-start(f32[64,64]{0,1:T(8,128)S(1)} %fusion.17), channel_id=1, source_target_pairs={{0,3},{1,2},{2,1},{3,0},{4,7},{5,6},{6,5},{7,4},{8,11},{9,10},{10,... | collective-permute-start | bytes 49160 | tf_op jit(solution)/shard_map/ppermute | solution.py:17
  193.6 8.1 %collective-permute-start.5 = (f32[64,64]{0,1:T(8,128)S(1)}, f32[64,64]{0,1:T(8,128)S(1)}, u32[]{:S(2)}, u32[]{:S(2)}) collective-permute-start(f32[64,64]{0,1:T(8,128)S(1)} %add_add_fusion.2), channel_id=1, source_target_pairs={{0,12},{1,13},{2,14},{3,15},{4,8},{5,9},{6,10},{7,11},{8,4},{9,5},... | collective-permute-start | bytes 49160 | tf_op jit(solution)/shard_map/ppermute | solution.py:17
  199.8 3.9 %collective-permute-start.4 = (f32[64,64]{0,1:T(8,128)S(1)}, f32[64,64]{0,1:T(8,128)S(1)}, u32[]{:S(2)}, u32[]{:S(2)}) collective-permute-start(f32[64,64]{0,1:T(8,128)S(1)} %add_add_fusion.2), channel_id=1, source_target_pairs={{0,8},{1,9},{2,10},{3,11},{4,12},{5,13},{6,14},{7,15},{8,0},{9,1},... | collective-permute-start | bytes 49160 | tf_op jit(solution)/shard_map/ppermute | solution.py:16
  199.8 5.4 %collective-permute-start.3 = (f32[64,64]{0,1:T(8,128)S(1)}, f32[64,64]{0,1:T(8,128)S(1)}, u32[]{:S(2)}, u32[]{:S(2)}) collective-permute-start(f32[64,64]{0,1:T(8,128)S(1)} %add_add_fusion.2), channel_id=1, source_target_pairs={{0,4},{1,5},{2,6},{3,7},{4,0},{5,1},{6,2},{7,3},{8,12},{9,13},{10,... | collective-permute-start | bytes 49160 | tf_op jit(solution)/shard_map/ppermute | solution.py:15
  205.3 6.6 %collective-permute-start.8 = (f32[64,64]{0,1:T(8,128)S(1)}, f32[64,64]{0,1:T(8,128)S(1)}, u32[]{:S(2)}, u32[]{:S(2)}) collective-permute-start(f32[64,64]{0,1:T(8,128)S(1)} %add_add_fusion.1), channel_id=1, source_target_pairs={{0,48},{1,49},{2,50},{3,51},{4,52},{5,53},{6,54},{7,55},{8,56},{9,... | collective-permute-start | bytes 49160 | tf_op jit(solution)/shard_map/ppermute | solution.py:17
  206.4 5.6 %collective-permute-start.7 = (f32[64,64]{0,1:T(8,128)S(1)}, f32[64,64]{0,1:T(8,128)S(1)}, u32[]{:S(2)}, u32[]{:S(2)}) collective-permute-start(f32[64,64]{0,1:T(8,128)S(1)} %add_add_fusion.1), channel_id=1, source_target_pairs={{0,32},{1,33},{2,34},{3,35},{4,36},{5,37},{6,38},{7,39},{8,40},{9,... | collective-permute-start | bytes 49160 | tf_op jit(solution)/shard_map/ppermute | solution.py:16
  209.8 5.4 %collective-permute-start.6 = (f32[64,64]{0,1:T(8,128)S(1)}, f32[64,64]{0,1:T(8,128)S(1)}, u32[]{:S(2)}, u32[]{:S(2)}) collective-permute-start(f32[64,64]{0,1:T(8,128)S(1)} %add_add_fusion.1), channel_id=1, source_target_pairs={{0,16},{1,17},{2,18},{3,19},{4,20},{5,21},{6,22},{7,23},{8,24},{9,... | collective-permute-start | bytes 49160 | tf_op jit(solution)/shard_map/ppermute | solution.py:15
  215.2 5.5 %collective-permute-start.9 = (f32[64,64]{0,1:T(8,128)S(1)}, f32[64,64]{0,1:T(8,128)S(1)}, u32[]{:S(2)}, u32[]{:S(2)}) collective-permute-start(f32[64,64]{0,1:T(8,128)S(1)} %add_add_fusion), channel_id=1, source_target_pairs={{0,64},{1,65},{2,66},{3,67},{4,68},{5,69},{6,70},{7,71},{8,72},{9,... | collective-permute-start | bytes 49160 | tf_op jit(solution)/shard_map/ppermute | solution.py:21
Sparse Core Ops, SparseCore 0:
  11.0 82.8 all-gather.2

commit v9 on v8

--- a/solution.py
+++ b/solution.py
@@ -23,22 +23,19 @@
     return x
 
 
-GROUP = 32
+TERMS_GROUP = 256
 
 
 def terms_kernel(rows_ref, live_ref, tiles_ref, own_ref, out_ref):
     step = pl.program_id(0)
     size = tiles_ref.shape[1]
 
-    def body(j, carry):
-        t = step * GROUP + j
+    for j in range(TERMS_GROUP):
+        t = step * TERMS_GROUP + j
         start = pl.multiple_of(rows_ref[t] * size, size)
         block = own_ref[:, pl.ds(start, size)]
         term = jnp.dot(block, tiles_ref[j], preferred_element_type=jnp.float32).astype(out_ref.dtype)
         out_ref[j] = jnp.where(live_ref[t] > 0, term, jnp.zeros_like(term))
-        return carry
-
-    lax.fori_loop(0, GROUP, body, 0, unroll=True)
 
 
 def mirror_terms(tiles, rows, live, own_t):
@@ -48,12 +45,12 @@
         terms_kernel,
         grid_spec=pltpu.PrefetchScalarGridSpec(
             num_scalar_prefetch=2,
-            grid=(slots // GROUP,),
+            grid=(slots // TERMS_GROUP,),
             in_specs=[
-                pl.BlockSpec((GROUP, size, size), lambda i, r, l: (i, 0, 0)),
+                pl.BlockSpec((TERMS_GROUP, size, size), lambda i, r, l: (i, 0, 0)),
                 pl.BlockSpec(memory_space=pltpu.VMEM),
             ],
-            out_specs=pl.BlockSpec((GROUP, width, size), lambda i, r, l: (i, 0, 0)),
+            out_specs=pl.BlockSpec((TERMS_GROUP, width, size), lambda i, r, l: (i, 0, 0)),
         ),
         out_shape=jax.ShapeDtypeStruct((slots, width, size), jnp.bfloat16),
     )(rows, live, tiles, own_t)

time: 241 us -> 248 us (1.029)
  starting transfers between devices: 42.3 us -> 49.7 us
  Pallas kernels: 35.8 us -> 29.1 us
  waiting for transfers between devices: 108 us -> 113 us
    all_gather x1, waiting for transfers between devices: 12.6 us -> 84.2 us  [shards(): vec_all = lax.all_gather(vec_t, AXES, axis=0)]
    all_to_all x1, waiting for transfers between devices: 66 us -> 0.69 us  [shards(): lax.all_to_all(terms, AXES, split_axis=0, concat_axis=0, tiled=True)]
    ppermute x3, starting transfers between devices: 7.46 us -> 14.9 us  [butterfly_sum(): lax.ppermute(x, AXES, [(i, i ^ 3 * step) for i in range(peer_count)])]
    pallas_call x1, Pallas kernels: 17.6 us -> 10.9 us  [mirror_terms(): pl.pallas_call(terms_kernel, grid_spec=pltpu.PrefetchScalarGridSpec(num_s...]
  transfers between devices with their start and end apart: 14 -> 14, of which waited for: 12 -> 12; matrix products, arithmetic and copies ran while one was open for 8% -> 8% of each run, Pallas kernels for 15% -> 12%
where the time goes in v9:
time: 248 us; the launch traced here: 246 us
  waiting for transfers between devices  113 us (46%)
  starting transfers between devices  49.7 us (20%)
  Pallas kernels  29.1 us (12%)
  other arithmetic  25 us (10%)
  between operations  14.2 us (6%)
  matrix products  10.8 us (4%)
  local copies, waits for them, and re-layouts  4.31 us (2%)
    all_gather x1, waiting for transfers between devices, shards(): vec_all = lax.all_gather(vec_t, AXES, axis=0)  84.2 us
    pallas_call x1, Pallas kernels, forward_product(): pl.pallas_call(forward_kernel, grid_spec=pltpu.PrefetchScalarGridSpec(num...  18.2 us
    ppermute x3, starting transfers between devices, butterfly_sum(): lax.ppermute(x, AXES, [(i, i ^ 3 * step) for i in range(peer_count)])  14.9 us
    all_to_all x1, starting transfers between devices, shards(): got = lax.all_to_all(payload, AXES, split_axis=0, concat_axis=0, tiled=True)  11.1 us
    pallas_call x1, Pallas kernels, mirror_terms(): pl.pallas_call(terms_kernel, grid_spec=pltpu.PrefetchScalarGridSpec(num_s...  10.9 us
    all_to_all x1, waiting for transfers between devices, shards(): got = lax.all_to_all(payload, AXES, split_axis=0, concat_axis=0, tiled=True)  10.6 us
    all_to_all x1, starting transfers between devices, shards(): lax.all_to_all(terms, AXES, split_axis=0, concat_axis=0, tiled=True)  10.4 us
    reduce_sum x1, other arithmetic, shards(): col_sums = jnp.sum(tiles, axis=1, dtype=jnp.float32)  10.2 us
  transfers between devices with their start and end apart: 14, of which 12 were waited for; matrix products, arithmetic and copies ran while one was open for 8% of the time, Pallas kernels for 12%

profile of v9, /device:TPU:0, one launch (start us, length us, event | category | flops | bytes accessed | tf_op | source)
XLA Modules:
  0.0 246.1 jit_solution(9026622751292350217)
XLA Ops:
  7.2 0.7 all-gather.3.cloned.1.call-update
  7.9 0.8 eq.49
  8.8 0.8 fusion.19
  9.6 10.2 %convert_reduce_fusion = (f32[512,128]{1,0:T(8,128)S(1)}, f32[512,128]{1,0:T(8,128)S(1)}) fusion(bf16[512,128,128]{2,1,0:T(8,128)(2,1)} %tiles_ref.3), kind=kLoop, calls=%fused_computation | loop fusion | flops 25034752 | bytes 17301504 | tf_op jit(solution)/shard_map/reduce_sum | solution.py:124
  20.6 0.9 copy.32
  21.5 11.1 %all-to-all-start = ((f32[128,1,516]{2,1,0:T(1,128)}), f32[128,1,516]{2,1,0:T(1,128)S(1)}, u32[]{:S(2)}, u32[]{:S(2)}) async-start(f32[128,1,516]{2,1,0:T(1,128)} %copy.32), calls=%async_computation | async-start | bytes 655360 | tf_op jit(solution)/shard_map/all_to_all | solution.py:135
  33.4 10.6 %all-to-all-done = f32[128,1,516]{2,1,0:T(1,128)S(1)} async-done(((f32[128,1,516]{2,1,0:T(1,128)}), f32[128,1,516]{2,1,0:T(1,128)S(1)}, u32[]{:S(2)}, u32[]{:S(2)}) %all-to-all-start) | async-done | bytes 264224 | tf_op jit(solution)/shard_map/all_to_all | solution.py:135
  44.4 1.1 fusion.40
  45.5 0.8 broadcast_in_dim.6
  46.3 4.8 %all-to-all-start.1 = ((f32[128,1,512]{2,1,0:T(1,128)}), f32[128,1,512]{2,1,0:T(1,128)S(1)}, u32[]{:S(2)}, u32[]{:S(2)}) async-start(f32[128,1,512]{2,1,0:T(1,128)} %broadcast_in_dim.6), calls=%async_computation.1 | async-start | bytes 524288 | tf_op jit(solution)/shard_map/all_to_all | solution.py:145
  51.7 10.9 %shard_map.68 = bf16[512,64,128]{2,1,0:T(8,128)(2,1)} custom-call(s32[512]{0:T(512)} %rows_ref.3, s32[512]{0:T(512)} %get-tuple-element.12.live_ref, bf16[512,128,128]{2,1,0:T(8,128)(2,1)} %tiles_ref.3, bf16[64,512]{1,0:T(8,128)(2,1)} %fusion.20.own_ref), custom_call_target="tpu_custom_call" | custom-call | tf_op jit(solution)/shard_map/pallas_call | solution.py:44
  62.7 10.4 %all-to-all-start.2 = ((bf16[512,64,128]{2,1,0:T(8,128)(2,1)}), bf16[512,64,128]{2,1,0:T(8,128)(2,1)}, u32[]{:S(2)}, u32[]{:S(2)}) async-start(bf16[512,64,128]{2,1,0:T(8,128)(2,1)} %shard_map.68), calls=%async_computation.2 | async-start | bytes 16777216 | tf_op jit(solution)/shard_map/all_to_all | solution.py:150
  73.9 0.9 reshape.92.inv_ref
  74.8 84.2 %all-gather.3.cloned.1.call-done = bf16[8192,512]{1,0:T(8,128)(2,1)} async-done(((bf16[64,512]{1,0:T(8,128)(2,1)}), bf16[8192,512]{1,0:T(8,128)(2,1)}) %all-gather.3.cloned.1.call-update) | async-done | bytes 8388624 | tf_op jit(solution)/shard_map/all_gather | solution.py:115
  159.0 18.2 %shard_map.69 = f32[4,64,128]{2,1,0:T(8,128)} custom-call(s32[512]{0:T(512)} %add_select_fusion.1.places_ref, s32[512]{0:T(512)} %cols_ref.1, s32[512]{0:T(512)} %rows_ref.3, s32[512]{0:T(512)} %get-tuple-element.12.live_ref, bf16[512,128,128]{2,1,0:T(8,128)(2,1)} %tiles_ref.3, bf16[128,64,512]{2,1,0:T(8,128)(2,1)} %bitcast.49, f32[128,1,512]{2,1,0:T(1,128)} %reshape.92.inv_ref), custom_call_target="tpu_custom_call" | custom-call | tf_op jit(solution)/shard_map/pallas_call | solution.py:86
  177.2 0.7 all-to-all-done.2
  177.9 7.8 %fusion = f32[4,64,128]{2,0,1:T(4,128)S(1)} fusion(bf16[512,64,128]{2,1,0:T(8,128)(2,1)} %all-to-all-done.2, s32[512]{0:T(512)S(1)} %eq.53), kind=kOutput, calls=%fused_computation.2 | convolution fusion | flops 33556480 | bytes 8521728 | tf_op jit(solution)/shard_map/tr,tka->rka/dot_general | solution.py:158
  186.0 5.0 %collective-permute-start.1 = (f32[64,64]{0,1:T(8,128)S(1)}, f32[64,64]{0,1:T(8,128)S(1)}, u32[]{:S(2)}, u32[]{:S(2)}) collective-permute-start(f32[64,64]{0,1:T(8,128)S(1)} %fusion.17), channel_id=1, source_target_pairs={{0,2},{1,3},{2,0},{3,1},{4,6},{5,7},{6,4},{7,5},{8,10},{9,11},{10,... | collective-permute-start | bytes 49160 | tf_op jit(solution)/shard_map/ppermute | solution.py:16
  191.2 1.7 collective-permute-done.1
  192.9 1.4 collective-permute-done.2
  194.4 12.3 %collective-permute-start.5 = (f32[64,64]{0,1:T(8,128)S(1)}, f32[64,64]{0,1:T(8,128)S(1)}, u32[]{:S(2)}, u32[]{:S(2)}) collective-permute-start(f32[64,64]{0,1:T(8,128)S(1)} %add_add_fusion.2), channel_id=1, source_target_pairs={{0,12},{1,13},{2,14},{3,15},{4,8},{5,9},{6,10},{7,11},{8,4},{9,5},... | collective-permute-start | bytes 49160 | tf_op jit(solution)/shard_map/ppermute | solution.py:17
  207.3 1.2 collective-permute-done.5
  208.5 2.0 collective-permute-done.4
  210.6 1.5 collective-permute-done.3
  212.1 2.4 collective-permute-start.8
  215.1 2.0 collective-permute-start.6
  217.2 1.4 collective-permute-done.8
  218.7 1.8 collective-permute-done.6
  220.7 5.4 %collective-permute-done.9 = f32[64,64]{0,1:T(8,128)S(1)} collective-permute-done((f32[64,64]{0,1:T(8,128)S(1)}, f32[64,64]{0,1:T(8,128)S(1)}, u32[]{:S(2)}, u32[]{:S(2)}) %collective-permute-start.9) | collective-permute-done | bytes 16416 | tf_op jit(solution)/shard_map/ppermute | solution.py:21
  226.2 5.8 %cholesky.16 = f32[64,64]{1,0:T(8,128)S(1)} custom-call(f32[64,64]{1,0:T(8,128)S(1)} %fusion.28), custom_call_target="Cholesky" | custom-call | tf_op jit(solution)/shard_map/jit(cholesky)/cholesky | solution.py:164
  233.3 4.9 %custom-call.7 = f32[1,64,64]{1,2,0:T(8,128)S(1)} custom-call(f32[1,64,64]{2,1,0:T(8,128)S(1)} %fusion.26), custom_call_target="InvertDiagBlocksLowerTriangular" | custom-call | tf_op jit(solution)/shard_map/jit(_solve_triangular)/triangular_solve | solution.py:165
  238.2 1.0 fusion.15
  (44 shorter events, 6.9 us)
Async XLA Ops:
  7.2 151.8 %all-gather.3.cloned.1.call-start = ((), (), s32[]{:S(2)}) async-start(), calls=%async_computation.3 | async-start | bytes 8454144 | tf_op jit(solution)/shard_map/all_gather | solution.py:115
  9.5 23.1 %copy-start.3 = (s32[128]{0:T(128)S(1)}, s32[128]{0:T(128)}, u32[]{:S(2)}) copy-start(s32[128]{0:T(128)} %param.8) | copy-start | bytes 1540
  9.5 34.8 %copy-start.2 = (s32[512]{0:T(512)S(1)}, s32[512]{0:T(512)}, u32[]{:S(2)}) copy-start(s32[512]{0:T(512)} %rows_ref.3) | copy-start | bytes 6148
  9.6 41.5 %copy-start.1 = (bf16[512,64]{0,1:T(8,128)(2,1)S(1)}, bf16[512,64]{0,1:T(8,128)(2,1)}, u32[]{:S(2)}) copy-start(bf16[512,64]{0,1:T(8,128)(2,1)} %param.9) | copy-start | bytes 196612
  21.5 22.6 %all-to-all-start = ((f32[128,1,516]{2,1,0:T(1,128)}), f32[128,1,516]{2,1,0:T(1,128)S(1)}, u32[]{:S(2)}, u32[]{:S(2)}) async-start(f32[128,1,516]{2,1,0:T(1,128)} %copy.32), calls=%async_computation | async-start | bytes 655360 | tf_op jit(solution)/shard_map/all_to_all | solution.py:135
  46.3 16.4 %all-to-all-start.1 = ((f32[128,1,512]{2,1,0:T(1,128)}), f32[128,1,512]{2,1,0:T(1,128)S(1)}, u32[]{:S(2)}, u32[]{:S(2)}) async-start(f32[128,1,512]{2,1,0:T(1,128)} %broadcast_in_dim.6), calls=%async_computation.1 | async-start | bytes 524288 | tf_op jit(solution)/shard_map/all_to_all | solution.py:145
  62.7 115.2 %all-to-all-start.2 = ((bf16[512,64,128]{2,1,0:T(8,128)(2,1)}), bf16[512,64,128]{2,1,0:T(8,128)(2,1)}, u32[]{:S(2)}, u32[]{:S(2)}) async-start(bf16[512,64,128]{2,1,0:T(8,128)(2,1)} %shard_map.68), calls=%async_computation.2 | async-start | bytes 16777216 | tf_op jit(solution)/shard_map/all_to_all | solution.py:150
  177.2 8.5 %copy-start = (f32[4,64,128]{2,1,0:T(8,128)S(1)}, f32[4,64,128]{2,1,0:T(8,128)}, u32[]{:S(2)}) copy-start(f32[4,64,128]{2,1,0:T(8,128)} %shard_map.69) | copy-start | bytes 393220
  186.0 6.9 %collective-permute-start.1 = (f32[64,64]{0,1:T(8,128)S(1)}, f32[64,64]{0,1:T(8,128)S(1)}, u32[]{:S(2)}, u32[]{:S(2)}) collective-permute-start(f32[64,64]{0,1:T(8,128)S(1)} %fusion.17), channel_id=1, source_target_pairs={{0,2},{1,3},{2,0},{3,1},{4,6},{5,7},{6,4},{7,5},{8,10},{9,11},{10,... | collective-permute-start | bytes 49160 | tf_op jit(solution)/shard_map/ppermute | solution.py:16
  191.0 1.9 collective-permute-start
  191.0 3.3 %collective-permute-start.2 = (f32[64,64]{0,1:T(8,128)S(1)}, f32[64,64]{0,1:T(8,128)S(1)}, u32[]{:S(2)}, u32[]{:S(2)}) collective-permute-start(f32[64,64]{0,1:T(8,128)S(1)} %fusion.17), channel_id=1, source_target_pairs={{0,3},{1,2},{2,1},{3,0},{4,7},{5,6},{6,5},{7,4},{8,11},{9,10},{10,... | collective-permute-start | bytes 49160 | tf_op jit(solution)/shard_map/ppermute | solution.py:17
  194.4 14.2 %collective-permute-start.5 = (f32[64,64]{0,1:T(8,128)S(1)}, f32[64,64]{0,1:T(8,128)S(1)}, u32[]{:S(2)}, u32[]{:S(2)}) collective-permute-start(f32[64,64]{0,1:T(8,128)S(1)} %add_add_fusion.2), channel_id=1, source_target_pairs={{0,12},{1,13},{2,14},{3,15},{4,8},{5,9},{6,10},{7,11},{8,4},{9,5},... | collective-permute-start | bytes 49160 | tf_op jit(solution)/shard_map/ppermute | solution.py:17
  206.7 3.9 %collective-permute-start.4 = (f32[64,64]{0,1:T(8,128)S(1)}, f32[64,64]{0,1:T(8,128)S(1)}, u32[]{:S(2)}, u32[]{:S(2)}) collective-permute-start(f32[64,64]{0,1:T(8,128)S(1)} %add_add_fusion.2), channel_id=1, source_target_pairs={{0,8},{1,9},{2,10},{3,11},{4,12},{5,13},{6,14},{7,15},{8,0},{9,1},... | collective-permute-start | bytes 49160 | tf_op jit(solution)/shard_map/ppermute | solution.py:16
  206.7 5.4 %collective-permute-start.3 = (f32[64,64]{0,1:T(8,128)S(1)}, f32[64,64]{0,1:T(8,128)S(1)}, u32[]{:S(2)}, u32[]{:S(2)}) collective-permute-start(f32[64,64]{0,1:T(8,128)S(1)} %add_add_fusion.2), channel_id=1, source_target_pairs={{0,4},{1,5},{2,6},{3,7},{4,0},{5,1},{6,2},{7,3},{8,12},{9,13},{10,... | collective-permute-start | bytes 49160 | tf_op jit(solution)/shard_map/ppermute | solution.py:15
  212.1 6.5 %collective-permute-start.8 = (f32[64,64]{0,1:T(8,128)S(1)}, f32[64,64]{0,1:T(8,128)S(1)}, u32[]{:S(2)}, u32[]{:S(2)}) collective-permute-start(f32[64,64]{0,1:T(8,128)S(1)} %add_add_fusion.1), channel_id=1, source_target_pairs={{0,48},{1,49},{2,50},{3,51},{4,52},{5,53},{6,54},{7,55},{8,56},{9,... | collective-permute-start | bytes 49160 | tf_op jit(solution)/shard_map/ppermute | solution.py:17
  214.5 4.3 %collective-permute-start.7 = (f32[64,64]{0,1:T(8,128)S(1)}, f32[64,64]{0,1:T(8,128)S(1)}, u32[]{:S(2)}, u32[]{:S(2)}) collective-permute-start(f32[64,64]{0,1:T(8,128)S(1)} %add_add_fusion.1), channel_id=1, source_target_pairs={{0,32},{1,33},{2,34},{3,35},{4,36},{5,37},{6,38},{7,39},{8,40},{9,... | collective-permute-start | bytes 49160 | tf_op jit(solution)/shard_map/ppermute | solution.py:16
  215.1 5.4 %collective-permute-start.6 = (f32[64,64]{0,1:T(8,128)S(1)}, f32[64,64]{0,1:T(8,128)S(1)}, u32[]{:S(2)}, u32[]{:S(2)}) collective-permute-start(f32[64,64]{0,1:T(8,128)S(1)} %add_add_fusion.1), channel_id=1, source_target_pairs={{0,16},{1,17},{2,18},{3,19},{4,20},{5,21},{6,22},{7,23},{8,24},{9,... | collective-permute-start | bytes 49160 | tf_op jit(solution)/shard_map/ppermute | solution.py:15
  220.6 5.5 %collective-permute-start.9 = (f32[64,64]{0,1:T(8,128)S(1)}, f32[64,64]{0,1:T(8,128)S(1)}, u32[]{:S(2)}, u32[]{:S(2)}) collective-permute-start(f32[64,64]{0,1:T(8,128)S(1)} %add_add_fusion), channel_id=1, source_target_pairs={{0,64},{1,65},{2,66},{3,67},{4,68},{5,69},{6,70},{7,71},{8,72},{9,... | collective-permute-start | bytes 49160 | tf_op jit(solution)/shard_map/ppermute | solution.py:21
Sparse Core Ops, SparseCore 0:
  11.0 147.9 all-gather.2

commit v10 on v8

--- a/solution.py
+++ b/solution.py
@@ -115,7 +115,13 @@
     highest = lax.Precision.HIGHEST
 
     vec_t = vectors.T
-    vec_all = lax.all_gather(vec_t, AXES, axis=0)
+    outer_me = lax.axis_index("outer")
+    shifted = [vec_t] + [
+        lax.ppermute(vec_t, "outer", [(i, (i + k) % outer_count) for i in range(outer_count)])
+        for k in range(1, outer_count)
+    ]
+    vec_all = lax.all_gather(jnp.stack(shifted), "inner", axis=0)
+    vec_all = vec_all.reshape(peer_count, vec_width, rows_dev)
 
     slot_number = jnp.arange(slot_total, dtype=jnp.int32) % slot_count
     live = slot_number < jnp.repeat(counts, slot_count)
@@ -152,10 +158,12 @@
     terms, inv_all = lax.optimization_barrier((terms, inv_all))
     got_terms = lax.all_to_all(terms, AXES, split_axis=0, concat_axis=0, tiled=True)
 
-    place = jnp.arange(slot_total, dtype=jnp.int32) // slot_count
-    forward = forward_product(
-        tiles, place, tile_col, tile_row, live_i, vec_all, inv_all.reshape(peer_count, 1, rows_dev), block_count
-    )
+    dest = jnp.arange(slot_total, dtype=jnp.int32) // slot_count
+    place = (dest % inner_count) * outer_count + (outer_me - dest // inner_count) % outer_count
+    held = jnp.arange(peer_count, dtype=jnp.int32)
+    source = ((outer_me - held % outer_count) % outer_count) * inner_count + held // outer_count
+    inv_held = inv_all[source].reshape(peer_count, 1, rows_dev)
+    forward = forward_product(tiles, place, tile_col, tile_row, live_i, vec_all, inv_held, block_count)
     forward, got_terms = lax.optimization_barrier((forward, got_terms))
     got_hot = (got_cols[:, None] == block_ids).astype(jnp.bfloat16)
     mirror = jnp.einsum("tr,tka->rka", got_hot, got_terms, preferred_element_type=jnp.float32)

time: 241 us -> 249 us (1.033)
  starting transfers between devices: 42.3 us -> 51.4 us
  waiting for transfers between devices: 108 us -> 104 us
    all_gather x1, waiting for transfers between devices: 12.6 us -> 0.01 us  [shards(): vec_all = lax.all_gather(jnp.stack(shifted), 'inner', axis=0)]
    all_to_all x1, waiting for transfers between devices: 66 us -> 77.6 us  [shards(): lax.all_to_all(terms, AXES, split_axis=0, concat_axis=0, tiled=True)]
    ppermute x0 -> x3, starting transfers between devices: none -> 7.28 us  [shards(): lax.ppermute(vec_t, 'outer', [(i, (i + k) % outer_count) for i in range(o...]
    ppermute x1, starting transfers between devices: 0.11 us -> 4.34 us  [butterfly_sum(): x = x + lax.ppermute(x, AXES, [(i, i ^ step) for i in range(peer_count)])]
    ppermute x1, waiting for transfers between devices: 5.39 us -> 1.89 us  [butterfly_sum(): x = x + lax.ppermute(x, AXES, [(i, i ^ step) for i in range(peer_count)])]
  transfers between devices with their start and end apart: 14 -> 17, of which waited for: 12 -> 11; matrix products, arithmetic and copies ran while one was open for 8% -> 8% of each run, Pallas kernels for 15% -> 14%
where the time goes in v10:
time: 249 us; the launch traced here: 248 us
  waiting for transfers between devices  104 us (42%)
  starting transfers between devices  51.4 us (21%)
  Pallas kernels  35.7 us (14%)
  other arithmetic  26.7 us (11%)
  between operations  14.2 us (6%)
  matrix products  10.8 us (4%)
  local copies, waits for them, and re-layouts  5.07 us (2%)
    all_to_all x1, waiting for transfers between devices, shards(): lax.all_to_all(terms, AXES, split_axis=0, concat_axis=0, tiled=True)  77.6 us
    pallas_call x1, Pallas kernels, forward_product(): pl.pallas_call(forward_kernel, grid_spec=pltpu.PrefetchScalarGridSpec(num...  18.2 us
    pallas_call x1, Pallas kernels, mirror_terms(): pl.pallas_call(terms_kernel, grid_spec=pltpu.PrefetchScalarGridSpec(num_s...  17.5 us
    all_to_all x1, waiting for transfers between devices, shards(): got = lax.all_to_all(payload, AXES, split_axis=0, concat_axis=0, tiled=True)  10.6 us
    all_to_all x1, starting transfers between devices, shards(): lax.all_to_all(terms, AXES, split_axis=0, concat_axis=0, tiled=True)  10.6 us
    all_to_all x1, starting transfers between devices, shards(): got = lax.all_to_all(payload, AXES, split_axis=0, concat_axis=0, tiled=True)  10.3 us
    reduce_sum x1, other arithmetic, shards(): col_sums = jnp.sum(tiles, axis=1, dtype=jnp.float32)  10.2 us
    dot_general x1, matrix products, shards(): jnp.einsum('tr,tka->rka', got_hot, got_terms, preferred_element_type=jnp....  7.83 us
  transfers between devices with their start and end apart: 17, of which 11 were waited for; matrix products, arithmetic and copies ran while one was open for 8% of the time, Pallas kernels for 14%

profile of v10, /device:TPU:0, one launch (start us, length us, event | category | flops | bytes accessed | tf_op | source)
XLA Modules:
  0.0 247.8 jit_solution(3534612814496149625)
XLA Ops:
  7.2 4.0 %collective-permute-start.1 = (bf16[64,512]{1,0:T(8,128)(2,1)}, bf16[64,512]{1,0:T(8,128)(2,1)S(1)}, u32[]{:S(2)}, u32[]{:S(2)}) collective-permute-start(bf16[64,512]{1,0:T(8,128)(2,1)} %bitcast.60), channel_id=1, source_target_pairs={{0,64},{32,96},{64,0},{96,32},{1,65},{33,97},{65,1},{97,33},{2,66}... | collective-permute-start | bytes 196616 | tf_op jit(solution)/shard_map/ppermute | solution.py:120
  11.2 1.0 collective-permute-start
  12.3 2.2 collective-permute-start.2
  14.5 2.4 collective-permute-done
  16.9 1.6 pad_maximum_fusion
  20.2 10.2 %convert_reduce_fusion = (f32[512,128]{1,0:T(8,128)S(1)}, f32[512,128]{1,0:T(8,128)S(1)}) fusion(bf16[512,128,128]{2,1,0:T(8,128)(2,1)} %tiles_ref.3), kind=kLoop, calls=%fused_computation.1 | loop fusion | flops 25034752 | bytes 17301504 | tf_op jit(solution)/shard_map/reduce_sum | solution.py:133
  31.2 0.9 copy.32
  32.2 10.3 %all-to-all-start = ((f32[128,1,516]{2,1,0:T(1,128)}), f32[128,1,516]{2,1,0:T(1,128)S(1)}, u32[]{:S(2)}, u32[]{:S(2)}) async-start(f32[128,1,516]{2,1,0:T(1,128)} %copy.32), calls=%async_computation | async-start | bytes 655360 | tf_op jit(solution)/shard_map/all_to_all | solution.py:144
  43.2 10.6 %all-to-all-done = f32[128,1,516]{2,1,0:T(1,128)S(1)} async-done(((f32[128,1,516]{2,1,0:T(1,128)}), f32[128,1,516]{2,1,0:T(1,128)S(1)}, u32[]{:S(2)}, u32[]{:S(2)}) %all-to-all-start) | async-done | bytes 264224 | tf_op jit(solution)/shard_map/all_to_all | solution.py:144
  54.2 1.1 fusion.54
  56.2 4.8 %all-to-all-start.1 = ((f32[128,1,512]{2,1,0:T(1,128)}), f32[128,1,512]{2,1,0:T(1,128)S(1)}, u32[]{:S(2)}, u32[]{:S(2)}) async-start(f32[128,1,512]{2,1,0:T(1,128)} %broadcast_in_dim.6), calls=%async_computation.1 | async-start | bytes 524288 | tf_op jit(solution)/shard_map/all_to_all | solution.py:154
  61.6 17.5 %shard_map.68 = bf16[512,64,128]{2,1,0:T(8,128)(2,1)} custom-call(s32[512]{0:T(512)} %rows_ref.3, s32[512]{0:T(512)} %get-tuple-element.12.live_ref, bf16[512,128,128]{2,1,0:T(8,128)(2,1)} %tiles_ref.3, bf16[64,512]{1,0:T(8,128)(2,1)} %fusion.20.own_ref), custom_call_target="tpu_custom_call" | custom-call | tf_op jit(solution)/shard_map/pallas_call | solution.py:47
  79.1 10.6 %all-to-all-start.2 = ((bf16[512,64,128]{2,1,0:T(8,128)(2,1)}), bf16[512,64,128]{2,1,0:T(8,128)(2,1)}, u32[]{:S(2)}, u32[]{:S(2)}) async-start(bf16[512,64,128]{2,1,0:T(8,128)(2,1)} %shard_map.68), calls=%async_computation.2 | async-start | bytes 16777216 | tf_op jit(solution)/shard_map/all_to_all | solution.py:159
  92.2 18.2 %shard_map.69 = f32[4,64,128]{2,1,0:T(8,128)} custom-call(s32[512]{0:T(512)} %fusion.38.places_ref, s32[512]{0:T(512)} %cols_ref.1, s32[512]{0:T(512)} %rows_ref.3, s32[512]{0:T(512)} %get-tuple-element.12.live_ref, bf16[512,128,128]{2,1,0:T(8,128)(2,1)} %tiles_ref.3, bf16[128,64,512]{2,1,0:T(8,128)(2,1)} %all-gather.3.cloned.1.call-done.vec_ref, ...), custom_call_target="tpu_custom_call" | custom-call | tf_op jit(solution)/shard_map/pallas_call | solution.py:89
  110.4 77.6 %all-to-all-done.2 = bf16[512,64,128]{2,1,0:T(8,128)(2,1)} async-done(((bf16[512,64,128]{2,1,0:T(8,128)(2,1)}), bf16[512,64,128]{2,1,0:T(8,128)(2,1)}, u32[]{:S(2)}, u32[]{:S(2)}) %all-to-all-start.2) | async-done | bytes 8388640 | tf_op jit(solution)/shard_map/all_to_all | solution.py:159
  188.0 7.8 %fusion = f32[4,64,128]{2,0,1:T(4,128)S(1)} fusion(bf16[512,64,128]{2,1,0:T(8,128)(2,1)} %all-to-all-done.2, s32[512]{0:T(512)S(1)} %eq.58), kind=kOutput, calls=%fused_computation.3 | convolution fusion | flops 33556480 | bytes 8521728 | tf_op jit(solution)/shard_map/tr,tka->rka/dot_general | solution.py:169
  196.1 3.5 %collective-permute-start.4 = (f32[64,64]{0,1:T(8,128)S(1)}, f32[64,64]{0,1:T(8,128)S(1)}, u32[]{:S(2)}, u32[]{:S(2)}) collective-permute-start(f32[64,64]{0,1:T(8,128)S(1)} %fusion.17), channel_id=1, source_target_pairs={{0,2},{1,3},{2,0},{3,1},{4,6},{5,7},{6,4},{7,5},{8,10},{9,11},{10,... | collective-permute-start | bytes 49160 | tf_op jit(solution)/shard_map/ppermute | solution.py:16
  199.9 1.7 collective-permute-done.4
  201.5 1.4 collective-permute-done.5
  203.0 4.6 %collective-permute-start.8 = (f32[64,64]{0,1:T(8,128)S(1)}, f32[64,64]{0,1:T(8,128)S(1)}, u32[]{:S(2)}, u32[]{:S(2)}) collective-permute-start(f32[64,64]{0,1:T(8,128)S(1)} %add_add_fusion.2), channel_id=1, source_target_pairs={{0,12},{1,13},{2,14},{3,15},{4,8},{5,9},{6,10},{7,11},{8,4},{9,5},... | collective-permute-start | bytes 49160 | tf_op jit(solution)/shard_map/ppermute | solution.py:17
  208.3 1.2 collective-permute-done.8
  209.5 2.0 collective-permute-done.7
  211.5 1.5 collective-permute-done.6
  213.6 2.5 collective-permute-start.10
  216.1 2.1 collective-permute-start.9
  218.1 1.3 collective-permute-done.11
  219.5 2.0 collective-permute-done.9
  221.5 4.3 %collective-permute-start.12 = (f32[64,64]{0,1:T(8,128)S(1)}, f32[64,64]{0,1:T(8,128)S(1)}, u32[]{:S(2)}, u32[]{:S(2)}) collective-permute-start(f32[64,64]{0,1:T(8,128)S(1)} %add_add_fusion), channel_id=1, source_target_pairs={{0,64},{1,65},{2,66},{3,67},{4,68},{5,69},{6,70},{7,71},{8,72},{9,... | collective-permute-start | bytes 49160 | tf_op jit(solution)/shard_map/ppermute | solution.py:21
  225.8 1.9 collective-permute-done.12
  227.8 5.8 %cholesky.16 = f32[64,64]{1,0:T(8,128)S(1)} custom-call(f32[64,64]{1,0:T(8,128)S(1)} %fusion.28), custom_call_target="Cholesky" | custom-call | tf_op jit(solution)/shard_map/jit(cholesky)/cholesky | solution.py:175
  235.0 4.9 %custom-call.7 = f32[1,64,64]{1,2,0:T(8,128)S(1)} custom-call(f32[1,64,64]{2,1,0:T(8,128)S(1)} %fusion.26), custom_call_target="InvertDiagBlocksLowerTriangular" | custom-call | tf_op jit(solution)/shard_map/jit(_solve_triangular)/triangular_solve | solution.py:176
  239.9 1.0 fusion.15
  (54 shorter events, 10.7 us)
Async XLA Ops:
  7.2 85.0 %all-gather.3.cloned.1.call-start = ((), (), s32[]{:S(2)}) async-start(), calls=%async_computation.3 | async-start | bytes 8650752 | tf_op jit(solution)/shard_map/all_gather | solution.py:123
  7.2 7.3 %collective-permute-start.1 = (bf16[64,512]{1,0:T(8,128)(2,1)}, bf16[64,512]{1,0:T(8,128)(2,1)S(1)}, u32[]{:S(2)}, u32[]{:S(2)}) collective-permute-start(bf16[64,512]{1,0:T(8,128)(2,1)} %bitcast.60), channel_id=1, source_target_pairs={{0,64},{32,96},{64,0},{96,32},{1,65},{33,97},{65,1},{97,33},{2,66}... | collective-permute-start | bytes 196616 | tf_op jit(solution)/shard_map/ppermute | solution.py:120
  11.2 5.7 %collective-permute-start = (bf16[64,512]{1,0:T(8,128)(2,1)}, bf16[64,512]{1,0:T(8,128)(2,1)S(1)}, u32[]{:S(2)}, u32[]{:S(2)}) collective-permute-start(bf16[64,512]{1,0:T(8,128)(2,1)} %bitcast.61), channel_id=1, source_target_pairs={{0,32},{32,64},{64,96},{96,0},{1,33},{33,65},{65,97},{97,1},{2,34}... | collective-permute-start | bytes 196616 | tf_op jit(solution)/shard_map/ppermute | solution.py:120
  12.3 4.7 %collective-permute-start.2 = (bf16[64,512]{1,0:T(8,128)(2,1)}, bf16[64,512]{1,0:T(8,128)(2,1)S(1)}, u32[]{:S(2)}, u32[]{:S(2)}) collective-permute-start(bf16[64,512]{1,0:T(8,128)(2,1)} %bitcast.62), channel_id=1, source_target_pairs={{0,96},{32,0},{64,32},{96,64},{1,97},{33,1},{65,33},{97,65},{2,98}... | collective-permute-start | bytes 196616 | tf_op jit(solution)/shard_map/ppermute | solution.py:120
  20.2 22.3 %copy-start.3 = (s32[128]{0:T(128)S(1)}, s32[128]{0:T(128)}, u32[]{:S(2)}) copy-start(s32[128]{0:T(128)} %param.8) | copy-start | bytes 1540
  20.2 34.0 %copy-start.2 = (s32[512]{0:T(512)S(1)}, s32[512]{0:T(512)}, u32[]{:S(2)}) copy-start(s32[512]{0:T(512)} %rows_ref.3) | copy-start | bytes 6148
  20.2 40.7 %copy-start.1 = (bf16[512,64]{0,1:T(8,128)(2,1)S(1)}, bf16[512,64]{0,1:T(8,128)(2,1)}, u32[]{:S(2)}) copy-start(bf16[512,64]{0,1:T(8,128)(2,1)} %param.9) | copy-start | bytes 196612
  32.2 21.7 %all-to-all-start = ((f32[128,1,516]{2,1,0:T(1,128)}), f32[128,1,516]{2,1,0:T(1,128)S(1)}, u32[]{:S(2)}, u32[]{:S(2)}) async-start(f32[128,1,516]{2,1,0:T(1,128)} %copy.32), calls=%async_computation | async-start | bytes 655360 | tf_op jit(solution)/shard_map/all_to_all | solution.py:144
  56.2 22.9 %all-to-all-start.1 = ((f32[128,1,512]{2,1,0:T(1,128)}), f32[128,1,512]{2,1,0:T(1,128)S(1)}, u32[]{:S(2)}, u32[]{:S(2)}) async-start(f32[128,1,512]{2,1,0:T(1,128)} %broadcast_in_dim.6), calls=%async_computation.1 | async-start | bytes 524288 | tf_op jit(solution)/shard_map/all_to_all | solution.py:154
  79.1 108.9 %all-to-all-start.2 = ((bf16[512,64,128]{2,1,0:T(8,128)(2,1)}), bf16[512,64,128]{2,1,0:T(8,128)(2,1)}, u32[]{:S(2)}, u32[]{:S(2)}) async-start(bf16[512,64,128]{2,1,0:T(8,128)(2,1)} %shard_map.68), calls=%async_computation.2 | async-start | bytes 16777216 | tf_op jit(solution)/shard_map/all_to_all | solution.py:159
  110.4 85.5 %copy-start = (f32[4,64,128]{2,1,0:T(8,128)S(1)}, f32[4,64,128]{2,1,0:T(8,128)}, u32[]{:S(2)}) copy-start(f32[4,64,128]{2,1,0:T(8,128)} %shard_map.69) | copy-start | bytes 393220
  196.1 5.4 %collective-permute-start.4 = (f32[64,64]{0,1:T(8,128)S(1)}, f32[64,64]{0,1:T(8,128)S(1)}, u32[]{:S(2)}, u32[]{:S(2)}) collective-permute-start(f32[64,64]{0,1:T(8,128)S(1)} %fusion.17), channel_id=1, source_target_pairs={{0,2},{1,3},{2,0},{3,1},{4,6},{5,7},{6,4},{7,5},{8,10},{9,11},{10,... | collective-permute-start | bytes 49160 | tf_op jit(solution)/shard_map/ppermute | solution.py:16
  199.6 1.9 collective-permute-start.3
  199.6 3.3 %collective-permute-start.5 = (f32[64,64]{0,1:T(8,128)S(1)}, f32[64,64]{0,1:T(8,128)S(1)}, u32[]{:S(2)}, u32[]{:S(2)}) collective-permute-start(f32[64,64]{0,1:T(8,128)S(1)} %fusion.17), channel_id=1, source_target_pairs={{0,3},{1,2},{2,1},{3,0},{4,7},{5,6},{6,5},{7,4},{8,11},{9,10},{10,... | collective-permute-start | bytes 49160 | tf_op jit(solution)/shard_map/ppermute | solution.py:17
  203.0 6.5 %collective-permute-start.8 = (f32[64,64]{0,1:T(8,128)S(1)}, f32[64,64]{0,1:T(8,128)S(1)}, u32[]{:S(2)}, u32[]{:S(2)}) collective-permute-start(f32[64,64]{0,1:T(8,128)S(1)} %add_add_fusion.2), channel_id=1, source_target_pairs={{0,12},{1,13},{2,14},{3,15},{4,8},{5,9},{6,10},{7,11},{8,4},{9,5},... | collective-permute-start | bytes 49160 | tf_op jit(solution)/shard_map/ppermute | solution.py:17
  207.6 3.9 %collective-permute-start.7 = (f32[64,64]{0,1:T(8,128)S(1)}, f32[64,64]{0,1:T(8,128)S(1)}, u32[]{:S(2)}, u32[]{:S(2)}) collective-permute-start(f32[64,64]{0,1:T(8,128)S(1)} %add_add_fusion.2), channel_id=1, source_target_pairs={{0,8},{1,9},{2,10},{3,11},{4,12},{5,13},{6,14},{7,15},{8,0},{9,1},... | collective-permute-start | bytes 49160 | tf_op jit(solution)/shard_map/ppermute | solution.py:16
  207.6 5.4 %collective-permute-start.6 = (f32[64,64]{0,1:T(8,128)S(1)}, f32[64,64]{0,1:T(8,128)S(1)}, u32[]{:S(2)}, u32[]{:S(2)}) collective-permute-start(f32[64,64]{0,1:T(8,128)S(1)} %add_add_fusion.2), channel_id=1, source_target_pairs={{0,4},{1,5},{2,6},{3,7},{4,0},{5,1},{6,2},{7,3},{8,12},{9,13},{10,... | collective-permute-start | bytes 49160 | tf_op jit(solution)/shard_map/ppermute | solution.py:15
  213.1 6.4 %collective-permute-start.11 = (f32[64,64]{0,1:T(8,128)S(1)}, f32[64,64]{0,1:T(8,128)S(1)}, u32[]{:S(2)}, u32[]{:S(2)}) collective-permute-start(f32[64,64]{0,1:T(8,128)S(1)} %add_add_fusion.1), channel_id=1, source_target_pairs={{0,48},{1,49},{2,50},{3,51},{4,52},{5,53},{6,54},{7,55},{8,56},{9,... | collective-permute-start | bytes 49160 | tf_op jit(solution)/shard_map/ppermute | solution.py:17
  213.6 5.9 %collective-permute-start.10 = (f32[64,64]{0,1:T(8,128)S(1)}, f32[64,64]{0,1:T(8,128)S(1)}, u32[]{:S(2)}, u32[]{:S(2)}) collective-permute-start(f32[64,64]{0,1:T(8,128)S(1)} %add_add_fusion.1), channel_id=1, source_target_pairs={{0,32},{1,33},{2,34},{3,35},{4,36},{5,37},{6,38},{7,39},{8,40},{9,... | collective-permute-start | bytes 49160 | tf_op jit(solution)/shard_map/ppermute | solution.py:16
  216.1 5.4 %collective-permute-start.9 = (f32[64,64]{0,1:T(8,128)S(1)}, f32[64,64]{0,1:T(8,128)S(1)}, u32[]{:S(2)}, u32[]{:S(2)}) collective-permute-start(f32[64,64]{0,1:T(8,128)S(1)} %add_add_fusion.1), channel_id=1, source_target_pairs={{0,16},{1,17},{2,18},{3,19},{4,20},{5,21},{6,22},{7,23},{8,24},{9,... | collective-permute-start | bytes 49160 | tf_op jit(solution)/shard_map/ppermute | solution.py:15
  221.5 6.2 %collective-permute-start.12 = (f32[64,64]{0,1:T(8,128)S(1)}, f32[64,64]{0,1:T(8,128)S(1)}, u32[]{:S(2)}, u32[]{:S(2)}) collective-permute-start(f32[64,64]{0,1:T(8,128)S(1)} %add_add_fusion), channel_id=1, source_target_pairs={{0,64},{1,65},{2,66},{3,67},{4,68},{5,69},{6,70},{7,71},{8,72},{9,... | collective-permute-start | bytes 49160 | tf_op jit(solution)/shard_map/ppermute | solution.py:21
Sparse Core Ops, SparseCore 0:
  18.7 57.1 all-gather.2

commit v11 on v8

--- a/solution.py
+++ b/solution.py
@@ -158,7 +158,9 @@
     )
     forward, got_terms = lax.optimization_barrier((forward, got_terms))
     got_hot = (got_cols[:, None] == block_ids).astype(jnp.bfloat16)
-    mirror = jnp.einsum("tr,tka->rka", got_hot, got_terms, preferred_element_type=jnp.float32)
+    mirror = jnp.dot(
+        got_hot.T, got_terms.reshape(got_terms.shape[0], -1), preferred_element_type=jnp.float32
+    ).reshape(block_count, vec_width, tile_size)
     total_t = (forward + mirror).transpose(1, 0, 2).reshape(vec_width, rows_dev)
 
     image_t = inv_root[None, :] * (total_t + scaled_t.astype(jnp.float32))

time: 241 us -> 276 us (1.15)
  local copies, waits for them, and re-layouts: 4.31 us -> 39.8 us
  waiting for transfers between devices: 108 us -> 112 us
    unnamed x9 -> x10, local copies, waits for them, and re-layouts: 0.04 us -> 23.6 us
    dot_general x0 -> x1, local copies, waits for them, and re-layouts: none -> 11.9 us  [shards(): jnp.dot(got_hot.T, got_terms.reshape(got_terms.shape[0], -1), preferred_e...]
    all_to_all x1, waiting for transfers between devices: 66 us -> 69.1 us  [shards(): lax.all_to_all(terms, AXES, split_axis=0, concat_axis=0, tiled=True)]
  transfers between devices with their start and end apart: 14 -> 14, of which waited for: 12 -> 11; matrix products, arithmetic and copies ran while one was open for 8% -> 7% of each run, Pallas kernels for 15% -> 13%
where the time goes in v11:
time: 276 us; the launch traced here: 275 us
  waiting for transfers between devices  112 us (41%)
  starting transfers between devices  40.1 us (15%)
  local copies, waits for them, and re-layouts  39.8 us (14%)
  Pallas kernels  35.8 us (13%)
  other arithmetic  25 us (9%)
  between operations  14.2 us (5%)
  matrix products  8.67 us (3%)
    all_to_all x1, waiting for transfers between devices, shards(): lax.all_to_all(terms, AXES, split_axis=0, concat_axis=0, tiled=True)  69.1 us
    unnamed x10, local copies, waits for them, and re-layouts  23.6 us
    pallas_call x1, Pallas kernels, forward_product(): pl.pallas_call(forward_kernel, grid_spec=pltpu.PrefetchScalarGridSpec(num...  18.2 us
    pallas_call x1, Pallas kernels, mirror_terms(): pl.pallas_call(terms_kernel, grid_spec=pltpu.PrefetchScalarGridSpec(num_s...  17.6 us
    all_gather x1, waiting for transfers between devices, shards(): vec_all = lax.all_gather(vec_t, AXES, axis=0)  12.6 us
    dot_general x1, local copies, waits for them, and re-layouts, shards(): jnp.dot(got_hot.T, got_terms.reshape(got_terms.shape[0], -1), preferred_e...  11.9 us
    all_to_all x1, starting transfers between devices, shards(): got = lax.all_to_all(payload, AXES, split_axis=0, concat_axis=0, tiled=True)  11.1 us
    all_to_all x1, waiting for transfers between devices, shards(): got = lax.all_to_all(payload, AXES, split_axis=0, concat_axis=0, tiled=True)  10.6 us
  transfers between devices with their start and end apart: 14, of which 11 were waited for; matrix products, arithmetic and copies ran while one was open for 7% of the time, Pallas kernels for 13%

profile of v11, /device:TPU:0, one launch (start us, length us, event | category | flops | bytes accessed | tf_op | source)
XLA Modules:
  0.0 275.5 jit_solution(10673787904141319411)
XLA Ops:
  9.6 10.2 %convert_reduce_fusion = (f32[512,128]{1,0:T(8,128)S(1)}, f32[512,128]{1,0:T(8,128)S(1)}) fusion(bf16[512,128,128]{2,1,0:T(8,128)(2,1)} %tiles_ref.3), kind=kLoop, calls=%fused_computation | loop fusion | flops 25034752 | bytes 17301504 | tf_op jit(solution)/shard_map/reduce_sum | solution.py:127
  20.6 0.9 copy.32
  21.5 11.1 %all-to-all-start = ((f32[128,1,516]{2,1,0:T(1,128)}), f32[128,1,516]{2,1,0:T(1,128)S(1)}, u32[]{:S(2)}, u32[]{:S(2)}) async-start(f32[128,1,516]{2,1,0:T(1,128)} %copy.32), calls=%async_computation | async-start | bytes 655360 | tf_op jit(solution)/shard_map/all_to_all | solution.py:138
  33.4 10.6 %all-to-all-done = f32[128,1,516]{2,1,0:T(1,128)S(1)} async-done(((f32[128,1,516]{2,1,0:T(1,128)}), f32[128,1,516]{2,1,0:T(1,128)S(1)}, u32[]{:S(2)}, u32[]{:S(2)}) %all-to-all-start) | async-done | bytes 264224 | tf_op jit(solution)/shard_map/all_to_all | solution.py:138
  44.4 1.1 fusion.39
  45.5 0.9 broadcast_in_dim.6
  46.3 4.8 %all-to-all-start.1 = ((f32[128,1,512]{2,1,0:T(1,128)}), f32[128,1,512]{2,1,0:T(1,128)S(1)}, u32[]{:S(2)}, u32[]{:S(2)}) async-start(f32[128,1,512]{2,1,0:T(1,128)} %broadcast_in_dim.6), calls=%async_computation.1 | async-start | bytes 524288 | tf_op jit(solution)/shard_map/all_to_all | solution.py:148
  51.8 17.6 %shard_map.68 = bf16[512,64,128]{2,1,0:T(8,128)(2,1)} custom-call(s32[512]{0:T(512)} %rows_ref.3, s32[512]{0:T(512)} %get-tuple-element.12.live_ref, bf16[512,128,128]{2,1,0:T(8,128)(2,1)} %tiles_ref.3, bf16[64,512]{1,0:T(8,128)(2,1)} %fusion.18.own_ref), custom_call_target="tpu_custom_call" | custom-call | tf_op jit(solution)/shard_map/pallas_call | solution.py:47
  69.4 10.2 %all-to-all-start.2 = ((bf16[512,64,128]{2,1,0:T(8,128)(2,1)}), bf16[512,64,128]{2,1,0:T(8,128)(2,1)}, u32[]{:S(2)}, u32[]{:S(2)}) async-start(bf16[512,64,128]{2,1,0:T(8,128)(2,1)} %shard_map.68), calls=%async_computation.2 | async-start | bytes 16777216 | tf_op jit(solution)/shard_map/all_to_all | solution.py:153
  80.4 0.9 reshape.97.inv_ref
  81.3 12.6 %all-gather.3.cloned.1.call-done = bf16[8192,512]{1,0:T(8,128)(2,1)} async-done(((bf16[64,512]{1,0:T(8,128)(2,1)}), bf16[8192,512]{1,0:T(8,128)(2,1)}) %all-gather.3.cloned.1.call-update) | async-done | bytes 8388624 | tf_op jit(solution)/shard_map/all_gather | solution.py:118
  93.9 18.2 %shard_map.69 = f32[4,64,128]{2,1,0:T(8,128)} custom-call(s32[512]{0:T(512)} %add_select_fusion.1.places_ref, s32[512]{0:T(512)} %cols_ref.1, s32[512]{0:T(512)} %rows_ref.3, s32[512]{0:T(512)} %get-tuple-element.12.live_ref, bf16[512,128,128]{2,1,0:T(8,128)(2,1)} %tiles_ref.3, bf16[128,64,512]{2,1,0:T(8,128)(2,1)} %bitcast.60, f32[128,1,512]{2,1,0:T(1,128)} %reshape.97.inv_ref), custom_call_target="tpu_custom_call" | custom-call | tf_op jit(solution)/shard_map/pallas_call | solution.py:89
  112.0 69.1 %all-to-all-done.2 = bf16[512,64,128]{2,1,0:T(8,128)(2,1)} async-done(((bf16[512,64,128]{2,1,0:T(8,128)(2,1)}), bf16[512,64,128]{2,1,0:T(8,128)(2,1)}, u32[]{:S(2)}, u32[]{:S(2)}) %all-to-all-start.2) | async-done | bytes 8388640 | tf_op jit(solution)/shard_map/all_to_all | solution.py:153
  181.1 23.6 %copy.60 = bf16[64,8,64,128]{3,1,2,0:T(8,128)(2,1)} copy(bf16[64,8,64,128]{3,2,1,0:T(8,128)(2,1)} %bitcast.19) | data formatting | bytes 16777216
  204.7 11.9 %copy.35 = bf16[8192,512]{1,0:T(8,128)(2,1)} copy(bf16[8192,512]{0,1:T(8,128)(2,1)} %bitcast.59) | data formatting | bytes 16777216 | tf_op jit(solution)/shard_map/dot_general | solution.py:161
  216.6 5.7 %fusion.28 = f32[4,64,128]{2,0,1:T(4,128)S(1)} fusion(bf16[64,128,512]{2,1,0:T(8,128)(2,1)} %bitcast.58, s32[512]{0:T(512)S(1)} %eq.53), kind=kOutput, calls=%fused_computation.48 | convolution fusion | flops 33556480 | bytes 8521728 | tf_op jit(solution)/shard_map/dot_general | solution.py:161
  223.1 1.2 collective-permute-start
  224.8 1.8 collective-permute-done.1
  226.6 1.2 collective-permute-done.2
  227.8 3.4 %collective-permute-start.5 = (f32[64,64]{0,1:T(8,128)S(1)}, f32[64,64]{0,1:T(8,128)S(1)}, u32[]{:S(2)}, u32[]{:S(2)}) collective-permute-start(f32[64,64]{0,1:T(8,128)S(1)} %add_add_fusion.2), channel_id=1, source_target_pairs={{0,12},{1,13},{2,14},{3,15},{4,8},{5,9},{6,10},{7,11},{8,4},{9,5},... | collective-permute-start | bytes 49160 | tf_op jit(solution)/shard_map/ppermute | solution.py:17
  231.2 1.3 collective-permute-start.4
  232.9 1.4 collective-permute-done.5
  234.3 0.9 collective-permute-done.4
  235.2 2.8 %collective-permute-done.3 = f32[64,64]{0,1:T(8,128)S(1)} collective-permute-done((f32[64,64]{0,1:T(8,128)S(1)}, f32[64,64]{0,1:T(8,128)S(1)}, u32[]{:S(2)}, u32[]{:S(2)}) %collective-permute-start.3) | collective-permute-done | bytes 16416 | tf_op jit(solution)/shard_map/ppermute | solution.py:15
  238.0 2.6 collective-permute-start.8
  240.5 4.0 %collective-permute-start.7 = (f32[64,64]{0,1:T(8,128)S(1)}, f32[64,64]{0,1:T(8,128)S(1)}, u32[]{:S(2)}, u32[]{:S(2)}) collective-permute-start(f32[64,64]{0,1:T(8,128)S(1)} %add_add_fusion.1), channel_id=1, source_target_pairs={{0,32},{1,33},{2,34},{3,35},{4,36},{5,37},{6,38},{7,39},{8,40},{9,... | collective-permute-start | bytes 49160 | tf_op jit(solution)/shard_map/ppermute | solution.py:16
  244.6 1.9 collective-permute-done.7
  246.4 3.5 %collective-permute-done.6 = f32[64,64]{0,1:T(8,128)S(1)} collective-permute-done((f32[64,64]{0,1:T(8,128)S(1)}, f32[64,64]{0,1:T(8,128)S(1)}, u32[]{:S(2)}, u32[]{:S(2)}) %collective-permute-start.6) | collective-permute-done | bytes 16416 | tf_op jit(solution)/shard_map/ppermute | solution.py:15
  250.1 5.4 %collective-permute-done.9 = f32[64,64]{0,1:T(8,128)S(1)} collective-permute-done((f32[64,64]{0,1:T(8,128)S(1)}, f32[64,64]{0,1:T(8,128)S(1)}, u32[]{:S(2)}, u32[]{:S(2)}) %collective-permute-start.9) | collective-permute-done | bytes 16416 | tf_op jit(solution)/shard_map/ppermute | solution.py:21
  255.6 5.8 %cholesky.16 = f32[64,64]{1,0:T(8,128)S(1)} custom-call(f32[64,64]{1,0:T(8,128)S(1)} %fusion.26), custom_call_target="Cholesky" | custom-call | tf_op jit(solution)/shard_map/jit(cholesky)/cholesky | solution.py:169
  262.8 4.9 %custom-call.7 = f32[1,64,64]{1,2,0:T(8,128)S(1)} custom-call(f32[1,64,64]{2,1,0:T(8,128)S(1)} %fusion.24), custom_call_target="InvertDiagBlocksLowerTriangular" | custom-call | tf_op jit(solution)/shard_map/jit(_solve_triangular)/triangular_solve | solution.py:170
  267.7 1.0 fusion.13
  (46 shorter events, 8.8 us)
Async XLA Ops:
  7.2 86.7 %all-gather.3.cloned.1.call-start = ((), (), s32[]{:S(2)}) async-start(), calls=%async_computation.3 | async-start | bytes 8454144 | tf_op jit(solution)/shard_map/all_gather | solution.py:118
  9.5 23.1 %copy-start.3 = (s32[128]{0:T(128)S(1)}, s32[128]{0:T(128)}, u32[]{:S(2)}) copy-start(s32[128]{0:T(128)} %param.8) | copy-start | bytes 1540
  9.5 34.8 %copy-start.2 = (s32[512]{0:T(512)S(1)}, s32[512]{0:T(512)}, u32[]{:S(2)}) copy-start(s32[512]{0:T(512)} %rows_ref.3) | copy-start | bytes 6148
  9.6 41.5 %copy-start.1 = (bf16[512,64]{0,1:T(8,128)(2,1)S(1)}, bf16[512,64]{0,1:T(8,128)(2,1)}, u32[]{:S(2)}) copy-start(bf16[512,64]{0,1:T(8,128)(2,1)} %param.9) | copy-start | bytes 196612
  21.5 22.6 %all-to-all-start = ((f32[128,1,516]{2,1,0:T(1,128)}), f32[128,1,516]{2,1,0:T(1,128)S(1)}, u32[]{:S(2)}, u32[]{:S(2)}) async-start(f32[128,1,516]{2,1,0:T(1,128)} %copy.32), calls=%async_computation | async-start | bytes 655360 | tf_op jit(solution)/shard_map/all_to_all | solution.py:138
  46.3 23.1 %all-to-all-start.1 = ((f32[128,1,512]{2,1,0:T(1,128)}), f32[128,1,512]{2,1,0:T(1,128)S(1)}, u32[]{:S(2)}, u32[]{:S(2)}) async-start(f32[128,1,512]{2,1,0:T(1,128)} %broadcast_in_dim.6), calls=%async_computation.1 | async-start | bytes 524288 | tf_op jit(solution)/shard_map/all_to_all | solution.py:148
  69.4 111.7 %all-to-all-start.2 = ((bf16[512,64,128]{2,1,0:T(8,128)(2,1)}), bf16[512,64,128]{2,1,0:T(8,128)(2,1)}, u32[]{:S(2)}, u32[]{:S(2)}) async-start(bf16[512,64,128]{2,1,0:T(8,128)(2,1)} %shard_map.68), calls=%async_computation.2 | async-start | bytes 16777216 | tf_op jit(solution)/shard_map/all_to_all | solution.py:153
  216.6 5.7 %copy-start = (f32[4,64,128]{2,1,0:T(8,128)S(1)}, f32[4,64,128]{2,1,0:T(8,128)}, u32[]{:S(2)}) copy-start(f32[4,64,128]{2,1,0:T(8,128)} %shard_map.69) | copy-start | bytes 393220
  222.6 4.0 %collective-permute-start.1 = (f32[64,64]{0,1:T(8,128)S(1)}, f32[64,64]{0,1:T(8,128)S(1)}, u32[]{:S(2)}, u32[]{:S(2)}) collective-permute-start(f32[64,64]{0,1:T(8,128)S(1)} %fusion.15), channel_id=1, source_target_pairs={{0,2},{1,3},{2,0},{3,1},{4,6},{5,7},{6,4},{7,5},{8,10},{9,11},{10,... | collective-permute-start | bytes 49160 | tf_op jit(solution)/shard_map/ppermute | solution.py:16
  223.1 3.5 %collective-permute-start = (f32[64,64]{0,1:T(8,128)S(1)}, f32[64,64]{0,1:T(8,128)S(1)}, u32[]{:S(2)}, u32[]{:S(2)}) collective-permute-start(f32[64,64]{0,1:T(8,128)S(1)} %fusion.15), channel_id=1, source_target_pairs={{0,1},{1,0},{2,3},{3,2},{4,5},{5,4},{6,7},{7,6},{8,9},{9,8},{10,11... | collective-permute-start | bytes 49160 | tf_op jit(solution)/shard_map/ppermute | solution.py:15
  224.3 3.5 %collective-permute-start.2 = (f32[64,64]{0,1:T(8,128)S(1)}, f32[64,64]{0,1:T(8,128)S(1)}, u32[]{:S(2)}, u32[]{:S(2)}) collective-permute-start(f32[64,64]{0,1:T(8,128)S(1)} %fusion.15), channel_id=1, source_target_pairs={{0,3},{1,2},{2,1},{3,0},{4,7},{5,6},{6,5},{7,4},{8,11},{9,10},{10,... | collective-permute-start | bytes 49160 | tf_op jit(solution)/shard_map/ppermute | solution.py:17
  227.8 6.5 %collective-permute-start.5 = (f32[64,64]{0,1:T(8,128)S(1)}, f32[64,64]{0,1:T(8,128)S(1)}, u32[]{:S(2)}, u32[]{:S(2)}) collective-permute-start(f32[64,64]{0,1:T(8,128)S(1)} %add_add_fusion.2), channel_id=1, source_target_pairs={{0,12},{1,13},{2,14},{3,15},{4,8},{5,9},{6,10},{7,11},{8,4},{9,5},... | collective-permute-start | bytes 49160 | tf_op jit(solution)/shard_map/ppermute | solution.py:17
  231.2 3.9 %collective-permute-start.4 = (f32[64,64]{0,1:T(8,128)S(1)}, f32[64,64]{0,1:T(8,128)S(1)}, u32[]{:S(2)}, u32[]{:S(2)}) collective-permute-start(f32[64,64]{0,1:T(8,128)S(1)} %add_add_fusion.2), channel_id=1, source_target_pairs={{0,8},{1,9},{2,10},{3,11},{4,12},{5,13},{6,14},{7,15},{8,0},{9,1},... | collective-permute-start | bytes 49160 | tf_op jit(solution)/shard_map/ppermute | solution.py:16
  232.6 5.4 %collective-permute-start.3 = (f32[64,64]{0,1:T(8,128)S(1)}, f32[64,64]{0,1:T(8,128)S(1)}, u32[]{:S(2)}, u32[]{:S(2)}) collective-permute-start(f32[64,64]{0,1:T(8,128)S(1)} %add_add_fusion.2), channel_id=1, source_target_pairs={{0,4},{1,5},{2,6},{3,7},{4,0},{5,1},{6,2},{7,3},{8,12},{9,13},{10,... | collective-permute-start | bytes 49160 | tf_op jit(solution)/shard_map/ppermute | solution.py:15
  238.0 6.6 %collective-permute-start.8 = (f32[64,64]{0,1:T(8,128)S(1)}, f32[64,64]{0,1:T(8,128)S(1)}, u32[]{:S(2)}, u32[]{:S(2)}) collective-permute-start(f32[64,64]{0,1:T(8,128)S(1)} %add_add_fusion.1), channel_id=1, source_target_pairs={{0,48},{1,49},{2,50},{3,51},{4,52},{5,53},{6,54},{7,55},{8,56},{9,... | collective-permute-start | bytes 49160 | tf_op jit(solution)/shard_map/ppermute | solution.py:17
  240.5 5.9 %collective-permute-start.7 = (f32[64,64]{0,1:T(8,128)S(1)}, f32[64,64]{0,1:T(8,128)S(1)}, u32[]{:S(2)}, u32[]{:S(2)}) collective-permute-start(f32[64,64]{0,1:T(8,128)S(1)} %add_add_fusion.1), channel_id=1, source_target_pairs={{0,32},{1,33},{2,34},{3,35},{4,36},{5,37},{6,38},{7,39},{8,40},{9,... | collective-permute-start | bytes 49160 | tf_op jit(solution)/shard_map/ppermute | solution.py:16
  244.5 5.4 %collective-permute-start.6 = (f32[64,64]{0,1:T(8,128)S(1)}, f32[64,64]{0,1:T(8,128)S(1)}, u32[]{:S(2)}, u32[]{:S(2)}) collective-permute-start(f32[64,64]{0,1:T(8,128)S(1)} %add_add_fusion.1), channel_id=1, source_target_pairs={{0,16},{1,17},{2,18},{3,19},{4,20},{5,21},{6,22},{7,23},{8,24},{9,... | collective-permute-start | bytes 49160 | tf_op jit(solution)/shard_map/ppermute | solution.py:15
  250.0 5.5 %collective-permute-start.9 = (f32[64,64]{0,1:T(8,128)S(1)}, f32[64,64]{0,1:T(8,128)S(1)}, u32[]{:S(2)}, u32[]{:S(2)}) collective-permute-start(f32[64,64]{0,1:T(8,128)S(1)} %add_add_fusion), channel_id=1, source_target_pairs={{0,64},{1,65},{2,66},{3,67},{4,68},{5,69},{6,70},{7,71},{8,72},{9,... | collective-permute-start | bytes 49160 | tf_op jit(solution)/shard_map/ppermute | solution.py:21
Sparse Core Ops, SparseCore 0:
  11.0 82.8 all-gather.2

commit v12 on v8

--- a/solution.py
+++ b/solution.py
@@ -164,7 +164,7 @@
     image_t = inv_root[None, :] * (total_t + scaled_t.astype(jnp.float32))
     local_gram = jnp.dot(image_t, image_t.T, precision=highest)
     gram = butterfly_sum(local_gram, peer_count) / jnp.float32(rows_dev * peer_count)
-    lower = jnp.linalg.cholesky(gram)
+    lower = lax.linalg.cholesky(gram, symmetrize_input=False)
     basis = jax.scipy.linalg.solve_triangular(lower, image_t, lower=True).T
     return (basis, degree)
 

time: 241 us -> 242 us (level)
    ppermute x3, starting transfers between devices: 7.46 us -> 10.8 us  [butterfly_sum(): lax.ppermute(x, AXES, [(i, i ^ 3 * step) for i in range(peer_count)])]
    ppermute x3, starting transfers between devices: 6.46 us -> 3.88 us  [butterfly_sum(): far = lax.ppermute(x, AXES, [(i, i ^ 2 * step) for i in range(peer_count)])]
where the time goes in v12:
time: 242 us; the launch traced here: 241 us
  waiting for transfers between devices  109 us (45%)
  starting transfers between devices  41.9 us (17%)
  Pallas kernels  35.8 us (15%)
  other arithmetic  25 us (10%)
  between operations  14.2 us (6%)
  matrix products  10.8 us (4%)
  local copies, waits for them, and re-layouts  4.24 us (2%)
    all_to_all x1, waiting for transfers between devices, shards(): lax.all_to_all(terms, AXES, split_axis=0, concat_axis=0, tiled=True)  66 us
    pallas_call x1, Pallas kernels, forward_product(): pl.pallas_call(forward_kernel, grid_spec=pltpu.PrefetchScalarGridSpec(num...  18.2 us
    pallas_call x1, Pallas kernels, mirror_terms(): pl.pallas_call(terms_kernel, grid_spec=pltpu.PrefetchScalarGridSpec(num_s...  17.6 us
    all_gather x1, waiting for transfers between devices, shards(): vec_all = lax.all_gather(vec_t, AXES, axis=0)  12.5 us
    all_to_all x1, starting transfers between devices, shards(): got = lax.all_to_all(payload, AXES, split_axis=0, concat_axis=0, tiled=True)  11.1 us
    ppermute x3, starting transfers between devices, butterfly_sum(): lax.ppermute(x, AXES, [(i, i ^ 3 * step) for i in range(peer_count)])  10.8 us
    all_to_all x1, waiting for transfers between devices, shards(): got = lax.all_to_all(payload, AXES, split_axis=0, concat_axis=0, tiled=True)  10.6 us
    all_to_all x1, starting transfers between devices, shards(): lax.all_to_all(terms, AXES, split_axis=0, concat_axis=0, tiled=True)  10.3 us
  transfers between devices with their start and end apart: 14, of which 12 were waited for; matrix products, arithmetic and copies ran while one was open for 8% of the time, Pallas kernels for 15%

profile of v12, /device:TPU:0, one launch (start us, length us, event | category | flops | bytes accessed | tf_op | source)
XLA Modules:
  0.0 241.0 jit_solution(14921925391529680585)
XLA Ops:
  7.9 0.8 eq.49
  8.8 0.8 fusion.19
  9.6 10.2 %convert_reduce_fusion = (f32[512,128]{1,0:T(8,128)S(1)}, f32[512,128]{1,0:T(8,128)S(1)}) fusion(bf16[512,128,128]{2,1,0:T(8,128)(2,1)} %tiles_ref.3), kind=kLoop, calls=%fused_computation | loop fusion | flops 25034752 | bytes 17301504 | tf_op jit(solution)/shard_map/reduce_sum | solution.py:127
  20.6 0.9 copy.17
  21.5 11.1 %all-to-all-start = ((f32[128,1,516]{2,1,0:T(1,128)}), f32[128,1,516]{2,1,0:T(1,128)S(1)}, u32[]{:S(2)}, u32[]{:S(2)}) async-start(f32[128,1,516]{2,1,0:T(1,128)} %copy.17), calls=%async_computation | async-start | bytes 655360 | tf_op jit(solution)/shard_map/all_to_all | solution.py:138
  33.4 10.6 %all-to-all-done = f32[128,1,516]{2,1,0:T(1,128)S(1)} async-done(((f32[128,1,516]{2,1,0:T(1,128)}), f32[128,1,516]{2,1,0:T(1,128)S(1)}, u32[]{:S(2)}, u32[]{:S(2)}) %all-to-all-start) | async-done | bytes 264224 | tf_op jit(solution)/shard_map/all_to_all | solution.py:138
  44.4 1.1 fusion.39
  45.5 0.8 broadcast_in_dim.5
  46.3 4.8 %all-to-all-start.1 = ((f32[128,1,512]{2,1,0:T(1,128)}), f32[128,1,512]{2,1,0:T(1,128)S(1)}, u32[]{:S(2)}, u32[]{:S(2)}) async-start(f32[128,1,512]{2,1,0:T(1,128)} %broadcast_in_dim.5), calls=%async_computation.1 | async-start | bytes 524288 | tf_op jit(solution)/shard_map/all_to_all | solution.py:148
  51.7 17.6 %shard_map.68 = bf16[512,64,128]{2,1,0:T(8,128)(2,1)} custom-call(s32[512]{0:T(512)} %rows_ref.3, s32[512]{0:T(512)} %get-tuple-element.12.live_ref, bf16[512,128,128]{2,1,0:T(8,128)(2,1)} %tiles_ref.3, bf16[64,512]{1,0:T(8,128)(2,1)} %fusion.20.own_ref), custom_call_target="tpu_custom_call" | custom-call | tf_op jit(solution)/shard_map/pallas_call | solution.py:47
  69.4 10.3 %all-to-all-start.2 = ((bf16[512,64,128]{2,1,0:T(8,128)(2,1)}), bf16[512,64,128]{2,1,0:T(8,128)(2,1)}, u32[]{:S(2)}, u32[]{:S(2)}) async-start(bf16[512,64,128]{2,1,0:T(8,128)(2,1)} %shard_map.68), calls=%async_computation.2 | async-start | bytes 16777216 | tf_op jit(solution)/shard_map/all_to_all | solution.py:153
  80.5 0.9 reshape.91.inv_ref
  81.4 12.5 %all-gather.3.cloned.1.call-done = bf16[8192,512]{1,0:T(8,128)(2,1)} async-done(((bf16[64,512]{1,0:T(8,128)(2,1)}), bf16[8192,512]{1,0:T(8,128)(2,1)}) %all-gather.3.cloned.1.call-update) | async-done | bytes 8388624 | tf_op jit(solution)/shard_map/all_gather | solution.py:118
  93.9 18.2 %shard_map.69 = f32[4,64,128]{2,1,0:T(8,128)} custom-call(s32[512]{0:T(512)} %add_select_fusion.1.places_ref, s32[512]{0:T(512)} %cols_ref.1, s32[512]{0:T(512)} %rows_ref.3, s32[512]{0:T(512)} %get-tuple-element.12.live_ref, bf16[512,128,128]{2,1,0:T(8,128)(2,1)} %tiles_ref.3, bf16[128,64,512]{2,1,0:T(8,128)(2,1)} %bitcast.45, f32[128,1,512]{2,1,0:T(1,128)} %reshape.91.inv_ref), custom_call_target="tpu_custom_call" | custom-call | tf_op jit(solution)/shard_map/pallas_call | solution.py:89
  112.1 66.0 %all-to-all-done.2 = bf16[512,64,128]{2,1,0:T(8,128)(2,1)} async-done(((bf16[512,64,128]{2,1,0:T(8,128)(2,1)}), bf16[512,64,128]{2,1,0:T(8,128)(2,1)}, u32[]{:S(2)}, u32[]{:S(2)}) %all-to-all-start.2) | async-done | bytes 8388640 | tf_op jit(solution)/shard_map/all_to_all | solution.py:153
  178.1 7.8 %fusion = f32[4,64,128]{2,0,1:T(4,128)S(1)} fusion(bf16[512,64,128]{2,1,0:T(8,128)(2,1)} %all-to-all-done.2, s32[512]{0:T(512)S(1)} %eq.53), kind=kOutput, calls=%fused_computation.2 | convolution fusion | flops 33556480 | bytes 8521728 | tf_op jit(solution)/shard_map/tr,tka->rka/dot_general | solution.py:161
  186.2 4.1 %collective-permute-start.2 = (f32[64,64]{1,0:T(8,128)S(1)}, f32[64,64]{1,0:T(8,128)S(1)}, u32[]{:S(2)}, u32[]{:S(2)}) collective-permute-start(f32[64,64]{1,0:T(8,128)S(1)} %fusion.17), channel_id=1, source_target_pairs={{0,3},{1,2},{2,1},{3,0},{4,7},{5,6},{6,5},{7,4},{8,11},{9,10},{10,... | collective-permute-start | bytes 49160 | tf_op jit(solution)/shard_map/ppermute | solution.py:17
  190.4 1.4 collective-permute-done.2
  191.8 2.3 collective-permute-done.1
  194.2 5.2 %collective-permute-start.5 = (f32[64,64]{1,0:T(8,128)S(1)}, f32[64,64]{1,0:T(8,128)S(1)}, u32[]{:S(2)}, u32[]{:S(2)}) collective-permute-start(f32[64,64]{1,0:T(8,128)S(1)} %add_add_fusion.2), channel_id=1, source_target_pairs={{0,12},{1,13},{2,14},{3,15},{4,8},{5,9},{6,10},{7,11},{8,4},{9,5},... | collective-permute-start | bytes 49160 | tf_op jit(solution)/shard_map/ppermute | solution.py:17
  200.0 1.2 collective-permute-done.5
  201.2 2.0 collective-permute-done.4
  203.3 1.5 collective-permute-done.3
  204.8 1.5 collective-permute-start.8
  206.3 3.9 %collective-permute-start.7 = (f32[64,64]{1,0:T(8,128)S(1)}, f32[64,64]{1,0:T(8,128)S(1)}, u32[]{:S(2)}, u32[]{:S(2)}) collective-permute-start(f32[64,64]{1,0:T(8,128)S(1)} %add_add_fusion.1), channel_id=1, source_target_pairs={{0,32},{1,33},{2,34},{3,35},{4,36},{5,37},{6,38},{7,39},{8,40},{9,... | collective-permute-start | bytes 49160 | tf_op jit(solution)/shard_map/ppermute | solution.py:16
  210.2 1.0 collective-permute-done.8
  211.2 0.9 collective-permute-done.7
  212.1 3.5 %collective-permute-done.6 = f32[64,64]{1,0:T(8,128)S(1)} collective-permute-done((f32[64,64]{1,0:T(8,128)S(1)}, f32[64,64]{1,0:T(8,128)S(1)}, u32[]{:S(2)}, u32[]{:S(2)}) %collective-permute-start.6) | collective-permute-done | bytes 16416 | tf_op jit(solution)/shard_map/ppermute | solution.py:15
  215.7 5.4 %collective-permute-done.9 = f32[64,64]{1,0:T(8,128)S(1)} collective-permute-done((f32[64,64]{1,0:T(8,128)S(1)}, f32[64,64]{1,0:T(8,128)S(1)}, u32[]{:S(2)}, u32[]{:S(2)}) %collective-permute-start.9) | collective-permute-done | bytes 16416 | tf_op jit(solution)/shard_map/ppermute | solution.py:21
  221.1 5.8 %cholesky.16 = f32[64,64]{1,0:T(8,128)S(1)} custom-call(f32[64,64]{1,0:T(8,128)S(1)} %add_multiply_fusion), custom_call_target="Cholesky" | custom-call | tf_op jit(solution)/shard_map/cholesky | solution.py:167
  228.3 4.9 %custom-call.6 = f32[1,64,64]{1,2,0:T(8,128)S(1)} custom-call(f32[1,64,64]{2,1,0:T(8,128)S(1)} %fusion.26), custom_call_target="InvertDiagBlocksLowerTriangular" | custom-call | tf_op jit(solution)/shard_map/jit(_solve_triangular)/triangular_solve | solution.py:168
  233.2 1.0 fusion.15
  (42 shorter events, 6.6 us)
Async XLA Ops:
  7.2 86.7 %all-gather.3.cloned.1.call-start = ((), (), s32[]{:S(2)}) async-start(), calls=%async_computation.3 | async-start | bytes 8454144 | tf_op jit(solution)/shard_map/all_gather | solution.py:118
  9.5 23.1 %copy-start.3 = (s32[128]{0:T(128)S(1)}, s32[128]{0:T(128)}, u32[]{:S(2)}) copy-start(s32[128]{0:T(128)} %param.8) | copy-start | bytes 1540
  9.5 34.8 %copy-start.2 = (s32[512]{0:T(512)S(1)}, s32[512]{0:T(512)}, u32[]{:S(2)}) copy-start(s32[512]{0:T(512)} %rows_ref.3) | copy-start | bytes 6148
  9.6 41.5 %copy-start.1 = (bf16[512,64]{0,1:T(8,128)(2,1)S(1)}, bf16[512,64]{0,1:T(8,128)(2,1)}, u32[]{:S(2)}) copy-start(bf16[512,64]{0,1:T(8,128)(2,1)} %param.9) | copy-start | bytes 196612
  21.5 22.6 %all-to-all-start = ((f32[128,1,516]{2,1,0:T(1,128)}), f32[128,1,516]{2,1,0:T(1,128)S(1)}, u32[]{:S(2)}, u32[]{:S(2)}) async-start(f32[128,1,516]{2,1,0:T(1,128)} %copy.17), calls=%async_computation | async-start | bytes 655360 | tf_op jit(solution)/shard_map/all_to_all | solution.py:138
  46.3 23.0 %all-to-all-start.1 = ((f32[128,1,512]{2,1,0:T(1,128)}), f32[128,1,512]{2,1,0:T(1,128)S(1)}, u32[]{:S(2)}, u32[]{:S(2)}) async-start(f32[128,1,512]{2,1,0:T(1,128)} %broadcast_in_dim.5), calls=%async_computation.1 | async-start | bytes 524288 | tf_op jit(solution)/shard_map/all_to_all | solution.py:148
  69.4 108.7 %all-to-all-start.2 = ((bf16[512,64,128]{2,1,0:T(8,128)(2,1)}), bf16[512,64,128]{2,1,0:T(8,128)(2,1)}, u32[]{:S(2)}, u32[]{:S(2)}) async-start(bf16[512,64,128]{2,1,0:T(8,128)(2,1)} %shard_map.68), calls=%async_computation.2 | async-start | bytes 16777216 | tf_op jit(solution)/shard_map/all_to_all | solution.py:153
  112.1 73.8 %copy-start = (f32[4,64,128]{2,1,0:T(8,128)S(1)}, f32[4,64,128]{2,1,0:T(8,128)}, u32[]{:S(2)}) copy-start(f32[4,64,128]{2,1,0:T(8,128)} %shard_map.69) | copy-start | bytes 393220
  186.2 5.7 %collective-permute-start.2 = (f32[64,64]{1,0:T(8,128)S(1)}, f32[64,64]{1,0:T(8,128)S(1)}, u32[]{:S(2)}, u32[]{:S(2)}) collective-permute-start(f32[64,64]{1,0:T(8,128)S(1)} %fusion.17), channel_id=1, source_target_pairs={{0,3},{1,2},{2,1},{3,0},{4,7},{5,6},{6,5},{7,4},{8,11},{9,10},{10,... | collective-permute-start | bytes 49160 | tf_op jit(solution)/shard_map/ppermute | solution.py:17
  190.2 3.9 %collective-permute-start.1 = (f32[64,64]{1,0:T(8,128)S(1)}, f32[64,64]{1,0:T(8,128)S(1)}, u32[]{:S(2)}, u32[]{:S(2)}) collective-permute-start(f32[64,64]{1,0:T(8,128)S(1)} %fusion.17), channel_id=1, source_target_pairs={{0,2},{1,3},{2,0},{3,1},{4,6},{5,7},{6,4},{7,5},{8,10},{9,11},{10,... | collective-permute-start | bytes 49160 | tf_op jit(solution)/shard_map/ppermute | solution.py:16
  190.2 3.9 %collective-permute-start = (f32[64,64]{1,0:T(8,128)S(1)}, f32[64,64]{1,0:T(8,128)S(1)}, u32[]{:S(2)}, u32[]{:S(2)}) collective-permute-start(f32[64,64]{1,0:T(8,128)S(1)} %fusion.17), channel_id=1, source_target_pairs={{0,1},{1,0},{2,3},{3,2},{4,5},{5,4},{6,7},{7,6},{8,9},{9,8},{10,11... | collective-permute-start | bytes 49160 | tf_op jit(solution)/shard_map/ppermute | solution.py:15
  194.2 7.1 %collective-permute-start.5 = (f32[64,64]{1,0:T(8,128)S(1)}, f32[64,64]{1,0:T(8,128)S(1)}, u32[]{:S(2)}, u32[]{:S(2)}) collective-permute-start(f32[64,64]{1,0:T(8,128)S(1)} %add_add_fusion.2), channel_id=1, source_target_pairs={{0,12},{1,13},{2,14},{3,15},{4,8},{5,9},{6,10},{7,11},{8,4},{9,5},... | collective-permute-start | bytes 49160 | tf_op jit(solution)/shard_map/ppermute | solution.py:17
  199.3 3.9 %collective-permute-start.4 = (f32[64,64]{1,0:T(8,128)S(1)}, f32[64,64]{1,0:T(8,128)S(1)}, u32[]{:S(2)}, u32[]{:S(2)}) collective-permute-start(f32[64,64]{1,0:T(8,128)S(1)} %add_add_fusion.2), channel_id=1, source_target_pairs={{0,8},{1,9},{2,10},{3,11},{4,12},{5,13},{6,14},{7,15},{8,0},{9,1},... | collective-permute-start | bytes 49160 | tf_op jit(solution)/shard_map/ppermute | solution.py:16
  199.3 5.4 %collective-permute-start.3 = (f32[64,64]{1,0:T(8,128)S(1)}, f32[64,64]{1,0:T(8,128)S(1)}, u32[]{:S(2)}, u32[]{:S(2)}) collective-permute-start(f32[64,64]{1,0:T(8,128)S(1)} %add_add_fusion.2), channel_id=1, source_target_pairs={{0,4},{1,5},{2,6},{3,7},{4,0},{5,1},{6,2},{7,3},{8,12},{9,13},{10,... | collective-permute-start | bytes 49160 | tf_op jit(solution)/shard_map/ppermute | solution.py:15
  204.8 6.4 %collective-permute-start.8 = (f32[64,64]{1,0:T(8,128)S(1)}, f32[64,64]{1,0:T(8,128)S(1)}, u32[]{:S(2)}, u32[]{:S(2)}) collective-permute-start(f32[64,64]{1,0:T(8,128)S(1)} %add_add_fusion.1), channel_id=1, source_target_pairs={{0,48},{1,49},{2,50},{3,51},{4,52},{5,53},{6,54},{7,55},{8,56},{9,... | collective-permute-start | bytes 49160 | tf_op jit(solution)/shard_map/ppermute | solution.py:17
  206.3 5.8 %collective-permute-start.7 = (f32[64,64]{1,0:T(8,128)S(1)}, f32[64,64]{1,0:T(8,128)S(1)}, u32[]{:S(2)}, u32[]{:S(2)}) collective-permute-start(f32[64,64]{1,0:T(8,128)S(1)} %add_add_fusion.1), channel_id=1, source_target_pairs={{0,32},{1,33},{2,34},{3,35},{4,36},{5,37},{6,38},{7,39},{8,40},{9,... | collective-permute-start | bytes 49160 | tf_op jit(solution)/shard_map/ppermute | solution.py:16
  210.2 5.4 %collective-permute-start.6 = (f32[64,64]{1,0:T(8,128)S(1)}, f32[64,64]{1,0:T(8,128)S(1)}, u32[]{:S(2)}, u32[]{:S(2)}) collective-permute-start(f32[64,64]{1,0:T(8,128)S(1)} %add_add_fusion.1), channel_id=1, source_target_pairs={{0,16},{1,17},{2,18},{3,19},{4,20},{5,21},{6,22},{7,23},{8,24},{9,... | collective-permute-start | bytes 49160 | tf_op jit(solution)/shard_map/ppermute | solution.py:15
  215.6 5.5 %collective-permute-start.9 = (f32[64,64]{1,0:T(8,128)S(1)}, f32[64,64]{1,0:T(8,128)S(1)}, u32[]{:S(2)}, u32[]{:S(2)}) collective-permute-start(f32[64,64]{1,0:T(8,128)S(1)} %add_add_fusion), channel_id=1, source_target_pairs={{0,64},{1,65},{2,66},{3,67},{4,68},{5,69},{6,70},{7,71},{8,72},{9,... | collective-permute-start | bytes 49160 | tf_op jit(solution)/shard_map/ppermute | solution.py:21
Sparse Core Ops, SparseCore 0:
  11.0 82.8 all-gather.2
